TPU v7x, 512 devices: a whole 4x8x8 slice. The times are simulated.
512 devices in a mesh: frames: 64 (over y, z), atoms: 8 (over x, core).
Axes of the slice: x: 4, y: 8, z: 8, core: 2. Of those that a mesh axis runs over, the one named last changes fastest.
Arguments:
- displacements: float32 [1024, 3, 16384], P('frames', None, 'atoms'), may hold values from -2 to 2
Outputs:
- msd: float32 [16384, 1024], P(('atoms', 'frames'))
All inputs are finite; a program needn't handle non-finite values.
Results may differ from a plain program's by a relative error of at most 0.0003.
Values sent between devices are 32-bit elements; how exact they have to be, the bound alone decides.
No kernel may reach another device: no remote copies, remote signals or barrier semaphores. Data moves between devices by JAX's collectives and lax.ppermute only.
A program may use at most 64 MiB of HBM per device.

v0:
```python
import math

import jax
import jax.numpy as jnp
from jax import lax
from jax.sharding import PartitionSpec as P


def carried_in(array, axis, combine, identity):
    count, index = (lax.axis_size(axis), lax.axis_index(axis))
    everything = lax.all_gather(array, axis)
    start = jnp.broadcast_to(jnp.asarray(identity, array.dtype), array.shape)

    def hop(k, before):
        reached = k < index
        new = combine(before, everything[k])
        return jnp.where(reached, new, before)

    return lax.fori_loop(0, count, hop, start)


def lag_table(positions):
    length = positions.shape[0]
    count = positions.shape[3]
    series = positions.reshape(length, 3 * count)
    squares = jnp.sum(positions * positions, axis=(1, 2))
    zero_row = jnp.zeros((1, count), jnp.float32)
    running = jnp.concatenate([zero_row, jnp.cumsum(squares, axis=0)], axis=0)
    head = running[length][None, :] - running[:length]
    tail = jnp.flip(running[1:], 0)
    block = min(256, length)
    frame = jnp.arange(length, dtype=jnp.int32)
    starts = jnp.arange(0, length, block, dtype=jnp.int32)

    def add_block(corr, start):
        freq = start + jnp.arange(block, dtype=jnp.int32)
        phase = frame[:, None] * freq[None, :] % (2 * length)
        angle = phase.astype(jnp.float32) * (math.pi / length)
        cosine = jnp.cos(angle)
        sine = jnp.sin(angle)
        real_part = lax.dot_general(
            series, cosine, (((0,), (0,)), ((), ())), precision=lax.Precision.HIGHEST
        )
        imag_part = lax.dot_general(
            series, sine, (((0,), (0,)), ((), ())), precision=lax.Precision.HIGHEST
        )
        power = jnp.sum(
            (real_part * real_part + imag_part * imag_part).reshape(3, count, block), axis=0
        )
        weight = jnp.where(freq == 0, 1.0, 2.0).astype(jnp.float32) / (2.0 * length)
        term = lax.dot_general(
            power * weight[None, :],
            cosine,
            (((1,), (1,)), ((), ())),
            precision=lax.Precision.HIGHEST,
        )
        return (corr + term, None)

    corr, _ = lax.scan(add_block, jnp.zeros((count, length), jnp.float32), starts)
    parity = jnp.where(frame % 2 == 0, 1.0, -1.0).astype(jnp.float32)
    highest = jnp.dot(parity, series, precision=lax.Precision.HIGHEST)
    power_top = jnp.sum((highest * highest).reshape(3, count), axis=0)
    corr = corr + power_top[:, None] * parity[None, :] / (2.0 * length)
    counts = (length - frame).astype(jnp.float32)
    return (jnp.transpose(head + tail) - 2.0 * corr) / counts[None, :]


def add_carry(earlier, later):
    return earlier + later


def per_device(displacements):
    local_frames, _, atom_count = displacements.shape
    groups = lax.axis_size("frames")
    atom_total = atom_count * lax.axis_size("atoms")
    summed = lax.psum(jnp.sum(displacements, axis=2), "atoms")
    centred = displacements - (summed / atom_total)[:, :, None]
    partial_value = jnp.cumsum(centred, axis=0)
    earlier = carried_in(partial_value[-1], "frames", add_carry, jnp.zeros_like(partial_value[-1]))
    positions = (partial_value + earlier[None]).reshape(
        local_frames, 3, groups, atom_count // groups
    )
    return lag_table(lax.all_to_all(positions, "frames", split_axis=2, concat_axis=0, tiled=True))


def solution(mesh):
    placed = (P("frames", None, "atoms"),)
    return jax.shard_map(
        per_device,
        mesh=mesh,
        in_specs=placed,
        out_specs=P(("atoms", "frames"), None),
        check_vma=False,
    )
```

profile of v0, /device:TPU:2, one launch (start us, length us, event | category | flops | bytes accessed | tf_op | source)
XLA Modules:
  0.0 278.3 jit_solution(1276726155812374562)
XLA Ops:
  6.5 1.1 reduce_sum.41
  7.6 14.8 %psum.7 = f32[16,3]{0,1:T(4,128)S(1)} all-reduce(f32[16,3]{0,1:T(4,128)S(1)} %reduce_sum.41), channel_id=1, replica_groups=mesh['frames'=64,'atoms'=8] {'atoms'}, use_global_device_ids=true, to_apply=%region_1.0 | all-reduce | flops 48 | bytes 384 | tf_op jit(solution)/shard_map/psum | solution.py:76
  22.5 1.1 broadcast_subtract_fusion
  25.3 85.1 %all-gather.2.cloned.1.call-done = f32[64,3,2048]{2,1,0:T(4,128)} async-done(((f32[1,3,2048]{2,1,0:T(4,128)}), f32[64,3,2048]{2,1,0:T(4,128)}) %all-gather.2.cloned.1.call-update) | async-done | bytes 1572880 | tf_op jit(solution)/shard_map/all_gather | solution.py:11
  110.3 51.5 %while.27 = (s32[]{:T(128)}, f32[3,2048]{1,0:T(4,128)S(1)}, s32[]{:T(128)}, f32[64,3,2048]{2,1,0:T(4,128)}, s32[]{:T(128)}, /*index=5*/s32[]{:T(128)}) while((s32[]{:T(128)}, f32[3,2048]{1,0:T(4,128)S(1)}, s32[]{:T(128)}, f32[64,3,2048]{2,1,0:T(4,128)}, s32[]{:T(128)}, /*index=5*/s32[]{:T(128)}) %tuple.57), condition=%wide.region_4.5_spmd.clone, body=%wide.region_3.4_spmd.clone.sunk | while | flops 18436 | bytes 73829 | solution.py:19
  112.8 0.8 add_select_fusion.4
  113.6 0.8 add_select_fusion.4
  117.6 0.8 add_select_fusion.4
  118.4 0.8 add_select_fusion.4
  122.4 0.8 add_select_fusion.4
  123.2 0.8 add_select_fusion.4
  162.1 0.9 copy.37
  163.0 1.4 reshape.68
  164.4 8.7 %all-to-all-start = ((f32[64,1,1536]{2,1,0:T(1,128)}), f32[64,1,1536]{2,1,0:T(1,128)S(1)}, u32[]{:S(2)}, u32[]{:S(2)}) async-start(f32[64,1,1536]{2,1,0:T(1,128)} %reshape.68), calls=%async_computation | async-start | bytes 786432 | tf_op jit(solution)/shard_map/all_to_all | solution.py:83
  173.2 14.3 %all-to-all-done = f32[64,1,1536]{2,1,0:T(1,128)S(1)} async-done(((f32[64,1,1536]{2,1,0:T(1,128)}), f32[64,1,1536]{2,1,0:T(1,128)S(1)}, u32[]{:S(2)}, u32[]{:S(2)}) %all-to-all-start) | async-done | bytes 393248 | tf_op jit(solution)/shard_map/all_to_all | solution.py:83
  188.0 1.6 reduce.3
  191.3 9.0 %reduce-window.6 = f32[32,8,128]{2,1,0:T(8,128)S(1)} reduce-window(f32[32,8,128]{2,1,0:T(8,128)S(1)} %copy.25, f32[]{:T(128)} %constant.122.clone.1), window={size=1x1x128 pad=0_0x0_0x127_0}, to_apply=%region_6.7 | reduce-window | flops 4161536 | bytes 262148 | tf_op jit(solution)/shard_map/reduce-window
  201.6 2.1 copy.28
  203.7 0.8 reshape.62
  204.6 65.6 %while.28 = (s32[]{:T(128)}, f32[32,1024]{1,0:T(8,128)S(1)}, s32[4]{0:T(128)S(1)}, f32[1024,96]{1,0:T(8,128)S(1)}, s32[]{:T(128)}, /*index=5*/s32[]{:T(128)}, f32[]{:T(128)}) while((s32[]{:T(128)}, f32[32,1024]{1,0:T(8,128)S(1)}, s32[4]{0:T(128)S(1)}, f32[1024,96]{1,0:T(8,128)S(1)}, s32[]{:T(128)}, /*index=5*/s32[]{:T(128)}, ...), condition=%wide.region_10.11_spmd.clone, body=%wide.region_8.10_spmd.clone.sunk | while | flops 715818240 | bytes 1513591 | solution.py:59
  206.7 4.8 %convolution_multiply_fusion.3 = f32[256,96]{0,1:T(8,128)S(1)} fusion(f32[1024,96]{1,0:T(8,128)S(1)} %get-tuple-element.285, s32[256]{0:T(256)S(1)} %iota_add_fusion.2), kind=kOutput, calls=%fused_computation.5.clone.1 | convolution fusion | flops 305684480 | bytes 492544 | tf_op jit(solution)/shard_map/while/body/eval_jaxpr/dot_general | solution.py:44
  211.5 4.8 %fusion.60 = f32[256,96]{0,1:T(8,128)S(1)} fusion(f32[256,96]{0,1:T(8,128)S(1)} %convolution_multiply_fusion.3, f32[1024,96]{1,0:T(8,128)S(1)} %get-tuple-element.285, s32[256]{0:T(256)S(1)} %iota_add_fusion.2), kind=kOutput, calls=%fused_computation.8.clone.1 | convolution fusion | flops 305709056 | bytes 590848 | tf_op jit(solution)/shard_map/while/body/eval_jaxpr/dot_general | solution.py:41
  216.3 4.8 %convolution_add_fusion.2 = f32[32,1024]{1,0:T(8,128)S(1)} fusion(s32[256]{0:T(256)S(1)} %iota_add_fusion.2, f32[32,1024]{1,0:T(8,128)S(1)} %get-tuple-element.276, pred[]{:T(512)S(6)} %compare.11, f32[32,256]{1,0:T(8,128)S(1)} %reduce_sum.48, f32[256]{0:T(256)S(1)} %fusion.61), kind=kOutput, calls=%fused_computation.7.clone.1 | convolution fusion | flops 104407040 | bytes 296961 | tf_op jit(solution)/shard_map/while/body/eval_jaxpr/dot_general | solution.py:51
  223.0 4.8 %convolution_multiply_fusion.3 = f32[256,96]{0,1:T(8,128)S(1)} fusion(f32[1024,96]{1,0:T(8,128)S(1)} %get-tuple-element.285, s32[256]{0:T(256)S(1)} %iota_add_fusion.2), kind=kOutput, calls=%fused_computation.5.clone.1 | convolution fusion | flops 305684480 | bytes 492544 | tf_op jit(solution)/shard_map/while/body/eval_jaxpr/dot_general | solution.py:44
  227.9 4.8 %fusion.60 = f32[256,96]{0,1:T(8,128)S(1)} fusion(f32[256,96]{0,1:T(8,128)S(1)} %convolution_multiply_fusion.3, f32[1024,96]{1,0:T(8,128)S(1)} %get-tuple-element.285, s32[256]{0:T(256)S(1)} %iota_add_fusion.2), kind=kOutput, calls=%fused_computation.8.clone.1 | convolution fusion | flops 305709056 | bytes 590848 | tf_op jit(solution)/shard_map/while/body/eval_jaxpr/dot_general | solution.py:41
  232.7 4.8 %convolution_add_fusion.2 = f32[32,1024]{1,0:T(8,128)S(1)} fusion(s32[256]{0:T(256)S(1)} %iota_add_fusion.2, f32[32,1024]{1,0:T(8,128)S(1)} %get-tuple-element.276, pred[]{:T(512)S(6)} %compare.11, f32[32,256]{1,0:T(8,128)S(1)} %reduce_sum.48, f32[256]{0:T(256)S(1)} %fusion.61), kind=kOutput, calls=%fused_computation.7.clone.1 | convolution fusion | flops 104407040 | bytes 296961 | tf_op jit(solution)/shard_map/while/body/eval_jaxpr/dot_general | solution.py:51
  239.4 4.8 %convolution_multiply_fusion.3 = f32[256,96]{0,1:T(8,128)S(1)} fusion(f32[1024,96]{1,0:T(8,128)S(1)} %get-tuple-element.285, s32[256]{0:T(256)S(1)} %iota_add_fusion.2), kind=kOutput, calls=%fused_computation.5.clone.1 | convolution fusion | flops 305684480 | bytes 492544 | tf_op jit(solution)/shard_map/while/body/eval_jaxpr/dot_general | solution.py:44
  244.2 4.8 %fusion.60 = f32[256,96]{0,1:T(8,128)S(1)} fusion(f32[256,96]{0,1:T(8,128)S(1)} %convolution_multiply_fusion.3, f32[1024,96]{1,0:T(8,128)S(1)} %get-tuple-element.285, s32[256]{0:T(256)S(1)} %iota_add_fusion.2), kind=kOutput, calls=%fused_computation.8.clone.1 | convolution fusion | flops 305709056 | bytes 590848 | tf_op jit(solution)/shard_map/while/body/eval_jaxpr/dot_general | solution.py:41
  249.1 4.8 %convolution_add_fusion.2 = f32[32,1024]{1,0:T(8,128)S(1)} fusion(s32[256]{0:T(256)S(1)} %iota_add_fusion.2, f32[32,1024]{1,0:T(8,128)S(1)} %get-tuple-element.276, pred[]{:T(512)S(6)} %compare.11, f32[32,256]{1,0:T(8,128)S(1)} %reduce_sum.48, f32[256]{0:T(256)S(1)} %fusion.61), kind=kOutput, calls=%fused_computation.7.clone.1 | convolution fusion | flops 104407040 | bytes 296961 | tf_op jit(solution)/shard_map/while/body/eval_jaxpr/dot_general | solution.py:51
  255.7 4.8 %convolution_multiply_fusion.3 = f32[256,96]{0,1:T(8,128)S(1)} fusion(f32[1024,96]{1,0:T(8,128)S(1)} %get-tuple-element.285, s32[256]{0:T(256)S(1)} %iota_add_fusion.2), kind=kOutput, calls=%fused_computation.5.clone.1 | convolution fusion | flops 305684480 | bytes 492544 | tf_op jit(solution)/shard_map/while/body/eval_jaxpr/dot_general | solution.py:44
  260.6 4.8 %fusion.60 = f32[256,96]{0,1:T(8,128)S(1)} fusion(f32[256,96]{0,1:T(8,128)S(1)} %convolution_multiply_fusion.3, f32[1024,96]{1,0:T(8,128)S(1)} %get-tuple-element.285, s32[256]{0:T(256)S(1)} %iota_add_fusion.2), kind=kOutput, calls=%fused_computation.8.clone.1 | convolution fusion | flops 305709056 | bytes 590848 | tf_op jit(solution)/shard_map/while/body/eval_jaxpr/dot_general | solution.py:41
  265.4 4.8 %convolution_add_fusion.2 = f32[32,1024]{1,0:T(8,128)S(1)} fusion(s32[256]{0:T(256)S(1)} %iota_add_fusion.2, f32[32,1024]{1,0:T(8,128)S(1)} %get-tuple-element.276, pred[]{:T(512)S(6)} %compare.11, f32[32,256]{1,0:T(8,128)S(1)} %reduce_sum.48, f32[256]{0:T(256)S(1)} %fusion.61), kind=kOutput, calls=%fused_computation.7.clone.1 | convolution fusion | flops 104407040 | bytes 296961 | tf_op jit(solution)/shard_map/while/body/eval_jaxpr/dot_general | solution.py:51
  (107 shorter events, 59.9 us)
Async XLA Ops:
  6.5 103.8 %all-gather.2.cloned.1.call-start = ((), (), s32[]{:S(2)}) async-start(), calls=%async_computation.1 | async-start | bytes 2129920 | tf_op jit(solution)/shard_map/all_gather | solution.py:11
  164.4 23.1 %all-to-all-start = ((f32[64,1,1536]{2,1,0:T(1,128)}), f32[64,1,1536]{2,1,0:T(1,128)S(1)}, u32[]{:S(2)}, u32[]{:S(2)}) async-start(f32[64,1,1536]{2,1,0:T(1,128)} %reshape.68), calls=%async_computation | async-start | bytes 786432 | tf_op jit(solution)/shard_map/all_to_all | solution.py:83
Sparse Core Ops, SparseCore 0:
  24.6 85.6 all-gather.1
where the time goes:
time: 283 us; the launch traced here: 278 us
  waiting for transfers between devices  99.4 us (35%)
  other arithmetic  70 us (25%)
  matrix products  58 us (20%)
  blocking collectives  14.8 us (5%)
  between operations  13.6 us (5%)
  local copies, waits for them, and re-layouts  12.4 us (4%)
  starting transfers between devices  8.74 us (3%)
    all_gather x1, waiting for transfers between devices, carried_in(): everything = lax.all_gather(array, axis)  85.1 us
    select_n x64, other arithmetic, hop(): return jnp.where(reached, new, before)  50.5 us
    dot_general x4, matrix products, add_block(): lax.dot_general(series, sine, (((0,), (0,)), ((), ())), precision=lax.Pre...  19.4 us
    dot_general x4, matrix products, add_block(): lax.dot_general(series, cosine, (((0,), (0,)), ((), ())), precision=lax.P...  19.3 us
    dot_general x4, matrix products, add_block(): lax.dot_general(power * weight[None, :], cosine, (((1,), (1,)), ((), ()))...  19 us
    psum x1, blocking collectives, per_device(): summed = lax.psum(jnp.sum(displacements, axis=2), 'atoms')  14.8 us
    all_to_all x1, waiting for transfers between devices, per_device(): lax.all_to_all(positions, 'frames', split_axis=2, concat_axis=0, tiled=True)  14.3 us
    another operation x3, other arithmetic  9.15 us
  transfers between devices with their start and end apart: 2, of which 2 were waited for; matrix products, arithmetic and copies ran while one was open for 0% of the time, Pallas kernels for 0%

commit v1 on v0

v1 whole, which is shorter than its diff:
```python
import numpy as np

import jax
import jax.numpy as jnp
from jax import lax
from jax.sharding import PartitionSpec as P


def angle_tables(length, split):
    frame = np.arange(length, dtype=np.int64)
    low = np.arange(split, dtype=np.int64)
    high = np.arange(length // split, dtype=np.int64) * split
    coarse = (high[:, None] * frame[None, :]) % (2 * length) * (np.pi / length)
    fine = (low[:, None] * frame[None, :]) % (2 * length) * (np.pi / length)
    return [
        jnp.asarray(t.astype(np.float32))
        for t in (np.cos(coarse), np.sin(coarse), np.cos(fine), np.sin(fine))
    ]


def spectral_tables(length):
    cos_hi, sin_hi, cos_lo, sin_lo = angle_tables(length, 32)
    cosine = (cos_hi[:, None, :] * cos_lo[None, :, :] - sin_hi[:, None, :] * sin_lo[None, :, :])
    sine = (sin_hi[:, None, :] * cos_lo[None, :, :] + cos_hi[:, None, :] * sin_lo[None, :, :])
    cosine = cosine.reshape(length, length)
    sine = sine.reshape(length, length)
    frame = jnp.arange(length, dtype=jnp.int32)
    parity = jnp.where(frame % 2 == 0, 1.0, -1.0).astype(jnp.float32)
    sine = jnp.where((frame == 0)[:, None], parity[None, :], sine)
    return cosine, sine, parity


def lag_table(series, count):
    length = series.shape[0]
    frame = jnp.arange(length, dtype=jnp.int32)
    lower = (frame[None, :] <= frame[:, None]).astype(jnp.float32)
    positions = jnp.dot(lower, series, precision=lax.Precision.HIGHEST)
    squares = jnp.sum((positions * positions).reshape(length, 3, count), axis=1)
    cosine, sine, parity = spectral_tables(length)
    both = jnp.concatenate([cosine, sine], axis=0)
    spectrum = jnp.dot(both, positions, precision=lax.Precision.HIGHEST)
    real_part = spectrum[:length].reshape(length, 3, count)
    imag_part = spectrum[length:].reshape(length, 3, count)
    imag_zeroed = jnp.where((frame == 0)[:, None, None], 0.0, imag_part)
    power = jnp.sum(real_part * real_part + imag_zeroed * imag_zeroed, axis=1)
    power_top = jnp.sum(imag_part[0] * imag_part[0], axis=0)
    window = (
        (frame[None, :] >= frame[:, None]).astype(jnp.float32)
        + (frame[None, :] <= (length - 1 - frame)[:, None]).astype(jnp.float32)
    )
    weight = jnp.where(frame == 0, 1.0, 2.0).astype(jnp.float32) * (2.0 / (2 * length))
    mixing = jnp.concatenate([window, -cosine * weight[None, :]], axis=1)
    stacked = jnp.concatenate([squares, power], axis=0)
    numer = jnp.dot(mixing, stacked, precision=lax.Precision.HIGHEST)
    numer = numer - power_top[None, :] * parity[:, None] * (2.0 / (2 * length))
    counts = (length - frame).astype(jnp.float32)
    return jnp.transpose(numer / counts[:, None])


def per_device(displacements):
    local_frames, _, atom_count = displacements.shape
    groups = lax.axis_size("frames")
    atom_total = atom_count * lax.axis_size("atoms")
    summed = lax.psum(jnp.sum(displacements, axis=2), "atoms")
    centred = displacements - (summed / atom_total)[:, :, None]
    blocks = centred.reshape(local_frames, 3, groups, atom_count // groups)
    moved = lax.all_to_all(blocks, "frames", split_axis=2, concat_axis=0, tiled=True)
    count = atom_count // groups
    series = moved.reshape(local_frames * groups, 3 * count)
    return lag_table(series, count)


def solution(mesh):
    placed = (P("frames", None, "atoms"),)
    return jax.shard_map(
        per_device,
        mesh=mesh,
        in_specs=placed,
        out_specs=P(("atoms", "frames"), None),
        check_vma=False,
    )
```

time: 283 us -> 79.8 us (0.28)
  the two profiles are of different devices: /device:TPU:2 before, /device:TPU:16 now
where the time goes in v1:
time: 79.8 us; the launch traced here: 79.5 us
  matrix products  24 us (30%)
  starting transfers between devices  16.5 us (21%)
  blocking collectives  14.6 us (18%)
  other arithmetic  11.4 us (14%)
  local copies, waits for them, and re-layouts  7.62 us (10%)
  waiting for transfers between devices  5.13 us (6%)
    all_to_all x1, starting transfers between devices, per_device(): lax.all_to_all(blocks, 'frames', split_axis=2, concat_axis=0, tiled=True)  16.5 us
    psum x1, blocking collectives, per_device(): summed = lax.psum(jnp.sum(displacements, axis=2), 'atoms')  14.6 us
    dot_general x1, matrix products, lag_table(): numer = jnp.dot(mixing, stacked, precision=lax.Precision.HIGHEST)  11.7 us
    dot_general x1, matrix products, lag_table(): spectrum = jnp.dot(both, positions, precision=lax.Precision.HIGHEST)  10.9 us
    all_to_all x1, waiting for transfers between devices, per_device(): lax.all_to_all(blocks, 'frames', split_axis=2, concat_axis=0, tiled=True)  5.13 us
    unnamed x12, local copies, waits for them, and re-layouts  3.81 us
    select_n x1, other arithmetic, spectral_tables(): sine = jnp.where((frame == 0)[:, None], parity[None, :], sine)  3.77 us
    add x1, other arithmetic, lag_table(): (frame[None, :] >= frame[:, None]).astype(jnp.float32)  2.38 us
  transfers between devices with their start and end apart: 1, of which 1 were waited for; matrix products, arithmetic and copies ran while one was open for 9% of the time, Pallas kernels for 0%

profile of v1, /device:TPU:16, one launch (start us, length us, event | category | flops | bytes accessed | tf_op | source)
XLA Modules:
  0.0 79.5 jit_solution(16667556693752365902)
XLA Ops:
  0.0 1.1 %reduce_sum.36 = f32[16,3]{0,1:T(4,128)S(1)} reduce(f32[16,3,2048]{2,0,1:T(8,128)} %param.5, f32[]{:T(128)} %constant.17.clone.1), dimensions={2}, to_apply=%region_0.0 | reduce | flops 98256 | bytes 393412 | tf_op jit(solution)/shard_map/reduce_sum | solution.py:64
  1.1 14.6 %psum.7 = f32[16,3]{0,1:T(4,128)S(1)} all-reduce(f32[16,3]{0,1:T(4,128)S(1)} %reduce_sum.36), channel_id=1, replica_groups=mesh['frames'=64,'atoms'=8] {'atoms'}, use_global_device_ids=true, to_apply=%region_1.0 | all-reduce | flops 48 | bytes 384 | tf_op jit(solution)/shard_map/psum | solution.py:64
  15.7 1.1 %broadcast_subtract_fusion = f32[16,3,2048]{2,0,1:T(8,128)S(1)} fusion(f32[16,3,2048]{2,0,1:T(8,128)} %param.5, f32[16,3]{0,1:T(4,128)S(1)} %broadcast_multiply_fusion), kind=kLoop, calls=%fused_computation.24 | loop fusion | flops 98304 | bytes 786624 | tf_op jit(solution)/shard_map/sub | solution.py:65
  16.8 0.5 reshape.85
  17.3 0.9 %copy.10 = f32[16,3,64,32]{3,0,1,2:T(8,128)S(1)} copy(f32[16,3,64,32]{3,2,0,1:T(8,128)S(1)} %reshape.85) | data formatting | bytes 786432 | tf_op jit(solution)/shard_map/reshape | solution.py:66
  18.2 0.0 copy-start.1
  18.2 0.0 copy-start.2
  18.3 0.0 copy-start.3
  18.3 0.0 copy-start.4
  18.3 1.4 %reshape.90 = f32[64,1,1536]{2,1,0:T(1,128)} reshape(f32[64,3,16,32]{3,2,1,0:T(8,128)S(1)} %bitcast.23) | data formatting | bytes 786432
  19.7 16.5 %all-to-all-start = ((f32[64,1,1536]{2,1,0:T(1,128)}), f32[64,1,1536]{2,1,0:T(1,128)S(1)}, u32[]{:S(2)}, u32[]{:S(2)}) async-start(f32[64,1,1536]{2,1,0:T(1,128)} %reshape.90), calls=%async_computation | async-start | bytes 786432 | tf_op jit(solution)/shard_map/all_to_all | solution.py:67
  36.2 2.4 %convert_add_fusion = f32[1024,1024]{1,0:T(8,128)} fusion(s32[1024]{0:T(1024)S(1)} %iota_subtract_fusion), kind=kLoop, calls=%fused_computation.12 | loop fusion | flops 5242880 | bytes 4198400 | tf_op jit(solution)/shard_map/add | solution.py:48
  38.6 0.0 copy-done.1
  38.6 0.0 copy-done.2
  38.6 0.0 copy-done.3
  38.6 1.2 %multiply_add_fusion = (f32[32,32,1024]{2,1,0:T(8,128)S(1)}, f32[32,32,1024]{2,1,0:T(8,128)S(1)}) fusion(f32[32,1024]{1,0:T(8,128)S(1)} %copy-done.4, f32[32,1024]{1,0:T(8,128)S(1)} %copy-done.2, f32[32,1024]{1,0:T(8,128)S(1)} %copy-done.3, f32[32,1024]{1,0:T(8,128)S(1)} %copy-done.1), kind=kLoop, calls=%fused_computation.13 | loop fusion | flops 6291456 | bytes 8912896 | tf_op jit(solution)/shard_map/add | solution.py:24
  39.9 1.9 %copy-done = f32[32,32,1024]{2,1,0:T(8,128)} copy-done((f32[32,32,1024]{2,1,0:T(8,128)}, f32[32,32,1024]{2,1,0:T(8,128)S(1)}, u32[]{:S(2)}) %copy-start) | copy-done | bytes 4194328
  41.8 3.8 %bitcast_select_fusion = (f32[1024,1024]{1,0:T(8,128)}, f32[1024,1024]{1,0:T(8,128)}) fusion(f32[32,32,1024]{2,1,0:T(8,128)S(1)} %get-tuple-element.7, f32[1024]{0:T(1024)S(1)} %fusion.23, pred[1024]{0:T(1024)(128)(4,1)S(1)} %iota_compare_fusion.4, f32[1024]{0:T(1024)S(1)} %select_multiply_fusion, f32[32,32,1024]{2,1,0:T(8,128)S(1)} %get-tuple-element.8), kind=kLoop, calls=%fused_computation.10 | loop fusion | flops 3145728 | bytes 16786432 | tf_op jit(solution)/shard_map/jit(_where)/select_n | solution.py:29
  45.6 5.1 %all-to-all-done = f32[64,1,1536]{2,1,0:T(1,128)S(1)} async-done(((f32[64,1,1536]{2,1,0:T(1,128)}), f32[64,1,1536]{2,1,0:T(1,128)S(1)}, u32[]{:S(2)}, u32[]{:S(2)}) %all-to-all-start) | async-done | bytes 393248 | tf_op jit(solution)/shard_map/all_to_all | solution.py:67
  50.7 0.5 broadcast.124
  51.2 1.6 %reduce.2 = f32[64,1536]{1,0:T(8,128)S(1)} reduce(f32[64,1,1536]{2,1,0:T(1,128)S(1)} %all-to-all-done, f32[]{:T(128)} %broadcast.124), dimensions={1}, to_apply=%all_to_all.11.reduce_sub_computation | reduce | bytes 786436 | tf_op jit(solution)/shard_map/all_to_all | solution.py:67
  52.8 0.4 reshape.91
  53.3 0.1 bitcast_bitcast_fusion
  53.4 0.9 %copy.8 = f32[64,16,3,1,32]{4,2,1,0,3:T(4,128)S(1)} copy(f32[64,16,3,1,32]{4,1,2,0,3:T(8,128)S(1)} %bitcast_bitcast_fusion) | data formatting | bytes 786432 | tf_op jit(solution)/shard_map/all_to_all | solution.py:67
  54.2 0.8 %reshape.86 = f32[1024,96]{1,0:T(8,128)S(1)} reshape(f32[64,16,3,1,32]{4,2,1,0,3:T(4,128)S(1)} %copy.8) | data formatting | bytes 786432 | tf_op jit(solution)/shard_map/reshape | solution.py:69
  55.1 1.5 %fusion.27 = (f32[1024,96]{0,1:T(8,128)S(1)}, f32[1024,96]{0,1:T(8,128)S(1)}) fusion(f32[1024,96]{1,0:T(8,128)S(1)} %reshape.86), kind=kOutput, calls=%fused_computation.42 | convolution fusion | flops 1209106432 | bytes 1179648 | tf_op jit(solution)/shard_map/dot_general | solution.py:37
  56.6 10.9 %fusion = f32[2048,96]{0,1:T(8,128)S(1)} fusion(f32[1024,96]{0,1:T(8,128)S(1)} %get-tuple-element.10, f32[1024,1024]{1,0:T(8,128)} %get-tuple-element.11, f32[1024,1024]{1,0:T(8,128)} %bitcast.22), kind=kOutput, calls=%fused_computation | convolution fusion | flops 2418016256 | bytes 9568256 | tf_op jit(solution)/shard_map/dot_general | solution.py:41
  67.5 0.1 fusion.26
  67.5 0.1 fusion.18
  67.6 0.1 mul.130
  67.8 0.1 add_reduce_fusion
  67.9 11.7 %fusion.12 = f32[32,1024]{1,0:T(8,128)} fusion(f32[1024,1024]{1,0:T(8,128)} %get-tuple-element.12, f32[1024,1024]{1,0:T(8,128)} %convert_add_fusion, f32[1024,32]{0,1:T(8,128)S(1)} %add_reduce_fusion, f32[1024,32]{0,1:T(8,128)S(1)} %reduce_sum.37, f32[1024]{0:T(1024)S(1)} %subtract_convert_fusion, f32[1024]{0:T(1024)S(1)} %fusion.23, f32[32]{0:T(128)S(1)} %reduce_sum.39), kind=kOutput, calls=%fused_computation.18 | convolution fusion | flops 807600128 | bytes 8790144 | tf_op jit(solution)/shard_map/dot_general | solution.py:54
  (10 shorter events, 0.1 us)
Async XLA Ops:
  18.2 20.4 %copy-start.1 = (f32[32,1024]{1,0:T(8,128)S(1)}, f32[32,1024]{1,0:T(8,128)}, u32[]{:S(2)}) copy-start(f32[32,1024]{1,0:T(8,128)} %constant.46.clone) | copy-start | bytes 393220
  18.2 20.4 %copy-start.2 = (f32[32,1024]{1,0:T(8,128)S(1)}, f32[32,1024]{1,0:T(8,128)}, u32[]{:S(2)}) copy-start(f32[32,1024]{1,0:T(8,128)} %constant.47.clone) | copy-start | bytes 393220
  18.3 20.4 %copy-start.3 = (f32[32,1024]{1,0:T(8,128)S(1)}, f32[32,1024]{1,0:T(8,128)}, u32[]{:S(2)}) copy-start(f32[32,1024]{1,0:T(8,128)} %constant.48.clone) | copy-start | bytes 393220
  18.3 20.4 %copy-start.4 = (f32[32,1024]{1,0:T(8,128)S(1)}, f32[32,1024]{1,0:T(8,128)}, u32[]{:S(2)}) copy-start(f32[32,1024]{1,0:T(8,128)} %constant.49.clone) | copy-start | bytes 393220
  19.7 31.0 %all-to-all-start = ((f32[64,1,1536]{2,1,0:T(1,128)}), f32[64,1,1536]{2,1,0:T(1,128)S(1)}, u32[]{:S(2)}, u32[]{:S(2)}) async-start(f32[64,1,1536]{2,1,0:T(1,128)} %reshape.90), calls=%async_computation | async-start | bytes 786432 | tf_op jit(solution)/shard_map/all_to_all | solution.py:67
  39.9 2.0 %copy-start = (f32[32,32,1024]{2,1,0:T(8,128)}, f32[32,32,1024]{2,1,0:T(8,128)S(1)}, u32[]{:S(2)}) copy-start(f32[32,32,1024]{2,1,0:T(8,128)S(1)} %get-tuple-element.8) | copy-start | bytes 12582916

commit v2 on v1

v2 whole, which is shorter than its diff:
```python
import numpy as np

import jax
import jax.numpy as jnp
from jax import lax
from jax.sharding import PartitionSpec as P


def angle_tables(length, split):
    frame = np.arange(length, dtype=np.int64)
    low = np.arange(split, dtype=np.int64)
    high = np.arange(length // split, dtype=np.int64) * split
    coarse = (high[:, None] * frame[None, :]) % (2 * length) * (np.pi / length)
    fine = (low[:, None] * frame[None, :]) % (2 * length) * (np.pi / length)
    return [
        jnp.asarray(t.astype(np.float32))
        for t in (np.cos(coarse), np.sin(coarse), np.cos(fine), np.sin(fine))
    ]


def spectral_tables(length, rows):
    split = 32
    cos_hi, sin_hi, cos_lo, sin_lo = angle_tables(length, split)
    blocks = -(-rows // split)
    cos_hi, sin_hi = cos_hi[:blocks], sin_hi[:blocks]
    cosine = cos_hi[:, None, :] * cos_lo[None, :, :] - sin_hi[:, None, :] * sin_lo[None, :, :]
    sine = sin_hi[:, None, :] * cos_lo[None, :, :] + cos_hi[:, None, :] * sin_lo[None, :, :]
    cosine = cosine.reshape(blocks * split, length)[:rows]
    sine = sine.reshape(blocks * split, length)[:rows]
    return cosine, sine


def split_three(values):
    first = lax.reduce_precision(values, exponent_bits=8, mantissa_bits=7)
    rest = values - first
    second = lax.reduce_precision(rest, exponent_bits=8, mantissa_bits=7)
    third = rest - second
    return jnp.concatenate([first, second, third], axis=1).astype(jnp.bfloat16)


def exact_product(matrix, values):
    width = values.shape[1]
    out = jnp.dot(
        matrix.astype(jnp.bfloat16), split_three(values), preferred_element_type=jnp.float32
    )
    return out[:, :width] + out[:, width : 2 * width] + out[:, 2 * width :]


def lag_table(series, count):
    length = series.shape[0]
    half = length // 2
    width = 3 * count
    frame = jnp.arange(length, dtype=jnp.int32)
    lower = (frame[None, :] <= frame[:, None]).astype(jnp.float32)
    positions = exact_product(lower, series)
    squares = jnp.sum((positions * positions).reshape(length, 3, count), axis=1)
    cosine, sine = spectral_tables(length, half + 1)
    parity = jnp.where(frame % 2 == 0, 1.0, -1.0).astype(jnp.float32)
    both = jnp.concatenate([cosine, sine[1:]], axis=0)
    signed = jnp.concatenate([positions, positions * parity[:, None]], axis=1)
    spectrum = jnp.dot(both, signed, precision=lax.Precision.HIGHEST)
    real_part = spectrum[: half + 1]
    imag_part = jnp.concatenate([jnp.zeros((1, 2 * width), jnp.float32), spectrum[half + 1 :]], axis=0)
    power = jnp.sum((real_part * real_part + imag_part * imag_part).reshape(half + 1, 2, 3, count), axis=2)
    low_q = jnp.arange(half, dtype=jnp.int32)
    weight = jnp.where(low_q == 0, 1.0, 2.0).astype(jnp.float32) / (2 * length)
    coef = power[:half] * weight[:, None, None]
    coef = coef.at[:, 1].set(jnp.where((low_q == 0)[:, None], power[0, 1][None, :] / (2 * length), coef[:, 1]))
    sign_q = jnp.where(low_q % 2 == 0, 1.0, -1.0).astype(jnp.float32)
    coef = coef.reshape(half, 2 * count)
    coef = jnp.concatenate([coef, coef * sign_q[:, None]], axis=1)
    middle = power[half, 0] * (2.0 / (2 * length))
    table = cosine[:, :half]
    folded = jnp.dot(table, coef, precision=lax.Precision.HIGHEST)
    lag = jnp.arange(half + 1, dtype=jnp.int32)
    sign_m = jnp.where(lag % 2 == 0, 1.0, -1.0).astype(jnp.float32)[:, None]
    quarter = jnp.where(lag % 4 == 0, 1.0, jnp.where(lag % 4 == 2, -1.0, 0.0)).astype(jnp.float32)[:, None]
    near = folded[:, :count] + sign_m * folded[:, count : 2 * count] + middle[None, :] * quarter
    far = folded[:, 2 * count : 3 * count] + sign_m * folded[:, 3 * count :] + middle[None, :] * quarter
    corr = jnp.concatenate([near, jnp.flip(far[1:half], axis=0)], axis=0)
    window = (
        (frame[None, :] >= frame[:, None]).astype(jnp.float32)
        + (frame[None, :] <= (length - 1 - frame)[:, None]).astype(jnp.float32)
    )
    numer = exact_product(window, squares) - 2.0 * corr
    counts = (length - frame).astype(jnp.float32)
    return jnp.transpose(numer / counts[:, None])


def per_device(displacements):
    local_frames, _, atom_count = displacements.shape
    groups = lax.axis_size("frames")
    atom_total = atom_count * lax.axis_size("atoms")
    summed = lax.psum(jnp.sum(displacements, axis=2), "atoms")
    centred = displacements - (summed / atom_total)[:, :, None]
    blocks = centred.reshape(local_frames, 3, groups, atom_count // groups)
    moved = lax.all_to_all(blocks, "frames", split_axis=2, concat_axis=0, tiled=True)
    count = atom_count // groups
    series = moved.reshape(local_frames * groups, 3 * count)
    return lag_table(series, count)


def solution(mesh):
    placed = (P("frames", None, "atoms"),)
    return jax.shard_map(
        per_device,
        mesh=mesh,
        in_specs=placed,
        out_specs=P(("atoms", "frames"), None),
        check_vma=False,
    )
```

time: 79.8 us -> 77.3 us (0.969)
  matrix products: 24 us -> 10.3 us
  local copies, waits for them, and re-layouts: 7.62 us -> 17.8 us
  waiting for transfers between devices: 5.13 us -> 8.43 us
  other arithmetic: 11.4 us -> 8.95 us
    dot_general x3 -> x4, matrix products: 24 us -> 10.3 us  [the longest x1 6.73 us: lag_table(): spectrum = jnp.dot(both, signed, precision=lax.Precision.HIGHEST)]
    slice x0 -> x4, local copies, waits for them, and re-layouts: none -> 3.37 us  [the longest x1 1.6 us: spectral_tables(): cosine = cosine.reshape(blocks * split, length)[:rows]]
    all_to_all x1, waiting for transfers between devices: 5.13 us -> 8.43 us  [per_device(): lax.all_to_all(blocks, 'frames', split_axis=2, concat_axis=0, tiled=True)]
    add x2 -> x3, other arithmetic: 3.61 us -> 0.39 us  [the longest x1 0.19 us: lag_table(): real_part * real_part + imag_part * imag_part]
    select_n x2 -> x3, other arithmetic: 3.78 us -> 0.58 us  [the longest x1 0.57 us: lag_table(): sign_q = jnp.where(low_q % 2 == 0, 1.0, -1.0).astype(jnp.float32)]
    all_to_all x3, local copies, waits for them, and re-layouts: 1.48 us -> 4.2 us  [per_device(): lax.all_to_all(blocks, 'frames', split_axis=2, concat_axis=0, tiled=True)]
    reshape x1, local copies, waits for them, and re-layouts: 0.82 us -> 2.65 us  [per_device(): series = moved.reshape(local_frames * groups, 3 * count)]
    unnamed x12 -> x22, local copies, waits for them, and re-layouts: 3.81 us -> 5.01 us
  transfers between devices with their start and end apart: 1 -> 1, of which waited for: 1 -> 1; matrix products, arithmetic and copies ran while one was open for 9% -> 8% of each run, Pallas kernels for 0% -> 0%
where the time goes in v2:
time: 77.3 us; the launch traced here: 76.9 us
  local copies, waits for them, and re-layouts  17.8 us (23%)
  starting transfers between devices  16.5 us (21%)
  blocking collectives  14.6 us (19%)
  matrix products  10.3 us (13%)
  other arithmetic  8.95 us (12%)
  waiting for transfers between devices  8.43 us (11%)
    all_to_all x1, starting transfers between devices, per_device(): lax.all_to_all(blocks, 'frames', split_axis=2, concat_axis=0, tiled=True)  16.5 us
    psum x1, blocking collectives, per_device(): summed = lax.psum(jnp.sum(displacements, axis=2), 'atoms')  14.6 us
    all_to_all x1, waiting for transfers between devices, per_device(): lax.all_to_all(blocks, 'frames', split_axis=2, concat_axis=0, tiled=True)  8.43 us
    dot_general x1, matrix products, lag_table(): spectrum = jnp.dot(both, signed, precision=lax.Precision.HIGHEST)  6.73 us
    unnamed x22, local copies, waits for them, and re-layouts  5.01 us
    all_to_all x3, local copies, waits for them, and re-layouts, per_device(): lax.all_to_all(blocks, 'frames', split_axis=2, concat_axis=0, tiled=True)  4.2 us
    reshape x1, local copies, waits for them, and re-layouts, per_device(): series = moved.reshape(local_frames * groups, 3 * count)  2.65 us
    reshape x2, local copies, waits for them, and re-layouts, per_device(): blocks = centred.reshape(local_frames, 3, groups, atom_count // groups)  2.58 us
  transfers between devices with their start and end apart: 1, of which 1 were waited for; matrix products, arithmetic and copies ran while one was open for 8% of the time, Pallas kernels for 0%

profile of v2, /device:TPU:16, one launch (start us, length us, event | category | flops | bytes accessed | tf_op | source)
XLA Modules:
  0.0 76.9 jit_solution(4486218463553606736)
XLA Ops:
  0.0 1.1 %reduce_sum.27 = f32[16,3]{0,1:T(4,128)S(1)} reduce(f32[16,3,2048]{2,0,1:T(8,128)} %param.7, f32[]{:T(128)} %constant.99.clone.1), dimensions={2}, to_apply=%region_0.0 | reduce | flops 98256 | bytes 393412 | tf_op jit(solution)/shard_map/reduce_sum | solution.py:94
  1.1 14.6 %psum.7 = f32[16,3]{0,1:T(4,128)S(1)} all-reduce(f32[16,3]{0,1:T(4,128)S(1)} %reduce_sum.27), channel_id=1, replica_groups=mesh['frames'=64,'atoms'=8] {'atoms'}, use_global_device_ids=true, to_apply=%region_1.0 | all-reduce | flops 48 | bytes 384 | tf_op jit(solution)/shard_map/psum | solution.py:94
  15.7 1.1 %broadcast_subtract_fusion = f32[16,3,2048]{2,0,1:T(8,128)S(1)} fusion(f32[16,3,2048]{2,0,1:T(8,128)} %param.7, f32[16,3]{0,1:T(4,128)S(1)} %broadcast_multiply_fusion.3), kind=kLoop, calls=%fused_computation.42 | loop fusion | flops 98304 | bytes 786624 | tf_op jit(solution)/shard_map/sub | solution.py:95
  16.8 0.5 reshape.156
  17.4 2.1 %copy.28 = f32[16,3,64,32]{3,0,1,2:T(8,128)} copy(f32[16,3,64,32]{3,2,0,1:T(8,128)S(1)} %reshape.156) | data formatting | bytes 786432 | tf_op jit(solution)/shard_map/reshape | solution.py:96
  19.4 2.8 %reshape.163 = f32[64,1,1536]{2,1,0:T(1,128)} reshape(f32[64,3,16,32]{3,2,1,0:T(8,128)} %bitcast.25) | data formatting | bytes 786432
  22.3 16.5 %all-to-all-start = ((f32[64,1,1536]{2,1,0:T(1,128)}), f32[64,1,1536]{2,1,0:T(1,128)S(1)}, u32[]{:S(2)}, u32[]{:S(2)}) async-start(f32[64,1,1536]{2,1,0:T(1,128)} %reshape.163), calls=%async_computation | async-start | bytes 786432 | tf_op jit(solution)/shard_map/all_to_all | solution.py:97
  38.8 0.5 multiply_subtract_fusion
  39.3 1.5 %slice.119 = f32[512,1024]{1,0:T(8,128)} slice(f32[544,1024]{1,0:T(8,128)S(1)} %bitcast.24), slice={[1:513], [0:1024]} | slice | bytes 4194304 | tf_op jit(solution)/shard_map/slice | solution.py:59
  40.8 1.6 %slice.118 = f32[513,1024]{1,0:T(8,128)} slice(f32[544,1024]{1,0:T(8,128)S(1)} %bitcast.22), slice={[0:513], [0:1024]} | slice | bytes 4202496 | tf_op jit(solution)/shard_map/slice | solution.py:28
  42.5 0.6 iota_compare_fusion.3
  43.1 0.6 fusion.54
  43.6 0.6 select_multiply_fusion
  44.2 0.6 iota_subtract_fusion
  44.8 8.4 %all-to-all-done = f32[64,1,1536]{2,1,0:T(1,128)S(1)} async-done(((f32[64,1,1536]{2,1,0:T(1,128)}), f32[64,1,1536]{2,1,0:T(1,128)S(1)}, u32[]{:S(2)}, u32[]{:S(2)}) %all-to-all-start) | async-done | bytes 393248 | tf_op jit(solution)/shard_map/all_to_all | solution.py:97
  53.3 0.5 broadcast.231
  53.8 1.6 %reduce.6 = f32[64,1536]{1,0:T(8,128)S(1)} reduce(f32[64,1,1536]{2,1,0:T(1,128)S(1)} %all-to-all-done, f32[]{:T(128)} %broadcast.231), dimensions={1}, to_apply=%all_to_all.11.reduce_sub_computation | reduce | bytes 786436 | tf_op jit(solution)/shard_map/all_to_all | solution.py:97
  55.4 1.6 %reshape.164 = f32[64,3,16,32]{3,2,1,0:T(8,128)} reshape(f32[64,1536]{1,0:T(8,128)S(1)} %reduce.6) | data formatting | bytes 786432
  57.0 1.5 %bitcast_bitcast_fusion = f32[64,16,3,1,32]{4,1,2,0,3:T(8,128)S(1)} fusion(f32[64,3,16,32]{3,2,1,0:T(8,128)} %reshape.164), kind=kLoop, calls=%fused_computation.107 | loop fusion | bytes 786432 | tf_op jit(solution)/shard_map/all_to_all | solution.py:97
  58.5 2.2 %copy.21 = f32[64,16,3,1,32]{4,2,1,0,3:T(4,128)} copy(f32[64,16,3,1,32]{4,1,2,0,3:T(8,128)S(1)} %bitcast_bitcast_fusion) | data formatting | bytes 786432 | tf_op jit(solution)/shard_map/all_to_all | solution.py:97
  60.7 2.7 %reshape.157 = f32[1024,96]{1,0:T(8,128)S(1)} reshape(f32[64,16,3,1,32]{4,2,1,0,3:T(4,128)} %copy.21) | data formatting | bytes 786432 | tf_op jit(solution)/shard_map/reshape | solution.py:99
  63.3 0.1 reduce-precision_convert_fusion.1
  63.5 1.3 %fusion.5 = f32[1024,288]{0,1:T(8,128)S(1)} fusion(bf16[1024,96]{1,0:T(8,128)(2,1)S(1)} %get-tuple-element.22, bf16[1024,96]{1,0:T(8,128)(2,1)S(1)} %get-tuple-element.23, bf16[1024,96]{1,0:T(8,128)(2,1)S(1)} %get-tuple-element.21), kind=kOutput, calls=%fused_computation.12 | convolution fusion | flops 608894976 | bytes 1769472 | tf_op jit(solution)/shard_map/dot_general | solution.py:43
  65.0 0.7 reduce-precision_convert_fusion.3
  65.6 6.7 %fusion = f32[1025,192]{0,1:T(8,128)S(1)} fusion(f32[512,1024]{1,0:T(8,128)} %slice.119, f32[513,1024]{1,0:T(8,128)} %slice.118, f32[1024,96]{0,1:T(8,128)S(1)} %get-tuple-element.19, f32[1024,96]{0,1:T(8,128)S(1)} %get-tuple-element.20), kind=kOutput, calls=%fused_computation.2 | convolution fusion | flops 2419524608 | bytes 5772032 | tf_op jit(solution)/shard_map/dot_general | solution.py:61
  72.4 0.2 slice.121
  72.6 0.2 fusion.18
  73.2 1.4 %fusion.7 = f32[513,128]{0,1:T(8,128)S(1)} fusion(f32[544,1024]{1,0:T(8,128)S(1)} %bitcast.23, f32[512,64]{0,1:T(8,128)S(1)} %broadcast_multiply_fusion.1, f32[512,64]{0,1:T(8,128)S(1)} %bitcast.27), kind=kOutput, calls=%fused_computation.14 | convolution fusion | flops 403505152 | bytes 1589760 | tf_op jit(solution)/shard_map/dot_general | solution.py:74
  74.7 0.1 slice_add_fusion.4
  74.8 0.3 reverse
  75.2 0.9 %fusion.4 = f32[1024,96]{0,1:T(8,128)S(1)} fusion(s32[1024]{0:T(1024)S(1)} %copy-done.7, bf16[1024,32]{0,1:T(8,128)(2,1)S(1)} %get-tuple-element.30, bf16[1024,32]{0,1:T(8,128)(2,1)S(1)} %copy-done.4, bf16[1024,32]{0,1:T(8,128)(2,1)S(1)} %get-tuple-element.29), kind=kOutput, calls=%fused_computation.11 | convolution fusion | flops 208207872 | bytes 593920 | tf_op jit(solution)/shard_map/dot_general | solution.py:43
  76.1 0.7 fusion.30
  (33 shorter events, 0.8 us)
Async XLA Ops:
  17.3 21.4 %copy-start = (f32[32,1024]{1,0:T(8,128)S(1)}, f32[32,1024]{1,0:T(8,128)}, u32[]{:S(2)}) copy-start(f32[32,1024]{1,0:T(8,128)} %constant.115.clone) | copy-start | bytes 393220
  17.3 21.4 %copy-start.1 = (f32[32,1024]{1,0:T(8,128)S(1)}, f32[32,1024]{1,0:T(8,128)}, u32[]{:S(2)}) copy-start(f32[32,1024]{1,0:T(8,128)} %constant.114.clone) | copy-start | bytes 393220
  17.3 21.4 %copy-start.2 = (f32[17,1024]{1,0:T(8,128)S(1)}, f32[17,1024]{1,0:T(8,128)}, u32[]{:S(2)}) copy-start(f32[17,1024]{1,0:T(8,128)} %constant.120) | copy-start | bytes 208900
  17.3 21.4 %copy-start.3 = (f32[17,1024]{1,0:T(8,128)S(1)}, f32[17,1024]{1,0:T(8,128)}, u32[]{:S(2)}) copy-start(f32[17,1024]{1,0:T(8,128)} %constant.119) | copy-start | bytes 208900
  22.3 31.0 %all-to-all-start = ((f32[64,1,1536]{2,1,0:T(1,128)}), f32[64,1,1536]{2,1,0:T(1,128)S(1)}, u32[]{:S(2)}, u32[]{:S(2)}) async-start(f32[64,1,1536]{2,1,0:T(1,128)} %reshape.163), calls=%async_computation | async-start | bytes 786432 | tf_op jit(solution)/shard_map/all_to_all | solution.py:97
  72.4 0.7 copy-start.6
  72.4 0.7 copy-start.8
  72.4 0.8 %copy-start.5 = (f32[512]{0:T(512)S(1)}, f32[512]{0:T(512)}, u32[]{:S(2)}) copy-start(f32[512]{0:T(512)} %fusion.54) | copy-start | bytes 6148
  72.8 2.4 %copy-start.4 = (bf16[1024,32]{0,1:T(8,128)(2,1)S(1)}, bf16[1024,32]{0,1:T(8,128)(2,1)}, u32[]{:S(2)}) copy-start(bf16[1024,32]{0,1:T(8,128)(2,1)} %get-tuple-element.31) | copy-start | bytes 196612
  72.8 2.4 %copy-start.7 = (s32[1024]{0:T(1024)S(1)}, s32[1024]{0:T(1024)}, u32[]{:S(2)}) copy-start(s32[1024]{0:T(1024)} %iota_subtract_fusion) | copy-start | bytes 12292

commit v3 on v2

--- a/solution.py
+++ b/solution.py
@@ -93,10 +93,11 @@
     atom_total = atom_count * lax.axis_size("atoms")
     summed = lax.psum(jnp.sum(displacements, axis=2), "atoms")
     centred = displacements - (summed / atom_total)[:, :, None]
-    blocks = centred.reshape(local_frames, 3, groups, atom_count // groups)
-    moved = lax.all_to_all(blocks, "frames", split_axis=2, concat_axis=0, tiled=True)
     count = atom_count // groups
-    series = moved.reshape(local_frames * groups, 3 * count)
+    blocks = centred.reshape(local_frames, 3, groups, count)
+    outgoing = jnp.transpose(blocks, (2, 0, 1, 3)).reshape(groups, local_frames * 3 * count)
+    moved = lax.all_to_all(outgoing, "frames", split_axis=0, concat_axis=0, tiled=True)
+    series = moved.reshape(groups * local_frames, 3 * count)
     return lag_table(series, count)
 
 

time: 77.3 us -> 64.8 us (0.84)
  local copies, waits for them, and re-layouts: 17.8 us -> 6.01 us
    reshape x3 -> x2, local copies, waits for them, and re-layouts: 5.23 us -> 0.68 us  [the longest x1 0.51 us: per_device(): blocks = centred.reshape(local_frames, 3, groups, count)]
    unnamed x22 -> x20, local copies, waits for them, and re-layouts: 5.01 us -> 0.54 us
    all_to_all x3 -> x1, local copies, waits for them, and re-layouts: 4.2 us -> 1.08 us  [per_device(): lax.all_to_all(outgoing, 'frames', split_axis=0, concat_axis=0, tiled=True)]
  transfers between devices with their start and end apart: 1 -> 1, of which waited for: 1 -> 1; matrix products, arithmetic and copies ran while one was open for 8% -> 9% of each run, Pallas kernels for 0% -> 0%
where the time goes in v3:
time: 64.8 us; the launch traced here: 64.5 us
  starting transfers between devices  16.5 us (25%)
  blocking collectives  14.6 us (23%)
  matrix products  10.3 us (16%)
  waiting for transfers between devices  8.64 us (13%)
  other arithmetic  8.22 us (13%)
  local copies, waits for them, and re-layouts  6.01 us (9%)
    all_to_all x1, starting transfers between devices, per_device(): lax.all_to_all(outgoing, 'frames', split_axis=0, concat_axis=0, tiled=True)  16.5 us
    psum x1, blocking collectives, per_device(): summed = lax.psum(jnp.sum(displacements, axis=2), 'atoms')  14.6 us
    all_to_all x1, waiting for transfers between devices, per_device(): lax.all_to_all(outgoing, 'frames', split_axis=0, concat_axis=0, tiled=True)  8.64 us
    dot_general x1, matrix products, lag_table(): spectrum = jnp.dot(both, signed, precision=lax.Precision.HIGHEST)  6.73 us
    dot_general x2, matrix products, exact_product(): jnp.dot(matrix.astype(jnp.bfloat16), split_three(values), preferred_eleme...  2.2 us
    slice x1, local copies, waits for them, and re-layouts, lag_table(): both = jnp.concatenate([cosine, sine[1:]], axis=0)  1.53 us
    slice x1, local copies, waits for them, and re-layouts, spectral_tables(): cosine = cosine.reshape(blocks * split, length)[:rows]  1.49 us
    dot_general x1, matrix products, lag_table(): folded = jnp.dot(table, coef, precision=lax.Precision.HIGHEST)  1.41 us
  transfers between devices with their start and end apart: 1, of which 1 were waited for; matrix products, arithmetic and copies ran while one was open for 9% of the time, Pallas kernels for 0%

profile of v3, /device:TPU:16, one launch (start us, length us, event | category | flops | bytes accessed | tf_op | source)
XLA Modules:
  0.0 64.5 jit_solution(11843583636242428239)
XLA Ops:
  0.0 1.1 %reduce_sum.27 = f32[16,3]{0,1:T(4,128)S(1)} reduce(f32[16,3,2048]{2,0,1:T(8,128)} %param.7, f32[]{:T(128)} %constant.99.clone.1), dimensions={2}, to_apply=%region_0.0 | reduce | flops 98256 | bytes 393412 | tf_op jit(solution)/shard_map/reduce_sum | solution.py:94
  1.1 14.6 %psum.7 = f32[16,3]{0,1:T(4,128)S(1)} all-reduce(f32[16,3]{0,1:T(4,128)S(1)} %reduce_sum.27), channel_id=1, replica_groups=mesh['frames'=64,'atoms'=8] {'atoms'}, use_global_device_ids=true, to_apply=%region_1.0 | all-reduce | flops 48 | bytes 384 | tf_op jit(solution)/shard_map/psum | solution.py:94
  15.7 1.1 %broadcast_subtract_fusion = f32[16,3,2048]{2,0,1:T(8,128)S(1)} fusion(f32[16,3,2048]{2,0,1:T(8,128)} %param.7, f32[16,3]{0,1:T(4,128)S(1)} %broadcast_multiply_fusion.3), kind=kLoop, calls=%fused_computation.42 | loop fusion | flops 98304 | bytes 786624 | tf_op jit(solution)/shard_map/sub | solution.py:95
  16.8 0.5 reshape.160
  17.4 0.5 copy.22
  17.8 1.1 %copy.23 = f32[64,1,1536]{2,1,0:T(1,128)} copy(f32[64,1,1536]{0,2,1:T(8,128)S(1)} %bitcast.17) | data formatting | bytes 786432 | tf_op jit(solution)/shard_map/all_to_all | solution.py:99
  18.9 16.5 %all-to-all-start = ((f32[64,1,1536]{2,1,0:T(1,128)}), f32[64,1,1536]{2,1,0:T(1,128)S(1)}, u32[]{:S(2)}, u32[]{:S(2)}) async-start(f32[64,1,1536]{2,1,0:T(1,128)} %copy.23), calls=%async_computation | async-start | bytes 786432 | tf_op jit(solution)/shard_map/all_to_all | solution.py:99
  35.4 0.5 multiply_subtract_fusion
  35.9 1.5 %slice.119 = f32[512,1024]{1,0:T(8,128)} slice(f32[544,1024]{1,0:T(8,128)S(1)} %bitcast.15), slice={[1:513], [0:1024]} | slice | bytes 4194304 | tf_op jit(solution)/shard_map/slice | solution.py:59
  37.4 1.5 %slice.118 = f32[513,1024]{1,0:T(8,128)} slice(f32[544,1024]{1,0:T(8,128)S(1)} %bitcast.13), slice={[0:513], [0:1024]} | slice | bytes 4202496 | tf_op jit(solution)/shard_map/slice | solution.py:28
  39.0 0.5 iota_compare_fusion.3
  39.5 0.6 fusion.54
  40.1 0.6 select_multiply_fusion
  40.7 0.6 iota_subtract_fusion
  41.3 8.6 %all-to-all-done = f32[64,1,1536]{2,1,0:T(1,128)S(1)} async-done(((f32[64,1,1536]{2,1,0:T(1,128)}), f32[64,1,1536]{2,1,0:T(1,128)S(1)}, u32[]{:S(2)}, u32[]{:S(2)}) %all-to-all-start) | async-done | bytes 393248 | tf_op jit(solution)/shard_map/all_to_all | solution.py:99
  49.9 0.9 %reduce.2 = f32[64,1536]{1,0:T(8,128)S(1)} reduce(f32[64,1,1536]{2,1,0:T(1,128)S(1)} %all-to-all-done, f32[]{:T(128)} %constant.121), dimensions={1}, to_apply=%all_to_all.7.reduce_sub_computation | reduce | bytes 786436 | tf_op jit(solution)/shard_map/all_to_all | solution.py:99
  50.8 0.2 reshape.161
  51.0 0.1 reduce-precision_convert_fusion.1
  51.2 1.3 %fusion.5 = f32[1024,288]{0,1:T(8,128)S(1)} fusion(bf16[1024,96]{1,0:T(8,128)(2,1)S(1)} %get-tuple-element.22, bf16[1024,96]{1,0:T(8,128)(2,1)S(1)} %get-tuple-element.23, bf16[1024,96]{1,0:T(8,128)(2,1)S(1)} %get-tuple-element.21), kind=kOutput, calls=%fused_computation.12 | convolution fusion | flops 608894976 | bytes 1769472 | tf_op jit(solution)/shard_map/dot_general | solution.py:43
  52.5 0.1 broadcast_multiply_fusion
  52.7 0.7 %reduce-precision_convert_fusion.3 = (bf16[1024,32]{0,1:T(8,128)(2,1)S(1)}, bf16[1024,32]{0,1:T(8,128)(2,1)S(1)}, bf16[1024,32]{0,1:T(8,128)(2,1)}) fusion(f32[1024,32]{0,1:T(8,128)S(1)} %reduce_sum.28), kind=kLoop, calls=%fused_computation.46 | loop fusion | flops 229376 | bytes 327680 | tf_op jit(solution)/shard_map/convert
  53.3 6.7 %fusion = f32[1025,192]{0,1:T(8,128)S(1)} fusion(f32[512,1024]{1,0:T(8,128)} %slice.119, f32[513,1024]{1,0:T(8,128)} %slice.118, f32[1024,96]{0,1:T(8,128)S(1)} %get-tuple-element.19, f32[1024,96]{0,1:T(8,128)S(1)} %get-tuple-element.20), kind=kOutput, calls=%fused_computation.2 | convolution fusion | flops 2419524608 | bytes 5772032 | tf_op jit(solution)/shard_map/dot_general | solution.py:61
  60.1 0.2 slice.121
  60.3 0.2 fusion.18
  60.5 0.1 fusion.35
  60.6 0.1 copy-done.6
  60.9 1.4 %fusion.7 = f32[513,128]{0,1:T(8,128)S(1)} fusion(f32[544,1024]{1,0:T(8,128)S(1)} %bitcast.14, f32[512,64]{0,1:T(8,128)S(1)} %broadcast_multiply_fusion.1, f32[512,64]{0,1:T(8,128)S(1)} %bitcast.19), kind=kOutput, calls=%fused_computation.14 | convolution fusion | flops 403505152 | bytes 1589760 | tf_op jit(solution)/shard_map/dot_general | solution.py:74
  62.3 0.1 fusion.32
  62.4 0.1 slice_add_fusion.4
  62.5 0.3 reverse
  62.9 0.9 %fusion.4 = f32[1024,96]{0,1:T(8,128)S(1)} fusion(s32[1024]{0:T(1024)S(1)} %copy-done.7, bf16[1024,32]{0,1:T(8,128)(2,1)S(1)} %get-tuple-element.30, bf16[1024,32]{0,1:T(8,128)(2,1)S(1)} %copy-done.4, bf16[1024,32]{0,1:T(8,128)(2,1)S(1)} %get-tuple-element.29), kind=kOutput, calls=%fused_computation.11 | convolution fusion | flops 208207872 | bytes 593920 | tf_op jit(solution)/shard_map/dot_general | solution.py:43
  63.8 0.7 %fusion.30 = f32[32,1024]{1,0:T(8,128)} fusion(f32[1024,96]{0,1:T(8,128)S(1)} %fusion.4, f32[511,32]{0,1:T(8,128)S(1)} %slice.178, f32[513,32]{0,1:T(8,128)S(1)} %get-tuple-element.26, f32[1024]{0:T(1024)S(1)} %subtract_convert_fusion), kind=kLoop, calls=%fused_computation.52 | loop fusion | flops 196608 | bytes 659456 | tf_op jit(solution)/shard_map/transpose | solution.py:87
  (29 shorter events, 0.4 us)
Async XLA Ops:
  17.3 18.1 %copy-start = (f32[32,1024]{1,0:T(8,128)S(1)}, f32[32,1024]{1,0:T(8,128)}, u32[]{:S(2)}) copy-start(f32[32,1024]{1,0:T(8,128)} %constant.115.clone) | copy-start | bytes 393220
  17.3 18.1 %copy-start.1 = (f32[32,1024]{1,0:T(8,128)S(1)}, f32[32,1024]{1,0:T(8,128)}, u32[]{:S(2)}) copy-start(f32[32,1024]{1,0:T(8,128)} %constant.114.clone) | copy-start | bytes 393220
  17.3 18.1 %copy-start.2 = (f32[17,1024]{1,0:T(8,128)S(1)}, f32[17,1024]{1,0:T(8,128)}, u32[]{:S(2)}) copy-start(f32[17,1024]{1,0:T(8,128)} %constant.120) | copy-start | bytes 208900
  17.4 18.1 %copy-start.3 = (f32[17,1024]{1,0:T(8,128)S(1)}, f32[17,1024]{1,0:T(8,128)}, u32[]{:S(2)}) copy-start(f32[17,1024]{1,0:T(8,128)} %constant.119) | copy-start | bytes 208900
  18.9 31.0 %all-to-all-start = ((f32[64,1,1536]{2,1,0:T(1,128)}), f32[64,1,1536]{2,1,0:T(1,128)S(1)}, u32[]{:S(2)}, u32[]{:S(2)}) async-start(f32[64,1,1536]{2,1,0:T(1,128)} %copy.23), calls=%async_computation | async-start | bytes 786432 | tf_op jit(solution)/shard_map/all_to_all | solution.py:99
  60.1 0.7 %copy-start.6 = (f32[512]{0:T(512)S(1)}, f32[512]{0:T(512)}, u32[]{:S(2)}) copy-start(f32[512]{0:T(512)} %select_multiply_fusion) | copy-start | bytes 6148
  60.1 0.7 %copy-start.8 = (pred[512]{0:T(512)(128)(4,1)S(1)}, pred[512]{0:T(512)(128)(4,1)}, u32[]{:S(2)}) copy-start(pred[512]{0:T(512)(128)(4,1)} %iota_compare_fusion.3) | copy-start | bytes 1540
  60.1 0.8 %copy-start.5 = (f32[512]{0:T(512)S(1)}, f32[512]{0:T(512)}, u32[]{:S(2)}) copy-start(f32[512]{0:T(512)} %fusion.54) | copy-start | bytes 6148
  60.5 2.4 %copy-start.4 = (bf16[1024,32]{0,1:T(8,128)(2,1)S(1)}, bf16[1024,32]{0,1:T(8,128)(2,1)}, u32[]{:S(2)}) copy-start(bf16[1024,32]{0,1:T(8,128)(2,1)} %get-tuple-element.31) | copy-start | bytes 196612
  60.5 2.4 %copy-start.7 = (s32[1024]{0:T(1024)S(1)}, s32[1024]{0:T(1024)}, u32[]{:S(2)}) copy-start(s32[1024]{0:T(1024)} %iota_subtract_fusion) | copy-start | bytes 12292

commit v4 on v3

--- a/solution.py
+++ b/solution.py
@@ -91,7 +91,11 @@
     local_frames, _, atom_count = displacements.shape
     groups = lax.axis_size("frames")
     atom_total = atom_count * lax.axis_size("atoms")
-    summed = lax.psum(jnp.sum(displacements, axis=2), "atoms")
+    members = lax.axis_size("atoms")
+    partial_sum = jnp.sum(displacements, axis=2).reshape(1, local_frames * 3)
+    spread = jnp.broadcast_to(partial_sum, (members, local_frames * 3))
+    gathered = lax.all_to_all(spread, "atoms", split_axis=0, concat_axis=0, tiled=True)
+    summed = jnp.sum(gathered, axis=0).reshape(local_frames, 3)
     centred = displacements - (summed / atom_total)[:, :, None]
     count = atom_count // groups
     blocks = centred.reshape(local_frames, 3, groups, count)

time: 64.8 us -> 65.1 us (level)
  the two profiles are of different devices: /device:TPU:16 before, /device:TPU:2 now
where the time goes in v4:
time: 65.1 us; the launch traced here: 64.7 us
  starting transfers between devices  21.4 us (33%)
  waiting for transfers between devices  14.8 us (23%)
  matrix products  10.3 us (16%)
  local copies, waits for them, and re-layouts  9.64 us (15%)
  other arithmetic  8.32 us (13%)
    all_to_all x1, waiting for transfers between devices, per_device(): lax.all_to_all(outgoing, 'frames', split_axis=0, concat_axis=0, tiled=True)  14.8 us
    all_to_all x1, starting transfers between devices, per_device(): lax.all_to_all(outgoing, 'frames', split_axis=0, concat_axis=0, tiled=True)  12.3 us
    all_to_all x1, starting transfers between devices, per_device(): lax.all_to_all(spread, 'atoms', split_axis=0, concat_axis=0, tiled=True)  9.13 us
    dot_general x1, matrix products, lag_table(): spectrum = jnp.dot(both, signed, precision=lax.Precision.HIGHEST)  6.73 us
    dot_general x2, matrix products, exact_product(): jnp.dot(matrix.astype(jnp.bfloat16), split_three(values), preferred_eleme...  2.18 us
    transpose x1, local copies, waits for them, and re-layouts, per_device(): jnp.transpose(blocks, (2, 0, 1, 3))  1.86 us
    reshape x1, local copies, waits for them, and re-layouts, per_device(): blocks = centred.reshape(local_frames, 3, groups, count)  1.7 us
    slice x1, local copies, waits for them, and re-layouts, spectral_tables(): cosine = cosine.reshape(blocks * split, length)[:rows]  1.6 us
  transfers between devices with their start and end apart: 2, of which 1 were waited for; matrix products, arithmetic and copies ran while one was open for 11% of the time, Pallas kernels for 0%

profile of v4, /device:TPU:2, one launch (start us, length us, event | category | flops | bytes accessed | tf_op | source)
XLA Modules:
  0.0 64.7 jit_solution(6005077855699717746)
XLA Ops:
  0.0 1.1 %reduce_sum.36 = f32[16,3]{0,1:T(4,128)S(1)} reduce(f32[16,3,2048]{2,0,1:T(8,128)} %param.7, f32[]{:T(128)} %constant.99.clone.1), dimensions={2}, to_apply=%region_0.0 | reduce | flops 98256 | bytes 393412 | tf_op jit(solution)/shard_map/reduce_sum | solution.py:95
  1.2 0.1 broadcast_in_dim.82
  1.3 0.6 broadcast_in_dim.83
  1.9 9.1 %all-to-all-start = ((f32[8,1,48]{2,1,0:T(1,128)}), f32[8,1,48]{2,1,0:T(1,128)S(1)}, u32[]{:S(2)}, u32[]{:S(2)}) async-start(f32[8,1,48]{2,1,0:T(1,128)} %broadcast_in_dim.83), calls=%async_computation | async-start | bytes 8192 | tf_op jit(solution)/shard_map/all_to_all | solution.py:97
  11.0 1.5 %multiply_subtract_fusion = (f32[17,32,1024]{2,1,0:T(8,128)S(1)}, f32[17,32,1024]{2,1,0:T(8,128)S(1)}) fusion(f32[32,1024]{1,0:T(8,128)} %constant.115.clone, f32[17,1024]{1,0:T(8,128)} %constant.120, f32[32,1024]{1,0:T(8,128)} %constant.114.clone, f32[17,1024]{1,0:T(8,128)} %constant.119), kind=kLoop, calls=%fused_computation.10 | loop fusion | flops 3342336 | bytes 4857856 | tf_op jit(solution)/shard_map/sub | solution.py:26
  12.5 1.5 %slice.119 = f32[512,1024]{1,0:T(8,128)} slice(f32[544,1024]{1,0:T(8,128)S(1)} %bitcast.16), slice={[1:513], [0:1024]} | slice | bytes 4194304 | tf_op jit(solution)/shard_map/slice | solution.py:59
  14.1 1.6 %slice.118 = f32[513,1024]{1,0:T(8,128)} slice(f32[544,1024]{1,0:T(8,128)S(1)} %bitcast.14), slice={[0:513], [0:1024]} | slice | bytes 4202496 | tf_op jit(solution)/shard_map/slice | solution.py:28
  15.9 0.1 broadcast_subtract_fusion
  16.0 1.7 %reshape.176 = f32[16,3,64,32]{3,2,0,1:T(8,128)} reshape(f32[16,3,2048]{2,0,1:T(8,128)S(1)} %broadcast_subtract_fusion) | data formatting | bytes 786432 | tf_op jit(solution)/shard_map/reshape | solution.py:101
  17.7 1.9 %copy.44 = f32[64,16,3,32]{0,3,2,1:T(8,128)S(1)} copy(f32[64,16,3,32]{3,0,1,2:T(8,128)} %bitcast.17) | data formatting | bytes 786432 | tf_op jit(solution)/shard_map/transpose | solution.py:102
  19.6 1.1 %copy.45 = f32[64,1,1536]{2,1,0:T(1,128)} copy(f32[64,1,1536]{0,2,1:T(8,128)S(1)} %bitcast.18) | data formatting | bytes 786432 | tf_op jit(solution)/shard_map/all_to_all | solution.py:103
  20.6 12.3 %all-to-all-start.1 = ((f32[64,1,1536]{2,1,0:T(1,128)}), f32[64,1,1536]{2,1,0:T(1,128)S(1)}, u32[]{:S(2)}, u32[]{:S(2)}) async-start(f32[64,1,1536]{2,1,0:T(1,128)} %copy.45), calls=%async_computation.1 | async-start | bytes 786432 | tf_op jit(solution)/shard_map/all_to_all | solution.py:103
  33.0 0.5 iota_compare_fusion.3
  33.5 0.6 fusion.54
  34.1 0.6 select_multiply_fusion
  34.7 0.6 iota_subtract_fusion
  35.3 14.8 %all-to-all-done.1 = f32[64,1,1536]{2,1,0:T(1,128)S(1)} async-done(((f32[64,1,1536]{2,1,0:T(1,128)}), f32[64,1,1536]{2,1,0:T(1,128)S(1)}, u32[]{:S(2)}, u32[]{:S(2)}) %all-to-all-start.1) | async-done | bytes 393248 | tf_op jit(solution)/shard_map/all_to_all | solution.py:103
  50.1 0.9 %reduce.3 = f32[64,1536]{1,0:T(8,128)S(1)} reduce(f32[64,1,1536]{2,1,0:T(1,128)S(1)} %all-to-all-done.1, f32[]{:T(128)} %constant.121), dimensions={1}, to_apply=%all_to_all.12.reduce_sub_computation | reduce | bytes 786436 | tf_op jit(solution)/shard_map/all_to_all | solution.py:103
  51.0 0.2 reshape.177
  51.2 0.1 reduce-precision_convert_fusion.1
  51.4 1.3 %fusion.5 = f32[1024,288]{0,1:T(8,128)S(1)} fusion(bf16[1024,96]{1,0:T(8,128)(2,1)S(1)} %get-tuple-element.22, bf16[1024,96]{1,0:T(8,128)(2,1)S(1)} %get-tuple-element.23, bf16[1024,96]{1,0:T(8,128)(2,1)S(1)} %get-tuple-element.21), kind=kOutput, calls=%fused_computation.12 | convolution fusion | flops 608894976 | bytes 1769472 | tf_op jit(solution)/shard_map/dot_general | solution.py:43
  52.8 0.7 %reduce-precision_convert_fusion.3 = (bf16[1024,32]{0,1:T(8,128)(2,1)S(1)}, bf16[1024,32]{0,1:T(8,128)(2,1)S(1)}, bf16[1024,32]{0,1:T(8,128)(2,1)}) fusion(f32[1024,32]{0,1:T(8,128)S(1)} %reduce_sum.38), kind=kLoop, calls=%fused_computation.46 | loop fusion | flops 229376 | bytes 327680 | tf_op jit(solution)/shard_map/convert
  53.5 6.7 %fusion = f32[1025,192]{0,1:T(8,128)S(1)} fusion(f32[512,1024]{1,0:T(8,128)} %slice.119, f32[513,1024]{1,0:T(8,128)} %slice.118, f32[1024,96]{0,1:T(8,128)S(1)} %get-tuple-element.19, f32[1024,96]{0,1:T(8,128)S(1)} %get-tuple-element.20), kind=kOutput, calls=%fused_computation.2 | convolution fusion | flops 2419524608 | bytes 5772032 | tf_op jit(solution)/shard_map/dot_general | solution.py:61
  60.3 0.2 slice.121
  60.4 0.2 fusion.18
  60.7 0.1 fusion.35
  60.8 0.1 copy-done.3
  61.0 1.4 %fusion.7 = f32[513,128]{0,1:T(8,128)S(1)} fusion(f32[544,1024]{1,0:T(8,128)S(1)} %bitcast.15, f32[512,64]{0,1:T(8,128)S(1)} %broadcast_multiply_fusion.1, f32[512,64]{0,1:T(8,128)S(1)} %bitcast.20), kind=kOutput, calls=%fused_computation.14 | convolution fusion | flops 403505152 | bytes 1589760 | tf_op jit(solution)/shard_map/dot_general | solution.py:74
  62.5 0.1 slice_add_fusion.4
  62.7 0.3 reverse
  63.1 0.9 %fusion.4 = f32[1024,96]{0,1:T(8,128)S(1)} fusion(s32[1024]{0:T(1024)S(1)} %copy-done.4, bf16[1024,32]{0,1:T(8,128)(2,1)S(1)} %get-tuple-element.30, bf16[1024,32]{0,1:T(8,128)(2,1)S(1)} %copy-done.1, bf16[1024,32]{0,1:T(8,128)(2,1)S(1)} %get-tuple-element.29), kind=kOutput, calls=%fused_computation.11 | convolution fusion | flops 208207872 | bytes 593920 | tf_op jit(solution)/shard_map/dot_general | solution.py:43
  64.0 0.7 %fusion.30 = f32[32,1024]{1,0:T(8,128)} fusion(f32[1024,96]{0,1:T(8,128)S(1)} %fusion.4, f32[511,32]{0,1:T(8,128)S(1)} %slice.178, f32[513,32]{0,1:T(8,128)S(1)} %get-tuple-element.26, f32[1024]{0:T(1024)S(1)} %subtract_convert_fusion), kind=kLoop, calls=%fused_computation.52 | loop fusion | flops 196608 | bytes 659456 | tf_op jit(solution)/shard_map/transpose | solution.py:87
  (30 shorter events, 0.9 us)
Async XLA Ops:
  1.9 13.8 %all-to-all-start = ((f32[8,1,48]{2,1,0:T(1,128)}), f32[8,1,48]{2,1,0:T(1,128)S(1)}, u32[]{:S(2)}, u32[]{:S(2)}) async-start(f32[8,1,48]{2,1,0:T(1,128)} %broadcast_in_dim.83), calls=%async_computation | async-start | bytes 8192 | tf_op jit(solution)/shard_map/all_to_all | solution.py:97
  14.1 1.8 %copy-start = (f32[16,3,2048]{2,0,1:T(8,128)S(1)}, f32[16,3,2048]{2,0,1:T(8,128)}, u32[]{:S(2)}) copy-start(f32[16,3,2048]{2,0,1:T(8,128)} %param.7) | copy-start | bytes 1179652
  20.6 29.5 %all-to-all-start.1 = ((f32[64,1,1536]{2,1,0:T(1,128)}), f32[64,1,1536]{2,1,0:T(1,128)S(1)}, u32[]{:S(2)}, u32[]{:S(2)}) async-start(f32[64,1,1536]{2,1,0:T(1,128)} %copy.45), calls=%async_computation.1 | async-start | bytes 786432 | tf_op jit(solution)/shard_map/all_to_all | solution.py:103
  60.2 0.7 %copy-start.3 = (f32[512]{0:T(512)S(1)}, f32[512]{0:T(512)}, u32[]{:S(2)}) copy-start(f32[512]{0:T(512)} %select_multiply_fusion) | copy-start | bytes 6148
  60.2 0.7 %copy-start.5 = (pred[512]{0:T(512)(128)(4,1)S(1)}, pred[512]{0:T(512)(128)(4,1)}, u32[]{:S(2)}) copy-start(pred[512]{0:T(512)(128)(4,1)} %iota_compare_fusion.3) | copy-start | bytes 1540
  60.3 0.8 %copy-start.2 = (f32[512]{0:T(512)S(1)}, f32[512]{0:T(512)}, u32[]{:S(2)}) copy-start(f32[512]{0:T(512)} %fusion.54) | copy-start | bytes 6148
  60.6 2.4 %copy-start.1 = (bf16[1024,32]{0,1:T(8,128)(2,1)S(1)}, bf16[1024,32]{0,1:T(8,128)(2,1)}, u32[]{:S(2)}) copy-start(bf16[1024,32]{0,1:T(8,128)(2,1)} %get-tuple-element.31) | copy-start | bytes 196612
  60.7 2.4 %copy-start.4 = (s32[1024]{0:T(1024)S(1)}, s32[1024]{0:T(1024)}, u32[]{:S(2)}) copy-start(s32[1024]{0:T(1024)} %iota_subtract_fusion) | copy-start | bytes 12292

commit v5 on v4

--- a/solution.py
+++ b/solution.py
@@ -18,16 +18,16 @@
     ]
 
 
-def spectral_tables(length, rows):
+def spectral_tables(length, rows, anchor):
     split = 32
+    blocks = rows // split
     cos_hi, sin_hi, cos_lo, sin_lo = angle_tables(length, split)
-    blocks = -(-rows // split)
-    cos_hi, sin_hi = cos_hi[:blocks], sin_hi[:blocks]
+    cos_hi, sin_hi, cos_lo, sin_lo, _ = lax.optimization_barrier(
+        (cos_hi[:blocks], sin_hi[:blocks], cos_lo, sin_lo, anchor)
+    )
     cosine = cos_hi[:, None, :] * cos_lo[None, :, :] - sin_hi[:, None, :] * sin_lo[None, :, :]
     sine = sin_hi[:, None, :] * cos_lo[None, :, :] + cos_hi[:, None, :] * sin_lo[None, :, :]
-    cosine = cosine.reshape(blocks * split, length)[:rows]
-    sine = sine.reshape(blocks * split, length)[:rows]
-    return cosine, sine
+    return cosine.reshape(rows, length), sine.reshape(rows, length)
 
 
 def split_three(values):
@@ -46,7 +46,7 @@
     return out[:, :width] + out[:, width : 2 * width] + out[:, 2 * width :]
 
 
-def lag_table(series, count):
+def lag_table(series, count, anchor):
     length = series.shape[0]
     half = length // 2
     width = 3 * count
@@ -54,23 +54,25 @@
     lower = (frame[None, :] <= frame[:, None]).astype(jnp.float32)
     positions = exact_product(lower, series)
     squares = jnp.sum((positions * positions).reshape(length, 3, count), axis=1)
-    cosine, sine = spectral_tables(length, half + 1)
+    cosine, sine = spectral_tables(length, half, anchor)
     parity = jnp.where(frame % 2 == 0, 1.0, -1.0).astype(jnp.float32)
-    both = jnp.concatenate([cosine, sine[1:]], axis=0)
+    quarter_cos = jnp.where(frame % 4 == 0, 1.0, jnp.where(frame % 4 == 2, -1.0, 0.0))
+    quarter_sin = jnp.where(frame % 4 == 1, 1.0, jnp.where(frame % 4 == 3, -1.0, 0.0))
+    extra = jnp.stack([quarter_cos, quarter_sin]).astype(jnp.float32)
+    both = jnp.concatenate([cosine, sine, extra], axis=0)
     signed = jnp.concatenate([positions, positions * parity[:, None]], axis=1)
     spectrum = jnp.dot(both, signed, precision=lax.Precision.HIGHEST)
-    real_part = spectrum[: half + 1]
-    imag_part = jnp.concatenate([jnp.zeros((1, 2 * width), jnp.float32), spectrum[half + 1 :]], axis=0)
-    power = jnp.sum((real_part * real_part + imag_part * imag_part).reshape(half + 1, 2, 3, count), axis=2)
+    real_part = spectrum[:half]
+    imag_part = spectrum[half : 2 * half]
+    power = jnp.sum((real_part * real_part + imag_part * imag_part).reshape(half, 2, 3, count), axis=2)
+    top = spectrum[2 * half :, :width]
+    middle = jnp.sum((top * top).reshape(2 * 3, count), axis=0) * (2.0 / (2 * length))
     low_q = jnp.arange(half, dtype=jnp.int32)
     weight = jnp.where(low_q == 0, 1.0, 2.0).astype(jnp.float32) / (2 * length)
-    coef = power[:half] * weight[:, None, None]
-    coef = coef.at[:, 1].set(jnp.where((low_q == 0)[:, None], power[0, 1][None, :] / (2 * length), coef[:, 1]))
+    coef = (power * weight[:, None, None]).reshape(half, 2 * count)
     sign_q = jnp.where(low_q % 2 == 0, 1.0, -1.0).astype(jnp.float32)
-    coef = coef.reshape(half, 2 * count)
     coef = jnp.concatenate([coef, coef * sign_q[:, None]], axis=1)
-    middle = power[half, 0] * (2.0 / (2 * length))
-    table = cosine[:, :half]
+    table = jnp.concatenate([cosine[:, :half], extra[:1, :half]], axis=0)
     folded = jnp.dot(table, coef, precision=lax.Precision.HIGHEST)
     lag = jnp.arange(half + 1, dtype=jnp.int32)
     sign_m = jnp.where(lag % 2 == 0, 1.0, -1.0).astype(jnp.float32)[:, None]
@@ -102,7 +104,7 @@
     outgoing = jnp.transpose(blocks, (2, 0, 1, 3)).reshape(groups, local_frames * 3 * count)
     moved = lax.all_to_all(outgoing, "frames", split_axis=0, concat_axis=0, tiled=True)
     series = moved.reshape(groups * local_frames, 3 * count)
-    return lag_table(series, count)
+    return lag_table(series, count, outgoing)
 
 
 def solution(mesh):

time: 65.1 us -> 61.2 us (0.940)
  the two profiles are of different devices: /device:TPU:2 before, /device:TPU:16 now
where the time goes in v5:
time: 61.2 us; the launch traced here: 60.8 us
  starting transfers between devices  20.8 us (34%)
  local copies, waits for them, and re-layouts  15.4 us (25%)
  matrix products  8.59 us (14%)
  waiting for transfers between devices  8.17 us (13%)
  other arithmetic  7.55 us (12%)
    all_to_all x1, starting transfers between devices, per_device(): lax.all_to_all(outgoing, 'frames', split_axis=0, concat_axis=0, tiled=True)  16.5 us
    concatenate x1, local copies, waits for them, and re-layouts, lag_table(): both = jnp.concatenate([cosine, sine, extra], axis=0)  9.33 us
    all_to_all x1, waiting for transfers between devices, per_device(): lax.all_to_all(spread, 'atoms', split_axis=0, concat_axis=0, tiled=True)  5.19 us
    dot_general x1, matrix products, lag_table(): spectrum = jnp.dot(both, signed, precision=lax.Precision.HIGHEST)  5 us
    all_to_all x1, starting transfers between devices, per_device(): lax.all_to_all(spread, 'atoms', split_axis=0, concat_axis=0, tiled=True)  4.3 us
    all_to_all x1, waiting for transfers between devices, per_device(): lax.all_to_all(outgoing, 'frames', split_axis=0, concat_axis=0, tiled=True)  2.98 us
    add x1, other arithmetic, spectral_tables(): sin_hi[:, None, :] * cos_lo[None, :, :]  2.93 us
    dot_general x2, matrix products, exact_product(): jnp.dot(matrix.astype(jnp.bfloat16), split_three(values), preferred_eleme...  2.18 us
  transfers between devices with their start and end apart: 2, of which 2 were waited for; matrix products, arithmetic and copies ran while one was open for 22% of the time, Pallas kernels for 0%

profile of v5, /device:TPU:16, one launch (start us, length us, event | category | flops | bytes accessed | tf_op | source)
XLA Modules:
  0.0 60.8 jit_solution(13882830845972017497)
XLA Ops:
  0.0 1.1 %reduce_sum.47 = f32[16,3]{0,1:T(4,128)S(1)} reduce(f32[16,3,2048]{2,0,1:T(8,128)} %param.5, f32[]{:T(128)} %constant.87.clone.1), dimensions={2}, to_apply=%region_0.0 | reduce | flops 98256 | bytes 393412 | tf_op jit(solution)/shard_map/reduce_sum | solution.py:97
  1.1 0.1 copy.47
  1.2 0.1 broadcast_in_dim.77
  1.3 0.6 broadcast_in_dim.78
  1.9 4.3 %all-to-all-start = ((f32[8,1,48]{2,1,0:T(1,128)}), f32[8,1,48]{2,1,0:T(1,128)S(1)}, u32[]{:S(2)}, u32[]{:S(2)}) async-start(f32[8,1,48]{2,1,0:T(1,128)} %broadcast_in_dim.78), calls=%async_computation | async-start | bytes 8192 | tf_op jit(solution)/shard_map/all_to_all | solution.py:99
  6.2 5.2 %all-to-all-done = f32[8,1,48]{2,1,0:T(1,128)S(1)} async-done(((f32[8,1,48]{2,1,0:T(1,128)}), f32[8,1,48]{2,1,0:T(1,128)S(1)}, u32[]{:S(2)}, u32[]{:S(2)}) %all-to-all-start) | async-done | bytes 1568 | tf_op jit(solution)/shard_map/all_to_all | solution.py:99
  11.5 0.1 copy.49
  11.6 1.1 %broadcast_subtract_fusion = f32[16,3,2048]{2,0,1:T(8,128)S(1)} fusion(f32[16,3,2048]{2,0,1:T(8,128)} %param.5, f32[16,3]{0,1:T(4,128)S(1)} %copy.49), kind=kLoop, calls=%fused_computation.42 | loop fusion | flops 98304 | bytes 786624 | tf_op jit(solution)/shard_map/sub | solution.py:101
  12.7 0.5 reshape.170
  13.2 0.5 copy.50
  13.7 1.1 %copy.51 = f32[64,1,1536]{2,1,0:T(1,128)} copy(f32[64,1,1536]{0,2,1:T(8,128)S(1)} %bitcast.20) | data formatting | bytes 786432 | tf_op jit(solution)/shard_map/all_to_all | solution.py:105
  14.7 16.5 %all-to-all-start.1 = ((f32[64,1,1536]{2,1,0:T(1,128)}), f32[64,1,1536]{2,1,0:T(1,128)S(1)}, u32[]{:S(2)}, u32[]{:S(2)}) async-start(f32[64,1,1536]{2,1,0:T(1,128)} %copy.51), calls=%async_computation.1 | async-start | bytes 786432 | tf_op jit(solution)/shard_map/all_to_all | solution.py:105
  31.2 2.9 %multiply_add_fusion = (f32[16,32,1024]{2,1,0:T(8,128)}, f32[16,32,1024]{2,1,0:T(8,128)S(1)}) fusion(f32[32,1024]{1,0:T(8,128)} %constant.103.clone, f32[16,1024]{1,0:T(8,128)} %constant.106, f32[32,1024]{1,0:T(8,128)} %constant.102.clone, f32[16,1024]{1,0:T(8,128)} %constant.105), kind=kLoop, calls=%fused_computation.7 | loop fusion | flops 3145728 | bytes 4587520 | tf_op jit(solution)/shard_map/add | solution.py:29
  34.2 0.1 slice.78
  34.3 0.6 slice.79
  34.9 0.7 %slice.87 = f32[511]{0:T(512)} slice(f32[513]{0:T(1024)S(1)} %get-tuple-element.34), slice={[1:512]} | slice | bytes 4088 | tf_op jit(solution)/shard_map/slice | solution.py:82
  35.5 9.3 %concatenate.26 = f32[1026,1024]{1,0:T(8,128)} concatenate(f32[512,1024]{1,0:T(8,128)S(1)} %bitcast.17, f32[512,1024]{1,0:T(8,128)} %bitcast.18, f32[1,1024]{1,0:T(1,128)S(1)} %get-tuple-element.30, f32[1,1024]{1,0:T(1,128)S(1)} %get-tuple-element.29), dimensions={0} | concatenate | bytes 8404992 | tf_op jit(solution)/shard_map/concatenate | solution.py:62
  44.9 3.0 %all-to-all-done.1 = f32[64,1,1536]{2,1,0:T(1,128)S(1)} async-done(((f32[64,1,1536]{2,1,0:T(1,128)}), f32[64,1,1536]{2,1,0:T(1,128)S(1)}, u32[]{:S(2)}, u32[]{:S(2)}) %all-to-all-start.1) | async-done | bytes 393248 | tf_op jit(solution)/shard_map/all_to_all | solution.py:105
  47.9 0.9 %reduce.1 = f32[64,1536]{1,0:T(8,128)S(1)} reduce(f32[64,1,1536]{2,1,0:T(1,128)S(1)} %all-to-all-done.1, f32[]{:T(128)} %constant.107), dimensions={1}, to_apply=%all_to_all.12.reduce_sub_computation | reduce | bytes 786436 | tf_op jit(solution)/shard_map/all_to_all | solution.py:105
  48.8 0.2 reshape.171
  49.0 0.1 reduce-precision_convert_fusion.1
  49.1 1.3 %fusion.1 = f32[1024,288]{0,1:T(8,128)S(1)} fusion(bf16[1024,96]{1,0:T(8,128)(2,1)S(1)} %get-tuple-element.18, bf16[1024,96]{1,0:T(8,128)(2,1)S(1)} %get-tuple-element.19, bf16[1024,96]{1,0:T(8,128)(2,1)S(1)} %get-tuple-element.17), kind=kOutput, calls=%fused_computation.6 | convolution fusion | flops 608894976 | bytes 1769472 | tf_op jit(solution)/shard_map/dot_general | solution.py:43
  50.4 0.1 broadcast_multiply_fusion
  50.5 0.8 %copy-done = f32[1026,1024]{1,0:T(8,128)S(1)} copy-done((f32[1026,1024]{1,0:T(8,128)S(1)}, f32[1026,1024]{1,0:T(8,128)}, u32[]{:S(2)}) %copy-start) | copy-done | bytes 4202520
  51.3 5.0 %fusion.12 = f32[1026,192]{0,1:T(8,128)S(1)} fusion(f32[1026,1024]{1,0:T(8,128)S(1)} %copy-done, f32[1024,96]{0,1:T(8,128)S(1)} %get-tuple-element.15, f32[1024,96]{0,1:T(8,128)S(1)} %get-tuple-element.16), kind=kOutput, calls=%fused_computation.19 | convolution fusion | flops 2420834304 | bytes 5776896 | tf_op jit(solution)/shard_map/dot_general | solution.py:64
  56.7 0.3 copy-done.2
  57.0 1.4 %fusion.3 = f32[513,128]{0,1:T(8,128)S(1)} fusion(f32[1,512]{1,0:T(1,128)S(1)} %copy-done.2, f32[512,512]{1,0:T(8,128)S(1)} %slice.78, f32[512,64]{0,1:T(8,128)S(1)} %get-tuple-element.13, f32[512,64]{0,1:T(8,128)S(1)} %get-tuple-element.14), kind=kOutput, calls=%fused_computation.10 | convolution fusion | flops 403767808 | bytes 1575424 | tf_op jit(solution)/shard_map/dot_general | solution.py:76
  58.4 0.1 fusion.31
  58.5 0.1 slice_add_fusion.4
  58.6 0.3 reverse
  59.1 0.9 %fusion = f32[1024,96]{0,1:T(8,128)S(1)} fusion(s32[1024]{0:T(1024)S(1)} %iota_subtract_fusion, bf16[1024,32]{0,1:T(8,128)(2,1)S(1)} %get-tuple-element.26, bf16[1024,32]{0,1:T(8,128)(2,1)S(1)} %get-tuple-element.27, bf16[1024,32]{0,1:T(8,128)(2,1)S(1)} %get-tuple-element.25), kind=kOutput, calls=%fused_computation.5 | convolution fusion | flops 208207872 | bytes 593920 | tf_op jit(solution)/shard_map/dot_general | solution.py:43
  60.0 0.7 %fusion.29 = f32[32,1024]{1,0:T(8,128)} fusion(f32[1024,96]{0,1:T(8,128)S(1)} %fusion, f32[511,32]{0,1:T(8,128)S(1)} %slice.127, f32[513,32]{0,1:T(8,128)S(1)} %get-tuple-element.22, f32[1024]{0:T(1024)S(1)} %subtract_convert_fusion), kind=kLoop, calls=%fused_computation.51 | loop fusion | flops 196608 | bytes 659456 | tf_op jit(solution)/shard_map/transpose | solution.py:89
  (25 shorter events, 0.6 us)
Async XLA Ops:
  1.9 9.5 %all-to-all-start = ((f32[8,1,48]{2,1,0:T(1,128)}), f32[8,1,48]{2,1,0:T(1,128)S(1)}, u32[]{:S(2)}, u32[]{:S(2)}) async-start(f32[8,1,48]{2,1,0:T(1,128)} %broadcast_in_dim.78), calls=%async_computation | async-start | bytes 8192 | tf_op jit(solution)/shard_map/all_to_all | solution.py:99
  14.7 33.1 %all-to-all-start.1 = ((f32[64,1,1536]{2,1,0:T(1,128)}), f32[64,1,1536]{2,1,0:T(1,128)S(1)}, u32[]{:S(2)}, u32[]{:S(2)}) async-start(f32[64,1,1536]{2,1,0:T(1,128)} %copy.51), calls=%async_computation.1 | async-start | bytes 786432 | tf_op jit(solution)/shard_map/all_to_all | solution.py:105
  49.1 2.2 %copy-start = (f32[1026,1024]{1,0:T(8,128)S(1)}, f32[1026,1024]{1,0:T(8,128)}, u32[]{:S(2)}) copy-start(f32[1026,1024]{1,0:T(8,128)} %concatenate.26) | copy-start | bytes 12607492
  56.3 0.7 %copy-start.2 = (f32[1,512]{1,0:T(1,128)S(1)}, f32[1,512]{1,0:T(1,128)}, u32[]{:S(2)}) copy-start(f32[1,512]{1,0:T(1,128)} %slice.79) | copy-start | bytes 6148
  56.4 2.1 %copy-start.1 = (f32[511]{0:T(512)S(1)}, f32[511]{0:T(512)}, u32[]{:S(2)}) copy-start(f32[511]{0:T(512)} %slice.87) | copy-start | bytes 6136

commit v6 on v5

--- a/solution.py
+++ b/solution.py
@@ -91,7 +91,7 @@
 
 def per_device(displacements):
     local_frames, _, atom_count = displacements.shape
-    groups = lax.axis_size("frames")
+    groups = lax.axis_size(("frames_high", "frames_low"))
     atom_total = atom_count * lax.axis_size("atoms")
     members = lax.axis_size("atoms")
     partial_sum = jnp.sum(displacements, axis=2).reshape(1, local_frames * 3)
@@ -101,18 +101,29 @@
     centred = displacements - (summed / atom_total)[:, :, None]
     count = atom_count // groups
     blocks = centred.reshape(local_frames, 3, groups, count)
-    outgoing = jnp.transpose(blocks, (2, 0, 1, 3)).reshape(groups, local_frames * 3 * count)
-    moved = lax.all_to_all(outgoing, "frames", split_axis=0, concat_axis=0, tiled=True)
+    outgoing = jnp.transpose(blocks, (2, 0, 1, 3))
+    inner = lax.axis_size("frames_low")
+    outer = groups // inner
+    row = local_frames * 3 * count
+    by_low = outgoing.reshape(outer, inner, row).transpose(1, 0, 2)
+    first = lax.all_to_all(by_low, "frames_low", split_axis=0, concat_axis=0, tiled=True)
+    by_high = first.transpose(1, 0, 2)
+    moved = lax.all_to_all(by_high, "frames_high", split_axis=0, concat_axis=0, tiled=True)
     series = moved.reshape(groups * local_frames, 3 * count)
     return lag_table(series, count, outgoing)
 
 
 def solution(mesh):
-    placed = (P("frames", None, "atoms"),)
+    frames, atoms = mesh.shape["frames"], mesh.shape["atoms"]
+    inner = 8 if frames % 8 == 0 else 1
+    split = jax.sharding.Mesh(
+        mesh.devices.reshape(frames // inner, inner, atoms), ("frames_high", "frames_low", "atoms")
+    )
+    placed = (P(("frames_high", "frames_low"), None, "atoms"),)
     return jax.shard_map(
         per_device,
-        mesh=mesh,
+        mesh=split,
         in_specs=placed,
-        out_specs=P(("atoms", "frames"), None),
+        out_specs=P(("atoms", "frames_high", "frames_low"), None),
         check_vma=False,
     )

time: 61.2 us -> 79 us (1.29)
  the two profiles are of different devices: /device:TPU:16 before, /device:TPU:8 now
where the time goes in v6:
time: 79 us; the launch traced here: 78.4 us
  local copies, waits for them, and re-layouts  20.2 us (26%)
  starting transfers between devices  17.9 us (23%)
  waiting for transfers between devices  14.1 us (18%)
  blocking collectives  9.36 us (12%)
  matrix products  8.58 us (11%)
  other arithmetic  7.97 us (10%)
    all_to_all x1, waiting for transfers between devices, per_device(): lax.all_to_all(by_low, 'frames_low', split_axis=0, concat_axis=0, tiled=T...  14.1 us
    all_to_all x1, starting transfers between devices, per_device(): lax.all_to_all(by_low, 'frames_low', split_axis=0, concat_axis=0, tiled=T...  10.3 us
    all_to_all x1, blocking collectives, per_device(): lax.all_to_all(spread, 'atoms', split_axis=0, concat_axis=0, tiled=True)  9.36 us
    concatenate x1, local copies, waits for them, and re-layouts, lag_table(): both = jnp.concatenate([cosine, sine, extra], axis=0)  9.33 us
    all_to_all x1, starting transfers between devices, per_device(): lax.all_to_all(by_high, 'frames_high', split_axis=0, concat_axis=0, tiled...  7.55 us
    dot_general x1, matrix products, lag_table(): spectrum = jnp.dot(both, signed, precision=lax.Precision.HIGHEST)  4.99 us
    transpose x1, local copies, waits for them, and re-layouts, per_device(): outgoing = jnp.transpose(blocks, (2, 0, 1, 3))  2.49 us
    dot_general x2, matrix products, exact_product(): jnp.dot(matrix.astype(jnp.bfloat16), split_three(values), preferred_eleme...  2.18 us
  transfers between devices with their start and end apart: 2, of which 1 were waited for; matrix products, arithmetic and copies ran while one was open for 19% of the time, Pallas kernels for 0%

profile of v6, /device:TPU:8, one launch (start us, length us, event | category | flops | bytes accessed | tf_op | source)
XLA Modules:
  0.0 78.4 jit_solution(15062178965638648449)
XLA Ops:
  0.0 1.1 %reduce_sum.47 = f32[16,3]{0,1:T(4,128)S(1)} reduce(f32[16,3,2048]{2,0,1:T(8,128)} %param.5, f32[]{:T(128)} %constant.87.clone.1), dimensions={2}, to_apply=%region_0.0 | reduce | flops 98256 | bytes 393412 | tf_op jit(solution)/shard_map/reduce_sum | solution.py:97
  1.2 0.1 broadcast_in_dim.77
  1.3 9.4 %all_to_all.16 = f32[8,1,48]{2,1,0:T(1,128)S(1)} all-to-all(f32[8,1,48]{2,1,0:T(1,128)S(1)} %broadcast_in_dim.78), channel_id=1, replica_groups=mesh['frames_high'=8,'frames_low'=8,'atoms'=8] {'atoms'}, dimensions={0} | all-to-all | bytes 3072 | tf_op jit(solution)/shard_map/all_to_all | solution.py:99
  10.8 1.1 %broadcast_subtract_fusion = f32[16,3,2048]{2,0,1:T(8,128)S(1)} fusion(f32[16,3,2048]{2,0,1:T(8,128)} %param.5, f32[16,3]{0,1:T(4,128)S(1)} %copy.61), kind=kLoop, calls=%fused_computation.42 | loop fusion | flops 98304 | bytes 786624 | tf_op jit(solution)/shard_map/sub | solution.py:101
  12.0 1.7 %reshape.168 = f32[16,3,64,32]{3,2,0,1:T(8,128)} reshape(f32[16,3,2048]{2,0,1:T(8,128)S(1)} %broadcast_subtract_fusion) | data formatting | bytes 786432 | tf_op jit(solution)/shard_map/reshape | solution.py:103
  13.6 2.5 %copy.62 = f32[64,16,3,32]{3,2,1,0:T(4,128)S(1)} copy(f32[64,16,3,32]{3,0,1,2:T(8,128)} %bitcast.20) | data formatting | bytes 786432 | tf_op jit(solution)/shard_map/transpose | solution.py:104
  16.1 1.3 %reshape.169 = f32[8,8,1536]{2,1,0:T(8,128)S(1)} reshape(f32[64,16,3,32]{3,2,1,0:T(4,128)S(1)} %copy.62) | data formatting | bytes 786432 | tf_op jit(solution)/shard_map/reshape | solution.py:108
  17.5 1.0 %copy.63 = f32[8,8,1536]{2,1,0:T(8,128)} copy(f32[8,8,1536]{2,0,1:T(8,128)S(1)} %bitcast.22) | data formatting | bytes 786432 | tf_op jit(solution)/shard_map/transpose | solution.py:108
  18.4 10.3 %all-to-all-start.1 = ((f32[8,8,1536]{2,1,0:T(8,128)}), f32[8,8,1536]{2,1,0:T(8,128)S(1)}, u32[]{:S(2)}, u32[]{:S(2)}) async-start(f32[8,8,1536]{2,1,0:T(8,128)} %copy.63), calls=%async_computation.1 | async-start | bytes 786432 | tf_op jit(solution)/shard_map/all_to_all | solution.py:109
  28.8 0.6 select_select_fusion
  29.4 14.1 %all-to-all-done.1 = f32[8,8,1536]{2,1,0:T(8,128)S(1)} async-done(((f32[8,8,1536]{2,1,0:T(8,128)}), f32[8,8,1536]{2,1,0:T(8,128)S(1)}, u32[]{:S(2)}, u32[]{:S(2)}) %all-to-all-start.1) | async-done | bytes 393248 | tf_op jit(solution)/shard_map/all_to_all | solution.py:109
  43.4 1.0 %copy.64 = f32[8,8,1536]{2,1,0:T(8,128)} copy(f32[8,8,1536]{2,0,1:T(8,128)S(1)} %bitcast.21) | data formatting | bytes 786432 | tf_op jit(solution)/shard_map/transpose | solution.py:110
  44.4 7.5 %all-to-all-start.2 = ((f32[8,8,1536]{2,1,0:T(8,128)}), f32[8,8,1536]{2,1,0:T(8,128)S(1)}, u32[]{:S(2)}, u32[]{:S(2)}) async-start(f32[8,8,1536]{2,1,0:T(8,128)} %copy.64), calls=%async_computation.2 | async-start | bytes 786432 | tf_op jit(solution)/shard_map/all_to_all | solution.py:111
  52.0 0.6 fusion.43
  52.6 0.6 slice.79
  53.1 0.6 slice.87
  53.8 0.6 select_multiply_fusion
  54.4 0.6 iota_subtract_fusion
  55.0 1.9 %multiply_add_fusion = (f32[16,32,1024]{2,1,0:T(8,128)}, f32[16,32,1024]{2,1,0:T(8,128)S(1)}) fusion(f32[32,1024]{1,0:T(8,128)S(1)} %copy-done.2, f32[16,1024]{1,0:T(8,128)S(1)} %copy-done.4, f32[32,1024]{1,0:T(8,128)S(1)} %copy-done.1, f32[16,1024]{1,0:T(8,128)S(1)} %copy-done.3), kind=kLoop, calls=%fused_computation.7 | loop fusion | flops 3145728 | bytes 4587520 | tf_op jit(solution)/shard_map/add | solution.py:29
  56.9 0.1 slice.78
  57.0 9.3 %concatenate.26 = f32[1026,1024]{1,0:T(8,128)} concatenate(f32[512,1024]{1,0:T(8,128)S(1)} %bitcast.18, f32[512,1024]{1,0:T(8,128)} %bitcast.19, f32[1,1024]{1,0:T(1,128)S(1)} %get-tuple-element.30, f32[1,1024]{1,0:T(1,128)S(1)} %get-tuple-element.29), dimensions={0} | concatenate | bytes 8404992 | tf_op jit(solution)/shard_map/concatenate | solution.py:62
  66.4 0.2 reshape.170
  66.5 0.1 reduce-precision_convert_fusion.1
  66.7 1.3 %fusion.1 = f32[1024,288]{0,1:T(8,128)S(1)} fusion(bf16[1024,96]{1,0:T(8,128)(2,1)S(1)} %get-tuple-element.18, bf16[1024,96]{1,0:T(8,128)(2,1)S(1)} %get-tuple-element.19, bf16[1024,96]{1,0:T(8,128)(2,1)S(1)} %get-tuple-element.17), kind=kOutput, calls=%fused_computation.6 | convolution fusion | flops 608894976 | bytes 1769472 | tf_op jit(solution)/shard_map/dot_general | solution.py:43
  68.1 0.8 %copy-done = f32[1026,1024]{1,0:T(8,128)S(1)} copy-done((f32[1026,1024]{1,0:T(8,128)S(1)}, f32[1026,1024]{1,0:T(8,128)}, u32[]{:S(2)}) %copy-start) | copy-done | bytes 4202520
  68.9 5.0 %fusion.12 = f32[1026,192]{0,1:T(8,128)S(1)} fusion(f32[1026,1024]{1,0:T(8,128)S(1)} %copy-done, f32[1024,96]{0,1:T(8,128)S(1)} %get-tuple-element.15, f32[1024,96]{0,1:T(8,128)S(1)} %get-tuple-element.16), kind=kOutput, calls=%fused_computation.19 | convolution fusion | flops 2420834304 | bytes 5776896 | tf_op jit(solution)/shard_map/dot_general | solution.py:64
  74.3 0.3 copy-done.9
  74.6 1.4 %fusion.3 = f32[513,128]{0,1:T(8,128)S(1)} fusion(f32[1,512]{1,0:T(1,128)S(1)} %copy-done.8, f32[512,512]{1,0:T(8,128)S(1)} %slice.78, f32[512,64]{0,1:T(8,128)S(1)} %get-tuple-element.13, f32[512,64]{0,1:T(8,128)S(1)} %get-tuple-element.14), kind=kOutput, calls=%fused_computation.10 | convolution fusion | flops 403767808 | bytes 1575424 | tf_op jit(solution)/shard_map/dot_general | solution.py:76
  76.1 0.1 slice_add_fusion.4
  76.3 0.3 reverse
  76.7 0.9 %fusion = f32[1024,96]{0,1:T(8,128)S(1)} fusion(s32[1024]{0:T(1024)S(1)} %copy-done.11, bf16[1024,32]{0,1:T(8,128)(2,1)S(1)} %get-tuple-element.26, bf16[1024,32]{0,1:T(8,128)(2,1)S(1)} %get-tuple-element.27, bf16[1024,32]{0,1:T(8,128)(2,1)S(1)} %get-tuple-element.25), kind=kOutput, calls=%fused_computation.5 | convolution fusion | flops 208207872 | bytes 593920 | tf_op jit(solution)/shard_map/dot_general | solution.py:43
  77.6 0.7 fusion.29
  (45 shorter events, 1.0 us)
Async XLA Ops:
  17.4 37.6 %copy-start.1 = (f32[32,1024]{1,0:T(8,128)S(1)}, f32[32,1024]{1,0:T(8,128)}, u32[]{:S(2)}) copy-start(f32[32,1024]{1,0:T(8,128)} %constant.102.clone) | copy-start | bytes 393220
  17.4 37.6 %copy-start.2 = (f32[32,1024]{1,0:T(8,128)S(1)}, f32[32,1024]{1,0:T(8,128)}, u32[]{:S(2)}) copy-start(f32[32,1024]{1,0:T(8,128)} %constant.103.clone) | copy-start | bytes 393220
  17.4 37.6 %copy-start.3 = (f32[16,1024]{1,0:T(8,128)S(1)}, f32[16,1024]{1,0:T(8,128)}, u32[]{:S(2)}) copy-start(f32[16,1024]{1,0:T(8,128)} %constant.105) | copy-start | bytes 196612
  17.4 37.6 %copy-start.4 = (f32[16,1024]{1,0:T(8,128)S(1)}, f32[16,1024]{1,0:T(8,128)}, u32[]{:S(2)}) copy-start(f32[16,1024]{1,0:T(8,128)} %constant.106) | copy-start | bytes 196612
  18.4 25.0 %all-to-all-start.1 = ((f32[8,8,1536]{2,1,0:T(8,128)}), f32[8,8,1536]{2,1,0:T(8,128)S(1)}, u32[]{:S(2)}, u32[]{:S(2)}) async-start(f32[8,8,1536]{2,1,0:T(8,128)} %copy.63), calls=%async_computation.1 | async-start | bytes 786432 | tf_op jit(solution)/shard_map/all_to_all | solution.py:109
  44.4 21.9 %all-to-all-start.2 = ((f32[8,8,1536]{2,1,0:T(8,128)}), f32[8,8,1536]{2,1,0:T(8,128)S(1)}, u32[]{:S(2)}, u32[]{:S(2)}) async-start(f32[8,8,1536]{2,1,0:T(8,128)} %copy.64), calls=%async_computation.2 | async-start | bytes 786432 | tf_op jit(solution)/shard_map/all_to_all | solution.py:111
  66.7 1.3 %copy-start.6 = (f32[1024]{0:T(1024)S(1)}, f32[1024]{0:T(1024)}, u32[]{:S(2)}) copy-start(f32[1024]{0:T(1024)} %fusion.43) | copy-start | bytes 12292
  66.7 2.2 %copy-start = (f32[1026,1024]{1,0:T(8,128)S(1)}, f32[1026,1024]{1,0:T(8,128)}, u32[]{:S(2)}) copy-start(f32[1026,1024]{1,0:T(8,128)} %concatenate.26) | copy-start | bytes 12607492
  73.9 0.7 copy-start.9
  73.9 0.7 copy-start.10
  73.9 0.7 copy-start.8
  74.0 2.0 %copy-start.5 = (f32[513]{0:T(1024)S(1)}, f32[513]{0:T(1024)}, u32[]{:S(2)}) copy-start(f32[513]{0:T(1024)} %get-tuple-element.33) | copy-start | bytes 6160
  74.0 2.1 %copy-start.7 = (f32[511]{0:T(512)S(1)}, f32[511]{0:T(512)}, u32[]{:S(2)}) copy-start(f32[511]{0:T(512)} %slice.87) | copy-start | bytes 6136
  74.1 2.6 %copy-start.11 = (s32[1024]{0:T(1024)S(1)}, s32[1024]{0:T(1024)}, u32[]{:S(2)}) copy-start(s32[1024]{0:T(1024)} %iota_subtract_fusion) | copy-start | bytes 12292

commit v7 on v5

--- a/solution.py
+++ b/solution.py
@@ -98,10 +98,10 @@
     spread = jnp.broadcast_to(partial_sum, (members, local_frames * 3))
     gathered = lax.all_to_all(spread, "atoms", split_axis=0, concat_axis=0, tiled=True)
     summed = jnp.sum(gathered, axis=0).reshape(local_frames, 3)
-    centred = displacements - (summed / atom_total)[:, :, None]
     count = atom_count // groups
-    blocks = centred.reshape(local_frames, 3, groups, count)
-    outgoing = jnp.transpose(blocks, (2, 0, 1, 3)).reshape(groups, local_frames * 3 * count)
+    blocks = jnp.transpose(displacements.reshape(local_frames, 3, groups, count), (2, 0, 1, 3))
+    outgoing = blocks - (summed / atom_total)[None, :, :, None]
+    outgoing = outgoing.reshape(groups, local_frames * 3 * count)
     moved = lax.all_to_all(outgoing, "frames", split_axis=0, concat_axis=0, tiled=True)
     series = moved.reshape(groups * local_frames, 3 * count)
     return lag_table(series, count, outgoing)

time: 61.2 us -> 59.9 us (0.979)
  waiting for transfers between devices: 8.17 us -> 6.75 us
  local copies, waits for them, and re-layouts: 15.4 us -> 16.5 us
  other arithmetic: 7.55 us -> 6.49 us
    all_to_all x1, waiting for transfers between devices: 5.19 us -> 3.68 us  [per_device(): lax.all_to_all(spread, 'atoms', split_axis=0, concat_axis=0, tiled=True)]
    reshape x1, local copies, waits for them, and re-layouts: 0.51 us -> 1.5 us  [per_device(): displacements.reshape(local_frames, 3, groups, count)]
    sub x1, other arithmetic: 1.1 us -> 0.18 us  [per_device(): outgoing = blocks - (summed / atom_total)[None, :, :, None]]
    unnamed x9 -> x13, local copies, waits for them, and re-layouts: 1.55 us -> 1.56 us
  transfers between devices with their start and end apart: 2 -> 2, of which waited for: 2 -> 2; matrix products, arithmetic and copies ran while one was open for 22% -> 25% of each run, Pallas kernels for 0% -> 0%
where the time goes in v7:
time: 59.9 us; the launch traced here: 59.3 us
  starting transfers between devices  20.8 us (35%)
  local copies, waits for them, and re-layouts  16.5 us (28%)
  matrix products  8.58 us (14%)
  waiting for transfers between devices  6.75 us (11%)
  other arithmetic  6.49 us (11%)
    all_to_all x1, starting transfers between devices, per_device(): lax.all_to_all(outgoing, 'frames', split_axis=0, concat_axis=0, tiled=True)  16.5 us
    concatenate x1, local copies, waits for them, and re-layouts, lag_table(): both = jnp.concatenate([cosine, sine, extra], axis=0)  9.35 us
    dot_general x1, matrix products, lag_table(): spectrum = jnp.dot(both, signed, precision=lax.Precision.HIGHEST)  4.99 us
    all_to_all x1, starting transfers between devices, per_device(): lax.all_to_all(spread, 'atoms', split_axis=0, concat_axis=0, tiled=True)  4.3 us
    all_to_all x1, waiting for transfers between devices, per_device(): lax.all_to_all(spread, 'atoms', split_axis=0, concat_axis=0, tiled=True)  3.68 us
    all_to_all x1, waiting for transfers between devices, per_device(): lax.all_to_all(outgoing, 'frames', split_axis=0, concat_axis=0, tiled=True)  3.07 us
    add x1, other arithmetic, spectral_tables(): sin_hi[:, None, :] * cos_lo[None, :, :]  2.79 us
    dot_general x2, matrix products, exact_product(): jnp.dot(matrix.astype(jnp.bfloat16), split_three(values), preferred_eleme...  2.18 us
  transfers between devices with their start and end apart: 2, of which 2 were waited for; matrix products, arithmetic and copies ran while one was open for 25% of the time, Pallas kernels for 0%

profile of v7, /device:TPU:16, one launch (start us, length us, event | category | flops | bytes accessed | tf_op | source)
XLA Modules:
  0.0 59.3 jit_solution(8517183683774389107)
XLA Ops:
  0.0 1.1 %reduce_sum.47 = f32[16,3]{0,1:T(4,128)S(1)} reduce(f32[16,3,2048]{2,0,1:T(8,128)} %param.5, f32[]{:T(128)} %constant.87.clone.1), dimensions={2}, to_apply=%region_0.0 | reduce | flops 98256 | bytes 393412 | tf_op jit(solution)/shard_map/reduce_sum | solution.py:97
  1.1 0.1 copy.47
  1.2 0.1 broadcast_in_dim.77
  1.3 0.6 %broadcast_in_dim.78 = f32[8,1,48]{2,1,0:T(1,128)} broadcast(f32[48]{0:T(128)S(1)} %broadcast_in_dim.77), dimensions={2} | broadcast | bytes 1728 | tf_op jit(solution)/shard_map/broadcast_in_dim | solution.py:98
  1.9 4.3 %all-to-all-start = ((f32[8,1,48]{2,1,0:T(1,128)}), f32[8,1,48]{2,1,0:T(1,128)S(1)}, u32[]{:S(2)}, u32[]{:S(2)}) async-start(f32[8,1,48]{2,1,0:T(1,128)} %broadcast_in_dim.78), calls=%async_computation | async-start | bytes 8192 | tf_op jit(solution)/shard_map/all_to_all | solution.py:99
  6.2 1.5 %reshape.170 = f32[16,3,64,32]{3,2,0,1:T(8,128)S(1)} reshape(f32[16,3,2048]{2,0,1:T(8,128)} %param.5) | data formatting | bytes 786432 | tf_op jit(solution)/shard_map/reshape | solution.py:102
  7.7 3.7 %all-to-all-done = f32[8,1,48]{2,1,0:T(1,128)S(1)} async-done(((f32[8,1,48]{2,1,0:T(1,128)}), f32[8,1,48]{2,1,0:T(1,128)S(1)}, u32[]{:S(2)}, u32[]{:S(2)}) %all-to-all-start) | async-done | bytes 1568 | tf_op jit(solution)/shard_map/all_to_all | solution.py:99
  11.5 0.1 copy.49
  11.6 0.2 subtract_bitcast_fusion
  11.8 0.5 copy.50
  12.2 1.1 %copy.51 = f32[64,1,1536]{2,1,0:T(1,128)} copy(f32[64,1,1536]{0,2,1:T(8,128)S(1)} %bitcast.20) | data formatting | bytes 786432 | tf_op jit(solution)/shard_map/all_to_all | solution.py:105
  13.3 16.5 %all-to-all-start.1 = ((f32[64,1,1536]{2,1,0:T(1,128)}), f32[64,1,1536]{2,1,0:T(1,128)S(1)}, u32[]{:S(2)}, u32[]{:S(2)}) async-start(f32[64,1,1536]{2,1,0:T(1,128)} %copy.51), calls=%async_computation.1 | async-start | bytes 786432 | tf_op jit(solution)/shard_map/all_to_all | solution.py:105
  29.8 2.8 %multiply_add_fusion = (f32[16,32,1024]{2,1,0:T(8,128)}, f32[16,32,1024]{2,1,0:T(8,128)S(1)}) fusion(f32[32,1024]{1,0:T(8,128)S(1)} %copy-done.2, f32[16,1024]{1,0:T(8,128)} %constant.106, f32[32,1024]{1,0:T(8,128)S(1)} %copy-done.1, f32[16,1024]{1,0:T(8,128)} %constant.105), kind=kLoop, calls=%fused_computation.7 | loop fusion | flops 3145728 | bytes 4587520 | tf_op jit(solution)/shard_map/add | solution.py:29
  32.6 0.1 slice.78
  32.8 0.6 slice.79
  33.3 0.7 %slice.87 = f32[511]{0:T(512)} slice(f32[513]{0:T(1024)S(1)} %get-tuple-element.34), slice={[1:512]} | slice | bytes 4088 | tf_op jit(solution)/shard_map/slice | solution.py:82
  34.0 9.3 %concatenate.26 = f32[1026,1024]{1,0:T(8,128)} concatenate(f32[512,1024]{1,0:T(8,128)S(1)} %bitcast.18, f32[512,1024]{1,0:T(8,128)} %bitcast.19, f32[1,1024]{1,0:T(1,128)S(1)} %get-tuple-element.30, f32[1,1024]{1,0:T(1,128)S(1)} %get-tuple-element.29), dimensions={0} | concatenate | bytes 8404992 | tf_op jit(solution)/shard_map/concatenate | solution.py:62
  43.4 3.1 %all-to-all-done.1 = f32[64,1,1536]{2,1,0:T(1,128)S(1)} async-done(((f32[64,1,1536]{2,1,0:T(1,128)}), f32[64,1,1536]{2,1,0:T(1,128)S(1)}, u32[]{:S(2)}, u32[]{:S(2)}) %all-to-all-start.1) | async-done | bytes 393248 | tf_op jit(solution)/shard_map/all_to_all | solution.py:105
  46.5 0.9 %reduce.1 = f32[64,1536]{1,0:T(8,128)S(1)} reduce(f32[64,1,1536]{2,1,0:T(1,128)S(1)} %all-to-all-done.1, f32[]{:T(128)} %constant.107), dimensions={1}, to_apply=%all_to_all.12.reduce_sub_computation | reduce | bytes 786436 | tf_op jit(solution)/shard_map/all_to_all | solution.py:105
  47.4 0.2 reshape.171
  47.6 0.1 reduce-precision_convert_fusion.1
  47.7 1.3 %fusion.1 = f32[1024,288]{0,1:T(8,128)S(1)} fusion(bf16[1024,96]{1,0:T(8,128)(2,1)S(1)} %get-tuple-element.18, bf16[1024,96]{1,0:T(8,128)(2,1)S(1)} %get-tuple-element.19, bf16[1024,96]{1,0:T(8,128)(2,1)S(1)} %get-tuple-element.17), kind=kOutput, calls=%fused_computation.6 | convolution fusion | flops 608894976 | bytes 1769472 | tf_op jit(solution)/shard_map/dot_general | solution.py:43
  49.0 0.1 broadcast_multiply_fusion
  49.1 0.8 %copy-done = f32[1026,1024]{1,0:T(8,128)S(1)} copy-done((f32[1026,1024]{1,0:T(8,128)S(1)}, f32[1026,1024]{1,0:T(8,128)}, u32[]{:S(2)}) %copy-start) | copy-done | bytes 4202520
  49.9 5.0 %fusion.12 = f32[1026,192]{0,1:T(8,128)S(1)} fusion(f32[1026,1024]{1,0:T(8,128)S(1)} %copy-done, f32[1024,96]{0,1:T(8,128)S(1)} %get-tuple-element.15, f32[1024,96]{0,1:T(8,128)S(1)} %get-tuple-element.16), kind=kOutput, calls=%fused_computation.20 | convolution fusion | flops 2420834304 | bytes 5776896 | tf_op jit(solution)/shard_map/dot_general | solution.py:64
  55.3 0.3 copy-done.4
  55.6 1.4 %fusion.3 = f32[513,128]{0,1:T(8,128)S(1)} fusion(f32[1,512]{1,0:T(1,128)S(1)} %copy-done.4, f32[512,512]{1,0:T(8,128)S(1)} %slice.78, f32[512,64]{0,1:T(8,128)S(1)} %get-tuple-element.13, f32[512,64]{0,1:T(8,128)S(1)} %get-tuple-element.14), kind=kOutput, calls=%fused_computation.11 | convolution fusion | flops 403767808 | bytes 1575424 | tf_op jit(solution)/shard_map/dot_general | solution.py:76
  57.0 0.1 fusion.31
  57.1 0.1 slice_add_fusion.4
  57.2 0.3 reverse
  57.7 0.9 %fusion = f32[1024,96]{0,1:T(8,128)S(1)} fusion(s32[1024]{0:T(1024)S(1)} %iota_subtract_fusion, bf16[1024,32]{0,1:T(8,128)(2,1)S(1)} %get-tuple-element.26, bf16[1024,32]{0,1:T(8,128)(2,1)S(1)} %get-tuple-element.27, bf16[1024,32]{0,1:T(8,128)(2,1)S(1)} %get-tuple-element.25), kind=kOutput, calls=%fused_computation.5 | convolution fusion | flops 208207872 | bytes 593920 | tf_op jit(solution)/shard_map/dot_general | solution.py:43
  58.6 0.7 %fusion.29 = f32[32,1024]{1,0:T(8,128)} fusion(f32[1024,96]{0,1:T(8,128)S(1)} %fusion, f32[511,32]{0,1:T(8,128)S(1)} %slice.127, f32[513,32]{0,1:T(8,128)S(1)} %get-tuple-element.22, f32[1024]{0:T(1024)S(1)} %subtract_convert_fusion), kind=kLoop, calls=%fused_computation.51 | loop fusion | flops 196608 | bytes 659456 | tf_op jit(solution)/shard_map/transpose | solution.py:89
  (29 shorter events, 0.6 us)
Async XLA Ops:
  1.9 9.5 %all-to-all-start = ((f32[8,1,48]{2,1,0:T(1,128)}), f32[8,1,48]{2,1,0:T(1,128)S(1)}, u32[]{:S(2)}, u32[]{:S(2)}) async-start(f32[8,1,48]{2,1,0:T(1,128)} %broadcast_in_dim.78), calls=%async_computation | async-start | bytes 8192 | tf_op jit(solution)/shard_map/all_to_all | solution.py:99
  11.8 18.1 %copy-start.1 = (f32[32,1024]{1,0:T(8,128)S(1)}, f32[32,1024]{1,0:T(8,128)}, u32[]{:S(2)}) copy-start(f32[32,1024]{1,0:T(8,128)} %constant.102.clone) | copy-start | bytes 393220
  11.8 18.1 %copy-start.2 = (f32[32,1024]{1,0:T(8,128)S(1)}, f32[32,1024]{1,0:T(8,128)}, u32[]{:S(2)}) copy-start(f32[32,1024]{1,0:T(8,128)} %constant.103.clone) | copy-start | bytes 393220
  13.3 33.1 %all-to-all-start.1 = ((f32[64,1,1536]{2,1,0:T(1,128)}), f32[64,1,1536]{2,1,0:T(1,128)S(1)}, u32[]{:S(2)}, u32[]{:S(2)}) async-start(f32[64,1,1536]{2,1,0:T(1,128)} %copy.51), calls=%async_computation.1 | async-start | bytes 786432 | tf_op jit(solution)/shard_map/all_to_all | solution.py:105
  47.7 2.2 %copy-start = (f32[1026,1024]{1,0:T(8,128)S(1)}, f32[1026,1024]{1,0:T(8,128)}, u32[]{:S(2)}) copy-start(f32[1026,1024]{1,0:T(8,128)} %concatenate.26) | copy-start | bytes 12607492
  54.9 0.7 %copy-start.4 = (f32[1,512]{1,0:T(1,128)S(1)}, f32[1,512]{1,0:T(1,128)}, u32[]{:S(2)}) copy-start(f32[1,512]{1,0:T(1,128)} %slice.79) | copy-start | bytes 6148
  55.0 2.1 %copy-start.3 = (f32[511]{0:T(512)S(1)}, f32[511]{0:T(512)}, u32[]{:S(2)}) copy-start(f32[511]{0:T(512)} %slice.87) | copy-start | bytes 6136

commit v8 on v7

--- a/solution.py
+++ b/solution.py
@@ -6,28 +6,34 @@
 from jax.sharding import PartitionSpec as P
 
 
-def angle_tables(length, split):
-    frame = np.arange(length, dtype=np.int64)
-    low = np.arange(split, dtype=np.int64)
-    high = np.arange(length // split, dtype=np.int64) * split
+def parity_tables(length):
+    frame = np.arange(length // 2, dtype=np.int64)
+    high = np.arange(length // 128, dtype=np.int64) * 64
+    low = np.arange(2, dtype=np.int64)[:, None] + 2 * np.arange(32, dtype=np.int64)[None, :]
     coarse = (high[:, None] * frame[None, :]) % (2 * length) * (np.pi / length)
-    fine = (low[:, None] * frame[None, :]) % (2 * length) * (np.pi / length)
+    fine = (low[:, :, None] * frame[None, None, :]) % (2 * length) * (np.pi / length)
     return [
         jnp.asarray(t.astype(np.float32))
         for t in (np.cos(coarse), np.sin(coarse), np.cos(fine), np.sin(fine))
     ]
 
 
-def spectral_tables(length, rows, anchor):
-    split = 32
-    blocks = rows // split
-    cos_hi, sin_hi, cos_lo, sin_lo = angle_tables(length, split)
+def folded_tables(length, anchor):
+    cos_hi, sin_hi, cos_lo, sin_lo = parity_tables(length)
     cos_hi, sin_hi, cos_lo, sin_lo, _ = lax.optimization_barrier(
-        (cos_hi[:blocks], sin_hi[:blocks], cos_lo, sin_lo, anchor)
+        (cos_hi, sin_hi, cos_lo, sin_lo, anchor)
     )
-    cosine = cos_hi[:, None, :] * cos_lo[None, :, :] - sin_hi[:, None, :] * sin_lo[None, :, :]
-    sine = sin_hi[:, None, :] * cos_lo[None, :, :] + cos_hi[:, None, :] * sin_lo[None, :, :]
-    return cosine.reshape(rows, length), sine.reshape(rows, length)
+    first = jnp.stack([cos_hi, sin_hi])
+    second = jnp.stack([-sin_hi, cos_hi])
+    rows = length // 2
+
+    def build(order):
+        lo_cos = cos_lo[jnp.array(order)]
+        lo_sin = sin_lo[jnp.array(order)]
+        table = first[:, :, None, :] * lo_cos[:, None, :, :] + second[:, :, None, :] * lo_sin[:, None, :, :]
+        return table.reshape(rows, rows)
+
+    return build((0, 1)), build((1, 0))
 
 
 def split_three(values):
@@ -54,25 +60,38 @@
     lower = (frame[None, :] <= frame[:, None]).astype(jnp.float32)
     positions = exact_product(lower, series)
     squares = jnp.sum((positions * positions).reshape(length, 3, count), axis=1)
-    cosine, sine = spectral_tables(length, half, anchor)
+    for_s, for_d = folded_tables(length, anchor)
     parity = jnp.where(frame % 2 == 0, 1.0, -1.0).astype(jnp.float32)
-    quarter_cos = jnp.where(frame % 4 == 0, 1.0, jnp.where(frame % 4 == 2, -1.0, 0.0))
-    quarter_sin = jnp.where(frame % 4 == 1, 1.0, jnp.where(frame % 4 == 3, -1.0, 0.0))
-    extra = jnp.stack([quarter_cos, quarter_sin]).astype(jnp.float32)
-    both = jnp.concatenate([cosine, sine, extra], axis=0)
     signed = jnp.concatenate([positions, positions * parity[:, None]], axis=1)
-    spectrum = jnp.dot(both, signed, precision=lax.Precision.HIGHEST)
-    real_part = spectrum[:half]
-    imag_part = spectrum[half : 2 * half]
+    head_part = signed[:half]
+    mirrored = jnp.concatenate([jnp.zeros((1, 2 * width), jnp.float32), jnp.flip(signed[half + 1 :], axis=0)], axis=0)
+    summed_pair = head_part + mirrored
+    differ_pair = head_part - mirrored
+    centre = signed[half]
+    out_s = jnp.dot(for_s, summed_pair, precision=lax.Precision.HIGHEST)
+    out_d = jnp.dot(for_d, differ_pair, precision=lax.Precision.HIGHEST)
+    quarter_rows = half // 2
+    q_even = 2 * jnp.arange(quarter_rows, dtype=jnp.int32)
+    centre_coef = jnp.where(q_even % 4 == 0, 1.0, -1.0).astype(jnp.float32)
+    centre_coef = jnp.concatenate([centre_coef, centre_coef])
+    out_s = out_s + centre_coef[:, None] * centre[None, :]
+    real_part = jnp.concatenate([out_s[:quarter_rows], out_d[:quarter_rows]], axis=0)
+    imag_part = jnp.concatenate([out_d[quarter_rows:], out_s[quarter_rows:]], axis=0)
     power = jnp.sum((real_part * real_part + imag_part * imag_part).reshape(half, 2, 3, count), axis=2)
-    top = spectrum[2 * half :, :width]
-    middle = jnp.sum((top * top).reshape(2 * 3, count), axis=0) * (2.0 / (2 * length))
-    low_q = jnp.arange(half, dtype=jnp.int32)
+    low_frame = jnp.arange(half, dtype=jnp.int32)
+    quarter_cos = jnp.where(low_frame % 4 == 0, 1.0, jnp.where(low_frame % 4 == 2, -1.0, 0.0)).astype(jnp.float32)
+    quarter_sin = jnp.where(low_frame % 4 == 1, 1.0, jnp.where(low_frame % 4 == 3, -1.0, 0.0)).astype(jnp.float32)
+    top_real = jnp.sum(quarter_cos[:, None] * summed_pair[:, :width], axis=0) + centre[:width]
+    top_imag = jnp.sum(quarter_sin[:, None] * differ_pair[:, :width], axis=0)
+    middle = jnp.sum((top_real * top_real + top_imag * top_imag).reshape(3, count), axis=0) * (2.0 / (2 * length))
+    low_q = jnp.concatenate([q_even, q_even + 1])
     weight = jnp.where(low_q == 0, 1.0, 2.0).astype(jnp.float32) / (2 * length)
     coef = (power * weight[:, None, None]).reshape(half, 2 * count)
     sign_q = jnp.where(low_q % 2 == 0, 1.0, -1.0).astype(jnp.float32)
     coef = jnp.concatenate([coef, coef * sign_q[:, None]], axis=1)
-    table = jnp.concatenate([cosine[:, :half], extra[:1, :half]], axis=0)
+    cos_rows = jnp.concatenate([for_s[:quarter_rows], for_d[:quarter_rows]], axis=0)
+    quarter_q = jnp.where(low_q % 4 == 0, 1.0, jnp.where(low_q % 4 == 2, -1.0, 0.0)).astype(jnp.float32)
+    table = jnp.concatenate([jnp.transpose(cos_rows), quarter_q[None, :]], axis=0)
     folded = jnp.dot(table, coef, precision=lax.Precision.HIGHEST)
     lag = jnp.arange(half + 1, dtype=jnp.int32)
     sign_m = jnp.where(lag % 2 == 0, 1.0, -1.0).astype(jnp.float32)[:, None]

time: 59.9 us -> 76.2 us (1.27)
  the two profiles are of different devices: /device:TPU:16 before, /device:TPU:2 now
where the time goes in v8:
time: 76.2 us; the launch traced here: 75.4 us
  starting transfers between devices  21.4 us (28%)
  local copies, waits for them, and re-layouts  19 us (25%)
  waiting for transfers between devices  15 us (20%)
  other arithmetic  13 us (17%)
  matrix products  6.62 us (9%)
    all_to_all x1, waiting for transfers between devices, per_device(): lax.all_to_all(outgoing, 'frames', split_axis=0, concat_axis=0, tiled=True)  15 us
    all_to_all x1, starting transfers between devices, per_device(): lax.all_to_all(outgoing, 'frames', split_axis=0, concat_axis=0, tiled=True)  12.3 us
    all_to_all x1, starting transfers between devices, per_device(): lax.all_to_all(spread, 'atoms', split_axis=0, concat_axis=0, tiled=True)  9.13 us
    unnamed x14, local copies, waits for them, and re-layouts  5.12 us
    gather x2, local copies, waits for them, and re-layouts, build(): lo_sin = sin_lo[jnp.array(order)]  2.97 us
    gather x2, local copies, waits for them, and re-layouts, build(): lo_cos = cos_lo[jnp.array(order)]  2.92 us
    sub x1, other arithmetic, per_device(): outgoing = blocks - (summed / atom_total)[None, :, :, None]  2.74 us
    dot_general x1, matrix products, lag_table(): out_s = jnp.dot(for_s, summed_pair, precision=lax.Precision.HIGHEST)  2.23 us
  transfers between devices with their start and end apart: 2, of which 1 were waited for; matrix products, arithmetic and copies ran while one was open for 19% of the time, Pallas kernels for 0%

profile of v8, /device:TPU:2, one launch (start us, length us, event | category | flops | bytes accessed | tf_op | source)
XLA Modules:
  0.0 75.4 jit_solution(797620051992118758)
XLA Ops:
  0.0 1.1 %reduce_sum.67 = f32[16,3]{0,1:T(4,128)S(1)} reduce(f32[16,3,2048]{2,0,1:T(8,128)} %param.9, f32[]{:T(128)} %constant.112.clone.1), dimensions={2}, to_apply=%region_0.0 | reduce | flops 98256 | bytes 393412 | tf_op jit(solution)/shard_map/reduce_sum | solution.py:116
  1.3 0.6 broadcast_in_dim.108
  1.9 9.1 %all-to-all-start = ((f32[8,1,48]{2,1,0:T(1,128)}), f32[8,1,48]{2,1,0:T(1,128)S(1)}, u32[]{:S(2)}, u32[]{:S(2)}) async-start(f32[8,1,48]{2,1,0:T(1,128)} %broadcast_in_dim.108), calls=%async_computation | async-start | bytes 8192 | tf_op jit(solution)/shard_map/all_to_all | solution.py:118
  11.0 1.5 %gather_fusion = f32[2,32,512]{2,1,0:T(8,128)S(1)} fusion(f32[2,32,512]{2,1,0:T(8,128)} %constant.127.clone, s32[1024]{0:T(1024)S(1)} %pad_clamp_fusion.1), kind=kCustom, calls=%fused_computation | custom fusion | bytes 262152 | tf_op jit(solution)/shard_map/gather | solution.py:31
  12.5 1.5 %gather_fusion.1 = f32[2,32,512]{2,1,0:T(8,128)S(1)} fusion(f32[2,32,512]{2,1,0:T(8,128)} %constant.128.clone, s32[1024]{0:T(1024)S(1)} %pad_clamp_fusion.1), kind=kCustom, calls=%fused_computation.1 | custom fusion | bytes 262152 | tf_op jit(solution)/shard_map/gather | solution.py:32
  14.0 0.7 pad_clamp_fusion
  14.7 1.5 %gather_fusion.2 = f32[2,32,512]{2,1,0:T(8,128)S(1)} fusion(f32[2,32,512]{2,1,0:T(8,128)} %constant.127.clone, s32[1024]{0:T(1024)S(1)} %pad_clamp_fusion), kind=kCustom, calls=%fused_computation.2 | custom fusion | bytes 262152 | tf_op jit(solution)/shard_map/gather | solution.py:31
  16.1 1.5 %gather_fusion.3 = f32[2,32,512]{2,1,0:T(8,128)S(1)} fusion(f32[2,32,512]{2,1,0:T(8,128)} %constant.128.clone, s32[1024]{0:T(1024)S(1)} %pad_clamp_fusion), kind=kCustom, calls=%fused_computation.3 | custom fusion | bytes 262152 | tf_op jit(solution)/shard_map/gather | solution.py:32
  17.7 0.7 negate_bitcast_fusion
  18.4 0.8 %pad_maximum_fusion.1 = (f32[2,8,512]{2,1,0:T(8,128)S(1)}, f32[2,8,512]{2,1,0:T(8,128)S(1)}) fusion(f32[1,8,512]{2,1,0:T(8,128)} %bitcast.46, f32[1,8,512]{2,1,0:T(8,128)} %bitcast.47, f32[1,8,512]{2,1,0:T(8,128)S(1)} %negate_bitcast_fusion), kind=kLoop, calls=%fused_computation.81 | loop fusion | flops 16384 | bytes 114688 | tf_op jit(solution)/shard_map/stack | solution.py:26
  19.2 0.3 multiply_add_fusion.1
  19.5 1.7 %reshape.280 = f32[16,3,64,32]{3,2,0,1:T(8,128)} reshape(f32[16,3,2048]{2,0,1:T(8,128)S(1)} %copy-done.3) | data formatting | bytes 786432 | tf_op jit(solution)/shard_map/reshape | solution.py:121
  21.3 0.9 %slice.121 = f32[1,8,32,512]{3,2,1,0:T(8,128)} slice(f32[2,8,32,512]{3,2,1,0:T(8,128)S(1)} %get-tuple-element.33), slice={[0:1], [0:8], [0:32], [0:512]} | slice | bytes 1048576 | tf_op jit(solution)/shard_map/slice | solution.py:92
  22.1 0.9 %copy.46 = f32[1,512]{0,1:T(8,128)} copy(f32[1,512]{1,0:T(1,128)S(1)} %compare_select_fusion.3) | data formatting | bytes 4096 | tf_op jit(solution)/shard_map/jit(_where)/select_n | solution.py:93
  23.3 2.7 %subtract_bitcast_fusion = f32[64,16,3,32]{3,0,1,2:T(8,128)} fusion(f32[16,3,64,32]{3,2,0,1:T(8,128)} %reshape.280, f32[16,3]{0,1:T(4,128)S(1)} %copy.43), kind=kLoop, calls=%fused_computation.12 | loop fusion | flops 98304 | bytes 786624 | tf_op jit(solution)/shard_map/sub | solution.py:122
  26.0 1.9 %copy.44 = f32[64,16,3,32]{0,3,2,1:T(8,128)S(1)} copy(f32[64,16,3,32]{3,0,1,2:T(8,128)} %subtract_bitcast_fusion) | data formatting | bytes 786432 | tf_op jit(solution)/shard_map/sub | solution.py:122
  27.9 1.1 %copy.45 = f32[64,1,1536]{2,1,0:T(1,128)} copy(f32[64,1,1536]{0,2,1:T(8,128)S(1)} %bitcast.36) | data formatting | bytes 786432 | tf_op jit(solution)/shard_map/all_to_all | solution.py:124
  29.0 12.3 %all-to-all-start.1 = ((f32[64,1,1536]{2,1,0:T(1,128)}), f32[64,1,1536]{2,1,0:T(1,128)S(1)}, u32[]{:S(2)}, u32[]{:S(2)}) async-start(f32[64,1,1536]{2,1,0:T(1,128)} %copy.45), calls=%async_computation.1 | async-start | bytes 786432 | tf_op jit(solution)/shard_map/all_to_all | solution.py:124
  41.3 2.1 %maximum_bitcast_fusion = f32[512,512]{0,1:T(8,128)} fusion(f32[256,512]{1,0:T(8,128)} %bitcast.38, f32[256,512]{1,0:T(8,128)S(1)} %bitcast.37), kind=kLoop, calls=%fused_computation.18 | loop fusion | flops 262144 | bytes 2097152 | tf_op jit(solution)/shard_map/transpose | solution.py:94
  43.4 15.0 %all-to-all-done.1 = f32[64,1,1536]{2,1,0:T(1,128)S(1)} async-done(((f32[64,1,1536]{2,1,0:T(1,128)}), f32[64,1,1536]{2,1,0:T(1,128)S(1)}, u32[]{:S(2)}, u32[]{:S(2)}) %all-to-all-start.1) | async-done | bytes 393248 | tf_op jit(solution)/shard_map/all_to_all | solution.py:124
  58.4 0.9 %reduce.1 = f32[64,1536]{1,0:T(8,128)S(1)} reduce(f32[64,1,1536]{2,1,0:T(1,128)S(1)} %all-to-all-done.1, f32[]{:T(128)} %constant.140), dimensions={1}, to_apply=%all_to_all.12.reduce_sub_computation | reduce | bytes 786436 | tf_op jit(solution)/shard_map/all_to_all | solution.py:124
  59.7 1.3 %fusion.1 = f32[1024,288]{0,1:T(8,128)S(1)} fusion(bf16[1024,96]{1,0:T(8,128)(2,1)S(1)} %get-tuple-element.20, bf16[1024,96]{1,0:T(8,128)(2,1)S(1)} %get-tuple-element.21, bf16[1024,96]{1,0:T(8,128)(2,1)S(1)} %get-tuple-element.19), kind=kOutput, calls=%fused_computation.10 | convolution fusion | flops 608894976 | bytes 1769472 | tf_op jit(solution)/shard_map/dot_general | solution.py:49
  61.2 0.9 %fusion.13 = f32[511,192]{0,1:T(8,128)} fusion(f32[1024,96]{0,1:T(8,128)S(1)} %get-tuple-element.16, f32[1024,96]{0,1:T(8,128)S(1)} %get-tuple-element.15), kind=kLoop, calls=%fused_computation.35 | loop fusion | flops 98112 | bytes 1178880 | tf_op jit(solution)/shard_map/concatenate | solution.py:65
  62.2 0.8 %mul.238 = f32[1024,96]{0,1:T(8,128)} multiply(f32[1024,96]{0,1:T(8,128)S(1)} %get-tuple-element.16, f32[1024,96]{0,1:T(8,128)S(1)} %get-tuple-element.16) | non-fusion elementwise | flops 98304 | bytes 1179648 | tf_op jit(solution)/shard_map/mul | solution.py:62
  63.0 3.8 %reverse = f32[512,192]{0,1:T(8,128)S(1)} reverse(f32[512,192]{0,1:T(8,128)} %bitcast.40), dimensions={0} | reverse | bytes 786432
  67.2 0.8 %copy-done.1 = f32[512,192]{0,1:T(8,128)} copy-done((f32[512,192]{0,1:T(8,128)}, f32[512,192]{0,1:T(8,128)S(1)}, u32[]{:S(2)}) %copy-start.1) | copy-done | bytes 393240
  68.4 2.2 %convolution_add_fusion = f32[512,192]{0,1:T(8,128)S(1)} fusion(f32[512,512]{1,0:T(8,128)S(1)} %bitcast.35, f32[512,192]{0,1:T(8,128)} %copy-done.1, f32[192]{0:T(256)S(1)} %fusion.31, f32[512]{0:T(512)S(1)} %pad_maximum_fusion.3), kind=kOutput, calls=%fused_computation.17 | convolution fusion | flops 604176384 | bytes 1837824 | tf_op jit(solution)/shard_map/dot_general | solution.py:71
  70.7 1.2 %fusion.67 = f32[512,192]{0,1:T(8,128)S(1)} fusion(f32[512,512]{1,0:T(8,128)S(1)} %bitcast.34, f32[512,192]{0,1:T(8,128)S(1)} %get-tuple-element.18), kind=kOutput, calls=%fused_computation.151 | convolution fusion | flops 603979776 | bytes 1835008 | tf_op jit(solution)/shard_map/dot_general | solution.py:72
  72.1 1.0 %fusion.3 = f32[513,128]{0,1:T(8,128)S(1)} fusion(f32[1,512]{0,1:T(8,128)S(1)} %copy-done.4, f32[512,512]{0,1:T(8,128)S(1)} %copy-done, f32[512,64]{0,1:T(8,128)S(1)} %get-tuple-element.13, f32[512,64]{0,1:T(8,128)S(1)} %get-tuple-element.14), kind=kOutput, calls=%fused_computation.13 | convolution fusion | flops 403767808 | bytes 1575424 | tf_op jit(solution)/shard_map/dot_general | solution.py:95
  73.2 0.3 reverse.1
  73.7 0.9 %fusion = f32[1024,96]{0,1:T(8,128)S(1)} fusion(s32[1024]{0:T(1024)S(1)} %iota_subtract_fusion, bf16[1024,32]{0,1:T(8,128)(2,1)S(1)} %get-tuple-element.30, bf16[1024,32]{0,1:T(8,128)(2,1)S(1)} %get-tuple-element.31, bf16[1024,32]{0,1:T(8,128)(2,1)S(1)} %get-tuple-element.29), kind=kOutput, calls=%fused_computation.9 | convolution fusion | flops 208207872 | bytes 593920 | tf_op jit(solution)/shard_map/dot_general | solution.py:49
  74.6 0.7 fusion.30
  (54 shorter events, 2.4 us)
Async XLA Ops:
  1.9 21.2 %all-to-all-start = ((f32[8,1,48]{2,1,0:T(1,128)}), f32[8,1,48]{2,1,0:T(1,128)S(1)}, u32[]{:S(2)}, u32[]{:S(2)}) async-start(f32[8,1,48]{2,1,0:T(1,128)} %broadcast_in_dim.108), calls=%async_computation | async-start | bytes 8192 | tf_op jit(solution)/shard_map/all_to_all | solution.py:118
  16.1 3.4 %copy-start.3 = (f32[16,3,2048]{2,0,1:T(8,128)S(1)}, f32[16,3,2048]{2,0,1:T(8,128)}, u32[]{:S(2)}) copy-start(f32[16,3,2048]{2,0,1:T(8,128)} %param.9) | copy-start | bytes 1179652
  29.0 29.5 %all-to-all-start.1 = ((f32[64,1,1536]{2,1,0:T(1,128)}), f32[64,1,1536]{2,1,0:T(1,128)S(1)}, u32[]{:S(2)}, u32[]{:S(2)}) async-start(f32[64,1,1536]{2,1,0:T(1,128)} %copy.45), calls=%async_computation.1 | async-start | bytes 786432 | tf_op jit(solution)/shard_map/all_to_all | solution.py:124
  67.2 0.8 %copy-start.1 = (f32[512,192]{0,1:T(8,128)}, f32[512,192]{0,1:T(8,128)S(1)}, u32[]{:S(2)}) copy-start(f32[512,192]{0,1:T(8,128)S(1)} %get-tuple-element.17) | copy-start | bytes 1179652
  70.6 1.4 %copy-start = (f32[512,512]{0,1:T(8,128)S(1)}, f32[512,512]{0,1:T(8,128)}, u32[]{:S(2)}) copy-start(f32[512,512]{0,1:T(8,128)} %maximum_bitcast_fusion) | copy-start | bytes 3145732
  70.6 1.4 %copy-start.4 = (f32[1,512]{0,1:T(8,128)S(1)}, f32[1,512]{0,1:T(8,128)}, u32[]{:S(2)}) copy-start(f32[1,512]{0,1:T(8,128)} %copy.46) | copy-start | bytes 6148
  72.0 1.6 %copy-start.2 = (f32[1024,96]{0,1:T(8,128)S(1)}, f32[1024,96]{0,1:T(8,128)}, u32[]{:S(2)}) copy-start(f32[1024,96]{0,1:T(8,128)} %mul.238) | copy-start | bytes 1179652

commit v9 on v8

--- a/solution.py
+++ b/solution.py
@@ -20,20 +20,19 @@
 
 def folded_tables(length, anchor):
     cos_hi, sin_hi, cos_lo, sin_lo = parity_tables(length)
-    cos_hi, sin_hi, cos_lo, sin_lo, _ = lax.optimization_barrier(
-        (cos_hi, sin_hi, cos_lo, sin_lo, anchor)
+    cos_swap, sin_swap = jnp.flip(cos_lo, axis=0), jnp.flip(sin_lo, axis=0)
+    cos_hi, sin_hi, cos_lo, sin_lo, cos_swap, sin_swap, _ = lax.optimization_barrier(
+        (cos_hi, sin_hi, cos_lo, sin_lo, cos_swap, sin_swap, anchor)
     )
     first = jnp.stack([cos_hi, sin_hi])
     second = jnp.stack([-sin_hi, cos_hi])
     rows = length // 2
 
-    def build(order):
-        lo_cos = cos_lo[jnp.array(order)]
-        lo_sin = sin_lo[jnp.array(order)]
+    def build(lo_cos, lo_sin):
         table = first[:, :, None, :] * lo_cos[:, None, :, :] + second[:, :, None, :] * lo_sin[:, None, :, :]
         return table.reshape(rows, rows)
 
-    return build((0, 1)), build((1, 0))
+    return build(cos_lo, sin_lo), build(cos_swap, sin_swap)
 
 
 def split_three(values):
@@ -58,16 +57,20 @@
     width = 3 * count
     frame = jnp.arange(length, dtype=jnp.int32)
     lower = (frame[None, :] <= frame[:, None]).astype(jnp.float32)
-    positions = exact_product(lower, series)
+    head_rows = frame[:half]
+    mirror = ((frame[None, :] <= (length - head_rows)[:, None]) & (head_rows >= 1)[:, None]).astype(jnp.float32)
+    pairs = jnp.concatenate([lower, lower[:half] + mirror, lower[:half] - mirror], axis=0)
+    combined = exact_product(pairs, series)
+    positions = combined[:length]
     squares = jnp.sum((positions * positions).reshape(length, 3, count), axis=1)
     for_s, for_d = folded_tables(length, anchor)
     parity = jnp.where(frame % 2 == 0, 1.0, -1.0).astype(jnp.float32)
-    signed = jnp.concatenate([positions, positions * parity[:, None]], axis=1)
-    head_part = signed[:half]
-    mirrored = jnp.concatenate([jnp.zeros((1, 2 * width), jnp.float32), jnp.flip(signed[half + 1 :], axis=0)], axis=0)
-    summed_pair = head_part + mirrored
-    differ_pair = head_part - mirrored
-    centre = signed[half]
+    low_parity = parity[:half, None]
+    pair_sum = combined[length : length + half]
+    pair_diff = combined[length + half :]
+    summed_pair = jnp.concatenate([pair_sum, pair_sum * low_parity], axis=1)
+    differ_pair = jnp.concatenate([pair_diff, pair_diff * low_parity], axis=1)
+    centre = jnp.concatenate([positions[half], positions[half]])
     out_s = jnp.dot(for_s, summed_pair, precision=lax.Precision.HIGHEST)
     out_d = jnp.dot(for_d, differ_pair, precision=lax.Precision.HIGHEST)
     quarter_rows = half // 2

time: 76.2 us -> 80.1 us (1.051)
  other arithmetic: 13 us -> 19.7 us
  local copies, waits for them, and re-layouts: 19 us -> 14 us
  matrix products: 6.62 us -> 10.8 us
  waiting for transfers between devices: 15 us -> 12.8 us
    gather x4 -> x0, local copies, waits for them, and re-layouts: 5.89 us -> none  [the longest x2 2.97 us: build(): lo_sin = sin_lo[jnp.array(order)]]
    another operation x2 -> x4, other arithmetic: 0.17 us -> 5.65 us
    dot_general x2, matrix products: 2.18 us -> 6.64 us  [exact_product(): jnp.dot(matrix.astype(jnp.bfloat16), split_three(values), preferred_eleme...]
    unnamed x14 -> x48, local copies, waits for them, and re-layouts: 5.12 us -> 2.43 us
    all_to_all x1, waiting for transfers between devices: 15 us -> 12.8 us  [per_device(): lax.all_to_all(outgoing, 'frames', split_axis=0, concat_axis=0, tiled=True)]
    transpose x1, other arithmetic: 2.1 us -> 0.07 us  [lag_table(): jnp.transpose(cos_rows)]
    squeeze x0 -> x1, local copies, waits for them, and re-layouts: none -> 1.31 us  [lag_table(): centre = jnp.concatenate([positions[half], positions[half]])]
    mul x1, other arithmetic: 0.09 us -> 1.22 us  [lag_table(): summed_pair = jnp.concatenate([pair_sum, pair_sum * low_parity], axis=1)]
  transfers between devices with their start and end apart: 2 -> 2, of which waited for: 1 -> 1; matrix products, arithmetic and copies ran while one was open for 19% -> 14% of each run, Pallas kernels for 0% -> 0%
where the time goes in v9:
time: 80.1 us; the launch traced here: 79.7 us
  starting transfers between devices  21.8 us (27%)
  other arithmetic  19.7 us (25%)
  local copies, waits for them, and re-layouts  14 us (17%)
  waiting for transfers between devices  12.8 us (16%)
  matrix products  10.8 us (13%)
    all_to_all x1, waiting for transfers between devices, per_device(): lax.all_to_all(outgoing, 'frames', split_axis=0, concat_axis=0, tiled=True)  12.8 us
    all_to_all x1, starting transfers between devices, per_device(): lax.all_to_all(outgoing, 'frames', split_axis=0, concat_axis=0, tiled=True)  12.8 us
    all_to_all x1, starting transfers between devices, per_device(): lax.all_to_all(spread, 'atoms', split_axis=0, concat_axis=0, tiled=True)  9.05 us
    dot_general x2, matrix products, exact_product(): jnp.dot(matrix.astype(jnp.bfloat16), split_three(values), preferred_eleme...  6.64 us
    another operation x4, other arithmetic  5.65 us
    sub x1, local copies, waits for them, and re-layouts, per_device(): outgoing = blocks - (summed / atom_total)[None, :, :, None]  2.76 us
    sub x1, other arithmetic, per_device(): outgoing = blocks - (summed / atom_total)[None, :, :, None]  2.74 us
    unnamed x48, local copies, waits for them, and re-layouts  2.43 us
  transfers between devices with their start and end apart: 2, of which 1 were waited for; matrix products, arithmetic and copies ran while one was open for 14% of the time, Pallas kernels for 0%

profile of v9, /device:TPU:2, one launch (start us, length us, event | category | flops | bytes accessed | tf_op | source)
XLA Modules:
  0.0 79.7 jit_solution(767368483873372953)
XLA Ops:
  0.0 1.2 %reduce_sum.67 = f32[16,3]{0,1:T(4,128)S(1)} reduce(f32[16,3,2048]{2,0,1:T(8,128)} %param.5, f32[]{:T(128)} %constant.108.clone.1), dimensions={2}, to_apply=%region_0.0 | reduce | flops 98256 | bytes 393412 | tf_op jit(solution)/shard_map/reduce_sum | solution.py:119
  1.4 0.6 broadcast_in_dim.99
  2.0 9.1 %all-to-all-start = ((f32[8,1,48]{2,1,0:T(1,128)}), f32[8,1,48]{2,1,0:T(1,128)S(1)}, u32[]{:S(2)}, u32[]{:S(2)}) async-start(f32[8,1,48]{2,1,0:T(1,128)} %broadcast_in_dim.99), calls=%async_computation | async-start | bytes 8192 | tf_op jit(solution)/shard_map/all_to_all | solution.py:121
  11.1 0.6 iota_subtract_fusion
  11.7 1.6 %fusion.12 = bf16[1024,1024]{1,0:T(8,128)(2,1)} fusion(), kind=kLoop, calls=%fused_computation.19 | loop fusion | flops 3145728 | bytes 2097152 | tf_op jit(solution)/shard_map/convert.6
  13.3 0.6 fusion.57
  13.8 0.6 select_select_fusion.1
  16.2 0.6 select_multiply_fusion
  17.4 1.7 %reshape.272 = f32[16,3,64,32]{3,2,0,1:T(8,128)} reshape(f32[16,3,2048]{2,0,1:T(8,128)S(1)} %copy-done.1) | data formatting | bytes 786432 | tf_op jit(solution)/shard_map/reshape | solution.py:124
  19.3 2.7 %subtract_bitcast_fusion = f32[64,16,3,32]{3,0,1,2:T(8,128)} fusion(f32[16,3,64,32]{3,2,0,1:T(8,128)} %reshape.272, f32[16,3]{0,1:T(4,128)S(1)} %copy.39), kind=kLoop, calls=%fused_computation.20 | loop fusion | flops 98304 | bytes 786624 | tf_op jit(solution)/shard_map/sub | solution.py:125
  22.0 2.8 %copy.40 = f32[64,16,3,32]{0,3,2,1:T(8,128)} copy(f32[64,16,3,32]{3,0,1,2:T(8,128)} %subtract_bitcast_fusion) | data formatting | bytes 786432 | tf_op jit(solution)/shard_map/sub | solution.py:125
  24.8 2.0 %copy.41 = f32[64,1,1536]{2,1,0:T(1,128)} copy(f32[64,1,1536]{0,2,1:T(8,128)} %bitcast.33) | data formatting | bytes 786432 | tf_op jit(solution)/shard_map/all_to_all | solution.py:127
  26.8 12.8 %all-to-all-start.1 = ((f32[64,1,1536]{2,1,0:T(1,128)}), f32[64,1,1536]{2,1,0:T(1,128)}, u32[]{:S(2)}, u32[]{:S(2)}) async-start(f32[64,1,1536]{2,1,0:T(1,128)} %copy.41), calls=%async_computation.1 | async-start | bytes 786432 | tf_op jit(solution)/shard_map/all_to_all | solution.py:127
  39.6 0.9 %copy.42 = f32[1,512]{0,1:T(8,128)} copy(f32[1,512]{1,0:T(1,128)S(1)} %compare_select_fusion.3) | data formatting | bytes 4096 | tf_op jit(solution)/shard_map/jit(_where)/select_n | solution.py:96
  40.5 0.6 slice.134
  41.7 1.9 %fusion.7 = (bf16[512,1024]{1,0:T(8,128)(2,1)}, bf16[512,1024]{1,0:T(8,128)(2,1)}) fusion(f32[1024,1024]{1,0:T(8,128)S(1)} %fusion.6, s32[512]{0:T(512)S(1)} %slice_subtract_fusion, pred[512]{0:T(512)(128)(4,1)S(1)} %copy-done.20), kind=kLoop, calls=%fused_computation.13 | loop fusion | flops 3670016 | bytes 4196864 | tf_op jit(solution)/shard_map/convert.7
  43.6 12.8 %all-to-all-done.1 = f32[64,1,1536]{2,1,0:T(1,128)} async-done(((f32[64,1,1536]{2,1,0:T(1,128)}), f32[64,1,1536]{2,1,0:T(1,128)}, u32[]{:S(2)}, u32[]{:S(2)}) %all-to-all-start.1) | async-done | bytes 393248 | tf_op jit(solution)/shard_map/all_to_all | solution.py:127
  56.4 1.9 %reduce.1 = f32[64,1536]{1,0:T(8,128)S(1)} reduce(f32[64,1,1536]{2,1,0:T(1,128)} %all-to-all-done.1, f32[]{:T(128)} %constant.126), dimensions={1}, to_apply=%all_to_all.12.reduce_sub_computation | reduce | bytes 786436 | tf_op jit(solution)/shard_map/all_to_all | solution.py:127
  58.4 1.0 %reshape.273 = f32[1024,96]{1,0:T(8,128)} reshape(f32[64,1536]{1,0:T(8,128)S(1)} %reduce.1) | data formatting | bytes 786432 | tf_op jit(solution)/shard_map/reshape | solution.py:128
  59.4 1.2 %reduce-precision_convert_fusion.1 = (bf16[1024,96]{1,0:T(8,128)(2,1)S(1)}, bf16[1024,96]{1,0:T(8,128)(2,1)S(1)}, bf16[1024,96]{1,0:T(8,128)(2,1)S(1)}) fusion(f32[1024,96]{1,0:T(8,128)} %reshape.273), kind=kLoop, calls=%fused_computation.39 | loop fusion | flops 688128 | bytes 983040 | tf_op jit(solution)/shard_map/convert.3
  60.5 5.7 %fusion = f32[2048,288]{0,1:T(8,128)S(1)} fusion(bf16[512,1024]{1,0:T(8,128)(2,1)} %get-tuple-element.22, bf16[512,1024]{1,0:T(8,128)(2,1)} %get-tuple-element.21, bf16[1024,1024]{1,0:T(8,128)(2,1)} %fusion.12, bf16[1024,96]{1,0:T(8,128)(2,1)S(1)} %get-tuple-element.31, bf16[1024,96]{1,0:T(8,128)(2,1)S(1)} %get-tuple-element.32, ...), kind=kOutput, calls=%fused_computation.2 | convolution fusion | flops 1222311936 | bytes 7143424 | tf_op jit(solution)/shard_map/dot_general | solution.py:48
  66.5 0.8 %copy-done = f32[2048,96]{0,1:T(8,128)} copy-done((f32[2048,96]{0,1:T(8,128)}, f32[2048,96]{0,1:T(8,128)S(1)}, u32[]{:S(2)}) %copy-start) | copy-done | bytes 786456
  67.9 0.6 pad_maximum_fusion.3
  68.6 1.3 %squeeze.7 = f32[3,32]{1,0:T(4,128)} reshape(f32[96]{0:T(128)} %copy-done.21) | data formatting | bytes 768 | tf_op jit(solution)/shard_map/squeeze | solution.py:73
  69.9 0.7 reduce_sum.69
  70.6 0.9 %reduce-precision_convert_fusion.3 = (bf16[1024,32]{0,1:T(8,128)(2,1)S(1)}, bf16[1024,32]{0,1:T(8,128)(2,1)S(1)}, bf16[1024,32]{0,1:T(8,128)(2,1)S(1)}) fusion(f32[1024,32]{0,1:T(8,128)} %reduce_sum.69), kind=kLoop, calls=%fused_computation.66 | loop fusion | flops 229376 | bytes 327680 | tf_op jit(solution)/shard_map/convert
  71.5 1.2 %broadcast_multiply_fusion.1 = (f32[512,96]{0,1:T(8,128)S(1)}, f32[512,96]{0,1:T(8,128)S(1)}, f32[512,96]{0,1:T(8,128)S(1)}, f32[96]{0:T(128)S(1)}, f32[96]{0:T(128)S(1)}, /*index=5*/f32[512,96]{0,1:T(8,128)S(1)}) fusion(f32[512]{0:T(512)S(1)} %slice-done, f32[2048,96]{0,1:T(8,128)} %copy-done, f32[512]{0:T(512)} %get-tuple-element.50, f32[512]{0:T(512)} %get-tuple-element.51), kind=kLoop, calls=%fused_computation.76 | loop fusion | flops 294720 | bytes 1186560 | tf_op jit(solution)/shard_map/mul | solution.py:71
  72.8 1.2 %fusion.26 = f32[512,192]{0,1:T(8,128)S(1)} fusion(f32[512,512]{1,0:T(8,128)S(1)} %bitcast.31, f32[512,96]{0,1:T(8,128)S(1)} %get-tuple-element.24, f32[512,96]{0,1:T(8,128)S(1)} %get-tuple-element.29), kind=kOutput, calls=%fused_computation.45 | convolution fusion | flops 604078080 | bytes 1835008 | tf_op jit(solution)/shard_map/dot_general | solution.py:75
  74.1 1.9 %convolution_add_fusion = f32[512,192]{0,1:T(8,128)S(1)} fusion(f32[512,512]{1,0:T(8,128)S(1)} %bitcast.32, f32[512,96]{0,1:T(8,128)S(1)} %get-tuple-element.23, f32[512,96]{0,1:T(8,128)S(1)} %get-tuple-element.26, f32[192]{0:T(256)S(1)} %copy-done.22, f32[512]{0:T(512)} %pad_maximum_fusion.2), kind=kOutput, calls=%fused_computation.25 | convolution fusion | flops 604274688 | bytes 1837824 | tf_op jit(solution)/shard_map/dot_general | solution.py:74
  76.4 1.0 %fusion.13 = f32[513,128]{0,1:T(8,128)S(1)} fusion(f32[1,512]{0,1:T(8,128)S(1)} %copy-done.2, f32[512,512]{0,1:T(8,128)S(1)} %maximum_bitcast_fusion, f32[512,64]{0,1:T(8,128)S(1)} %get-tuple-element.19, f32[512,64]{0,1:T(8,128)S(1)} %get-tuple-element.20), kind=kOutput, calls=%fused_computation.21 | convolution fusion | flops 403767808 | bytes 1575424 | tf_op jit(solution)/shard_map/dot_general | solution.py:98
  78.0 0.9 %fusion.9 = f32[1024,96]{0,1:T(8,128)S(1)} fusion(s32[1024]{0:T(1024)S(1)} %copy-done.19, bf16[1024,32]{0,1:T(8,128)(2,1)S(1)} %get-tuple-element.41, bf16[1024,32]{0,1:T(8,128)(2,1)S(1)} %get-tuple-element.42, bf16[1024,32]{0,1:T(8,128)(2,1)S(1)} %get-tuple-element.40), kind=kOutput, calls=%fused_computation.15 | convolution fusion | flops 208207872 | bytes 593920 | tf_op jit(solution)/shard_map/dot_general | solution.py:48
  78.9 0.7 fusion.43
  (86 shorter events, 4.9 us)
Async XLA Ops:
  0.0 15.6 %copy-start.7 = (f32[8,512]{1,0:T(8,128)S(1)}, f32[8,512]{1,0:T(8,128)}, u32[]{:S(2)}) copy-start(f32[8,512]{1,0:T(8,128)} %constant.120.clone) | copy-start | bytes 49156
  0.0 15.6 %copy-start.8 = (f32[8,512]{1,0:T(8,128)S(1)}, f32[8,512]{1,0:T(8,128)}, u32[]{:S(2)}) copy-start(f32[8,512]{1,0:T(8,128)} %constant.119.clone) | copy-start | bytes 49156
  0.0 15.6 %copy-start.3 = (f32[2,32,512]{2,1,0:T(8,128)S(1)}, f32[2,32,512]{2,1,0:T(8,128)}, u32[]{:S(2)}) copy-start(f32[2,32,512]{2,1,0:T(8,128)} %constant.121.clone) | copy-start | bytes 393220
  0.0 15.6 %copy-start.4 = (f32[2,32,512]{2,1,0:T(8,128)S(1)}, f32[2,32,512]{2,1,0:T(8,128)}, u32[]{:S(2)}) copy-start(f32[2,32,512]{2,1,0:T(8,128)} %constant.122.clone) | copy-start | bytes 393220
  0.0 15.6 %copy-start.5 = (f32[2,32,512]{2,1,0:T(8,128)S(1)}, f32[2,32,512]{2,1,0:T(8,128)}, u32[]{:S(2)}) copy-start(f32[2,32,512]{2,1,0:T(8,128)} %constant.124) | copy-start | bytes 393220
  0.0 15.6 %copy-start.6 = (f32[2,32,512]{2,1,0:T(8,128)S(1)}, f32[2,32,512]{2,1,0:T(8,128)}, u32[]{:S(2)}) copy-start(f32[2,32,512]{2,1,0:T(8,128)} %constant.125) | copy-start | bytes 393220
  2.0 17.1 %all-to-all-start = ((f32[8,1,48]{2,1,0:T(1,128)}), f32[8,1,48]{2,1,0:T(1,128)S(1)}, u32[]{:S(2)}, u32[]{:S(2)}) async-start(f32[8,1,48]{2,1,0:T(1,128)} %broadcast_in_dim.99), calls=%async_computation | async-start | bytes 8192 | tf_op jit(solution)/shard_map/all_to_all | solution.py:121
  13.3 2.9 %copy-start.11 = (s32[256]{0:T(256)}, s32[256]{0:T(256)S(1)}, u32[]{:S(2)}) copy-start(s32[256]{0:T(256)S(1)} %get-tuple-element.52) | copy-start | bytes 3076
  13.3 2.9 %copy-start.13 = (s32[256]{0:T(256)}, s32[256]{0:T(256)S(1)}, u32[]{:S(2)}) copy-start(s32[256]{0:T(256)S(1)} %get-tuple-element.53) | copy-start | bytes 3076
  14.5 0.6 copy-start.9
  16.0 1.4 %copy-start.1 = (f32[16,3,2048]{2,0,1:T(8,128)S(1)}, f32[16,3,2048]{2,0,1:T(8,128)}, u32[]{:S(2)}) copy-start(f32[16,3,2048]{2,0,1:T(8,128)} %param.5) | copy-start | bytes 1179652
  22.0 17.6 %copy-start.12 = (s32[256]{0:T(256)S(1)}, s32[256]{0:T(256)}, u32[]{:S(2)}) copy-start(s32[256]{0:T(256)} %copy-done.11) | copy-start | bytes 3076
  22.0 17.6 %copy-start.14 = (s32[256]{0:T(256)S(1)}, s32[256]{0:T(256)}, u32[]{:S(2)}) copy-start(s32[256]{0:T(256)} %copy-done.13) | copy-start | bytes 3076
  26.8 29.7 %all-to-all-start.1 = ((f32[64,1,1536]{2,1,0:T(1,128)}), f32[64,1,1536]{2,1,0:T(1,128)}, u32[]{:S(2)}, u32[]{:S(2)}) async-start(f32[64,1,1536]{2,1,0:T(1,128)} %copy.41), calls=%async_computation.1 | async-start | bytes 786432 | tf_op jit(solution)/shard_map/all_to_all | solution.py:127
  39.6 2.1 %copy-start.10 = (s32[1024]{0:T(1024)S(1)}, s32[1024]{0:T(1024)}, u32[]{:S(2)}) copy-start(s32[1024]{0:T(1024)} %copy-done.9) | copy-start | bytes 12292
  39.6 2.1 %copy-start.20 = (pred[512]{0:T(512)(128)(4,1)S(1)}, pred[512]{0:T(512)(128)(4,1)}, u32[]{:S(2)}) copy-start(pred[512]{0:T(512)(128)(4,1)} %slice_compare_fusion) | copy-start | bytes 1540
  66.3 5.2 %slice-start = ((f32[1024]{0:T(1024)}), f32[512]{0:T(512)S(1)}, s32[]{:S(2)}) async-start(f32[1024]{0:T(1024)} %fusion.57), calls=%async_computation.2 | async-start | bytes 4096 | tf_op jit(solution)/shard_map/slice | solution.py:68
  66.4 0.9 %copy-start = (f32[2048,96]{0,1:T(8,128)}, f32[2048,96]{0,1:T(8,128)S(1)}, u32[]{:S(2)}) copy-start(f32[2048,96]{0,1:T(8,128)S(1)} %slice_add_fusion) | copy-start | bytes 2359300
  67.4 0.5 copy-start.21
  70.6 3.5 %copy-start.22 = (f32[192]{0:T(256)S(1)}, f32[192]{0:T(256)}, u32[]{:S(2)}) copy-start(f32[192]{0:T(256)} %pad_maximum_fusion.3) | copy-start | bytes 2308
  72.7 3.5 %copy-start.18 = (f32[3,32]{1,0:T(4,128)S(1)}, f32[3,32]{1,0:T(4,128)}, u32[]{:S(2)}) copy-start(f32[3,32]{1,0:T(4,128)} %squeeze.7) | copy-start | bytes 1156
  74.0 2.4 %copy-start.15 = (f32[512]{0:T(512)S(1)}, f32[512]{0:T(512)}, u32[]{:S(2)}) copy-start(f32[512]{0:T(512)} %get-tuple-element.48) | copy-start | bytes 6148
  74.0 2.4 %copy-start.16 = (f32[512]{0:T(512)S(1)}, f32[512]{0:T(512)}, u32[]{:S(2)}) copy-start(f32[512]{0:T(512)} %get-tuple-element.49) | copy-start | bytes 6148
  74.0 2.4 %copy-start.2 = (f32[1,512]{0,1:T(8,128)S(1)}, f32[1,512]{0,1:T(8,128)}, u32[]{:S(2)}) copy-start(f32[1,512]{0,1:T(8,128)} %copy.42) | copy-start | bytes 6148
  76.0 1.5 %copy-start.17 = (f32[511]{0:T(512)S(1)}, f32[511]{0:T(512)}, u32[]{:S(2)}) copy-start(f32[511]{0:T(512)} %slice.134) | copy-start | bytes 6136
  76.1 1.9 %copy-start.19 = (s32[1024]{0:T(1024)S(1)}, s32[1024]{0:T(1024)}, u32[]{:S(2)}) copy-start(s32[1024]{0:T(1024)} %iota_subtract_fusion) | copy-start | bytes 12292

commit v10 on v7

--- a/solution.py
+++ b/solution.py
@@ -101,10 +101,17 @@
     count = atom_count // groups
     blocks = jnp.transpose(displacements.reshape(local_frames, 3, groups, count), (2, 0, 1, 3))
     outgoing = blocks - (summed / atom_total)[None, :, :, None]
-    outgoing = outgoing.reshape(groups, local_frames * 3 * count)
-    moved = lax.all_to_all(outgoing, "frames", split_axis=0, concat_axis=0, tiled=True)
-    series = moved.reshape(groups * local_frames, 3 * count)
-    return lag_table(series, count, outgoing)
+    half_count = count // 2
+    results = []
+    for part in range(2):
+        piece = outgoing[..., part * half_count : (part + 1) * half_count]
+        piece = piece.reshape(groups, local_frames * 3 * half_count)
+        moved = lax.all_to_all(piece, "frames", split_axis=0, concat_axis=0, tiled=True)
+        if results:
+            moved, _ = lax.optimization_barrier((moved, results[-1]))
+        series = moved.reshape(groups * local_frames, 3 * half_count)
+        results.append(lag_table(series, half_count, outgoing))
+    return jnp.concatenate(results, axis=0)
 
 
 def solution(mesh):

time: 59.9 us -> 82.5 us (1.38)
  the two profiles are of different devices: /device:TPU:16 before, /device:TPU:2 now
where the time goes in v10:
time: 82.5 us; the launch traced here: 82 us
  starting transfers between devices  33.1 us (40%)
  local copies, waits for them, and re-layouts  21.1 us (26%)
  matrix products  16.1 us (20%)
  waiting for transfers between devices  5.82 us (7%)
  other arithmetic  5.37 us (7%)
    all_to_all x2, starting transfers between devices, per_device(): lax.all_to_all(piece, 'frames', split_axis=0, concat_axis=0, tiled=True)  24 us
    dot_general x2, matrix products, lag_table(): spectrum = jnp.dot(both, signed, precision=lax.Precision.HIGHEST)  10.7 us
    concatenate x1, local copies, waits for them, and re-layouts, lag_table(): both = jnp.concatenate([cosine, sine, extra], axis=0)  9.34 us
    all_to_all x1, starting transfers between devices, per_device(): lax.all_to_all(spread, 'atoms', split_axis=0, concat_axis=0, tiled=True)  9.13 us
    slice x3, local copies, waits for them, and re-layouts, per_device(): piece = outgoing[..., part * half_count:(part + 1) * half_count]  4.03 us
    all_to_all x2, waiting for transfers between devices, per_device(): lax.all_to_all(piece, 'frames', split_axis=0, concat_axis=0, tiled=True)  3.64 us
    dot_general x4, matrix products, exact_product(): jnp.dot(matrix.astype(jnp.bfloat16), split_three(values), preferred_eleme...  3.07 us
    unnamed x17, local copies, waits for them, and re-layouts  2.45 us
  transfers between devices with their start and end apart: 3, of which 3 were waited for; matrix products, arithmetic and copies ran while one was open for 28% of the time, Pallas kernels for 0%

profile of v10, /device:TPU:2, one launch (start us, length us, event | category | flops | bytes accessed | tf_op | source)
XLA Modules:
  0.0 82.0 jit_solution(17770175773011717397)
XLA Ops:
  0.0 1.1 %reduce_sum.76 = f32[16,3]{0,1:T(4,128)S(1)} reduce(f32[16,3,2048]{2,0,1:T(8,128)} %param.9, f32[]{:T(128)} %constant.114.clone.1), dimensions={2}, to_apply=%region_0.0 | reduce | flops 98256 | bytes 393412 | tf_op jit(solution)/shard_map/reduce_sum | solution.py:97
  1.3 0.6 broadcast_in_dim.117
  1.9 9.1 %all-to-all-start = ((f32[8,1,48]{2,1,0:T(1,128)}), f32[8,1,48]{2,1,0:T(1,128)S(1)}, u32[]{:S(2)}, u32[]{:S(2)}) async-start(f32[8,1,48]{2,1,0:T(1,128)} %broadcast_in_dim.117), calls=%async_computation | async-start | bytes 8192 | tf_op jit(solution)/shard_map/all_to_all | solution.py:99
  11.1 1.5 %reshape.211 = f32[16,3,64,32]{3,2,0,1:T(8,128)S(1)} reshape(f32[16,3,2048]{2,0,1:T(8,128)} %param.9) | data formatting | bytes 786432 | tf_op jit(solution)/shard_map/reshape | solution.py:102
  12.6 2.2 %all-to-all-done = f32[8,1,48]{2,1,0:T(1,128)S(1)} async-done(((f32[8,1,48]{2,1,0:T(1,128)}), f32[8,1,48]{2,1,0:T(1,128)S(1)}, u32[]{:S(2)}, u32[]{:S(2)}) %all-to-all-start) | async-done | bytes 1568 | tf_op jit(solution)/shard_map/all_to_all | solution.py:99
  15.0 0.2 subtract_bitcast_fusion
  15.2 1.7 %fusion.86 = (f32[64,16,3,16]{3,0,1,2:T(8,128)}, f32[64,16,3,16]{3,0,1,2:T(8,128)S(1)}) fusion(f32[64,16,3,32]{3,0,1,2:T(8,128)S(1)} %subtract_bitcast_fusion), kind=kLoop, calls=%fused_computation.166 | loop fusion | bytes 786432 | tf_op jit(solution)/shard_map/slice | solution.py:107
  16.9 1.9 %copy.48 = f32[64,16,3,16]{0,3,2,1:T(8,128)S(1)} copy(f32[64,16,3,16]{3,0,1,2:T(8,128)} %get-tuple-element.31) | data formatting | bytes 393216 | tf_op jit(solution)/shard_map/slice | solution.py:107
  18.8 0.8 %copy.49 = f32[64,1,768]{2,1,0:T(1,128)} copy(f32[64,1,768]{0,2,1:T(8,128)S(1)} %bitcast.33) | data formatting | bytes 393216 | tf_op jit(solution)/shard_map/all_to_all | solution.py:109
  19.6 12.3 %all-to-all-start.1 = ((f32[64,1,768]{2,1,0:T(1,128)}), f32[64,1,768]{2,1,0:T(1,128)S(1)}, u32[]{:S(2)}, u32[]{:S(2)}) async-start(f32[64,1,768]{2,1,0:T(1,128)} %copy.49), calls=%async_computation.1 | async-start | bytes 393216 | tf_op jit(solution)/shard_map/all_to_all | solution.py:109
  32.0 0.4 copy.53
  32.4 0.8 %copy.54 = f32[64,1,768]{2,1,0:T(1,128)} copy(f32[64,1,768]{0,2,1:T(8,128)S(1)} %bitcast.34) | data formatting | bytes 393216 | tf_op jit(solution)/shard_map/all_to_all | solution.py:109
  33.3 1.9 %multiply_add_fusion = (f32[16,32,1024]{2,1,0:T(8,128)}, f32[16,32,1024]{2,1,0:T(8,128)S(1)}) fusion(f32[32,1024]{1,0:T(8,128)S(1)} %copy-done.2, f32[16,1024]{1,0:T(8,128)S(1)} %copy-done.4, f32[32,1024]{1,0:T(8,128)S(1)} %copy-done.1, f32[16,1024]{1,0:T(8,128)S(1)} %copy-done.3), kind=kLoop, calls=%fused_computation.9 | loop fusion | flops 3145728 | bytes 4587520 | tf_op jit(solution)/shard_map/add | solution.py:29
  35.3 9.3 %concatenate.52 = f32[1026,1024]{1,0:T(8,128)} concatenate(f32[512,1024]{1,0:T(8,128)S(1)} %bitcast.31, f32[512,1024]{1,0:T(8,128)} %bitcast.32, f32[1,1024]{1,0:T(1,128)S(1)} %get-tuple-element.56, f32[1,1024]{1,0:T(1,128)S(1)} %get-tuple-element.55), dimensions={0} | concatenate | bytes 8404992 | tf_op jit(solution)/shard_map/concatenate | solution.py:62
  44.6 1.0 %all-to-all-done.1 = f32[64,1,768]{2,1,0:T(1,128)S(1)} async-done(((f32[64,1,768]{2,1,0:T(1,128)}), f32[64,1,768]{2,1,0:T(1,128)S(1)}, u32[]{:S(2)}, u32[]{:S(2)}) %all-to-all-start.1) | async-done | bytes 196640 | tf_op jit(solution)/shard_map/all_to_all | solution.py:109
  45.6 11.7 %all-to-all-start.2 = ((f32[64,1,768]{2,1,0:T(1,128)}), f32[64,1,768]{2,1,0:T(1,128)S(1)}, u32[]{:S(2)}, u32[]{:S(2)}) async-start(f32[64,1,768]{2,1,0:T(1,128)} %copy.54), calls=%async_computation.2 | async-start | bytes 393216 | tf_op jit(solution)/shard_map/all_to_all | solution.py:109
  57.3 0.5 reduce.1
  57.8 0.3 reshape.212
  58.3 0.7 fusion.1
  59.1 1.4 %copy-done = f32[1026,1024]{1,0:T(8,128)S(1)} copy-done((f32[1026,1024]{1,0:T(8,128)S(1)}, f32[1026,1024]{1,0:T(8,128)}, u32[]{:S(2)}) %copy-start) | copy-done | bytes 4202520
  60.5 4.2 %fusion.8 = f32[1026,96]{0,1:T(8,128)S(1)} fusion(f32[1026,1024]{1,0:T(8,128)S(1)} %copy-done, f32[1024,48]{0,1:T(8,128)S(1)} %get-tuple-element.29, f32[1024,48]{0,1:T(8,128)S(1)} %get-tuple-element.30), kind=kOutput, calls=%fused_computation.17 | convolution fusion | flops 1210417152 | bytes 4989696 | tf_op jit(solution)/shard_map/dot_general | solution.py:64
  65.1 1.2 %fusion.7 = f32[513,64]{0,1:T(8,128)S(1)} fusion(f32[1,512]{1,0:T(1,128)S(1)} %slice.159, f32[512,512]{1,0:T(8,128)S(1)} %slice.158, f32[512,32]{0,1:T(8,128)S(1)} %get-tuple-element.27, f32[512,32]{0,1:T(8,128)S(1)} %get-tuple-element.28), kind=kOutput, calls=%fused_computation.16 | convolution fusion | flops 202015232 | bytes 1313024 | tf_op jit(solution)/shard_map/dot_general | solution.py:76
  66.5 0.4 reverse
  66.9 0.9 %fusion.3 = f32[1024,48]{0,1:T(8,128)S(1)} fusion(s32[1024]{0:T(1024)S(1)} %iota_subtract_fusion, bf16[1024,16]{0,1:T(8,128)(2,1)S(1)} %get-tuple-element.51, bf16[1024,16]{0,1:T(8,128)(2,1)S(1)} %get-tuple-element.52, bf16[1024,16]{0,1:T(8,128)(2,1)S(1)} %get-tuple-element.50), kind=kOutput, calls=%fused_computation.8 | convolution fusion | flops 107249664 | bytes 299008 | tf_op jit(solution)/shard_map/dot_general | solution.py:43
  67.9 2.7 %all-to-all-done.2 = f32[64,1,768]{2,1,0:T(1,128)S(1)} async-done(((f32[64,1,768]{2,1,0:T(1,128)}), f32[64,1,768]{2,1,0:T(1,128)S(1)}, u32[]{:S(2)}, u32[]{:S(2)}) %all-to-all-start.2) | async-done | bytes 196640 | tf_op jit(solution)/shard_map/all_to_all | solution.py:109
  70.6 0.3 reshape.216
  71.1 0.7 fusion
  71.8 6.4 %fusion.12 = f32[1026,96]{0,1:T(8,128)S(1)} fusion(f32[1026,1024]{1,0:T(8,128)} %concatenate.52, f32[1024,48]{0,1:T(8,128)S(1)} %get-tuple-element.25, f32[1024,48]{0,1:T(8,128)S(1)} %get-tuple-element.26), kind=kOutput, calls=%fused_computation.21 | convolution fusion | flops 1210417152 | bytes 4989696 | tf_op jit(solution)/shard_map/dot_general | solution.py:64
  78.6 1.2 %fusion.6 = f32[513,64]{0,1:T(8,128)S(1)} fusion(f32[1,512]{1,0:T(1,128)S(1)} %slice.159, f32[512,512]{1,0:T(8,128)S(1)} %slice.158, f32[512,32]{0,1:T(8,128)S(1)} %get-tuple-element.23, f32[512,32]{0,1:T(8,128)S(1)} %get-tuple-element.24), kind=kOutput, calls=%fused_computation.15 | convolution fusion | flops 202015232 | bytes 1313024 | tf_op jit(solution)/shard_map/dot_general | solution.py:76
  80.0 0.3 reverse.1
  80.3 0.9 %fusion.2 = f32[1024,48]{0,1:T(8,128)S(1)} fusion(s32[1024]{0:T(1024)S(1)} %iota_subtract_fusion, bf16[1024,16]{0,1:T(8,128)(2,1)S(1)} %get-tuple-element.48, bf16[1024,16]{0,1:T(8,128)(2,1)S(1)} %get-tuple-element.49, bf16[1024,16]{0,1:T(8,128)(2,1)S(1)} %get-tuple-element.47), kind=kOutput, calls=%fused_computation.7 | convolution fusion | flops 107249664 | bytes 299008 | tf_op jit(solution)/shard_map/dot_general | solution.py:43
  81.3 0.7 pad_maximum_fusion.3
  (61 shorter events, 2.4 us)
Async XLA Ops:
  1.9 12.9 %all-to-all-start = ((f32[8,1,48]{2,1,0:T(1,128)}), f32[8,1,48]{2,1,0:T(1,128)S(1)}, u32[]{:S(2)}, u32[]{:S(2)}) async-start(f32[8,1,48]{2,1,0:T(1,128)} %broadcast_in_dim.117), calls=%async_computation | async-start | bytes 8192 | tf_op jit(solution)/shard_map/all_to_all | solution.py:99
  18.7 14.5 %copy-start.1 = (f32[32,1024]{1,0:T(8,128)S(1)}, f32[32,1024]{1,0:T(8,128)}, u32[]{:S(2)}) copy-start(f32[32,1024]{1,0:T(8,128)} %constant.129.clone) | copy-start | bytes 393220
  18.7 14.5 %copy-start.2 = (f32[32,1024]{1,0:T(8,128)S(1)}, f32[32,1024]{1,0:T(8,128)}, u32[]{:S(2)}) copy-start(f32[32,1024]{1,0:T(8,128)} %constant.130.clone) | copy-start | bytes 393220
  18.7 14.5 %copy-start.3 = (f32[16,1024]{1,0:T(8,128)S(1)}, f32[16,1024]{1,0:T(8,128)}, u32[]{:S(2)}) copy-start(f32[16,1024]{1,0:T(8,128)} %constant.132) | copy-start | bytes 196612
  18.8 14.5 %copy-start.4 = (f32[16,1024]{1,0:T(8,128)S(1)}, f32[16,1024]{1,0:T(8,128)}, u32[]{:S(2)}) copy-start(f32[16,1024]{1,0:T(8,128)} %constant.133) | copy-start | bytes 196612
  19.6 26.0 %all-to-all-start.1 = ((f32[64,1,768]{2,1,0:T(1,128)}), f32[64,1,768]{2,1,0:T(1,128)S(1)}, u32[]{:S(2)}, u32[]{:S(2)}) async-start(f32[64,1,768]{2,1,0:T(1,128)} %copy.49), calls=%async_computation.1 | async-start | bytes 393216 | tf_op jit(solution)/shard_map/all_to_all | solution.py:109
  45.6 24.9 %all-to-all-start.2 = ((f32[64,1,768]{2,1,0:T(1,128)}), f32[64,1,768]{2,1,0:T(1,128)S(1)}, u32[]{:S(2)}, u32[]{:S(2)}) async-start(f32[64,1,768]{2,1,0:T(1,128)} %copy.54), calls=%async_computation.2 | async-start | bytes 393216 | tf_op jit(solution)/shard_map/all_to_all | solution.py:109
  58.3 2.2 %copy-start = (f32[1026,1024]{1,0:T(8,128)S(1)}, f32[1026,1024]{1,0:T(8,128)}, u32[]{:S(2)}) copy-start(f32[1026,1024]{1,0:T(8,128)} %concatenate.52) | copy-start | bytes 12607492

commit v11 on v7

--- a/solution.py
+++ b/solution.py
@@ -12,22 +12,23 @@
     high = np.arange(length // split, dtype=np.int64) * split
     coarse = (high[:, None] * frame[None, :]) % (2 * length) * (np.pi / length)
     fine = (low[:, None] * frame[None, :]) % (2 * length) * (np.pi / length)
-    return [
-        jnp.asarray(t.astype(np.float32))
-        for t in (np.cos(coarse), np.sin(coarse), np.cos(fine), np.sin(fine))
-    ]
+    return np.cos(coarse), np.sin(coarse), np.cos(fine), np.sin(fine)
 
 
-def spectral_tables(length, rows, anchor):
+def spectral_table(length, rows, anchor):
     split = 32
     blocks = rows // split
     cos_hi, sin_hi, cos_lo, sin_lo = angle_tables(length, split)
-    cos_hi, sin_hi, cos_lo, sin_lo, _ = lax.optimization_barrier(
-        (cos_hi[:blocks], sin_hi[:blocks], cos_lo, sin_lo, anchor)
-    )
-    cosine = cos_hi[:, None, :] * cos_lo[None, :, :] - sin_hi[:, None, :] * sin_lo[None, :, :]
-    sine = sin_hi[:, None, :] * cos_lo[None, :, :] + cos_hi[:, None, :] * sin_lo[None, :, :]
-    return cosine.reshape(rows, length), sine.reshape(rows, length)
+    first = np.concatenate([cos_hi[:blocks], sin_hi[:blocks]]).astype(np.float32)
+    second = np.concatenate([-sin_hi[:blocks], cos_hi[:blocks]]).astype(np.float32)
+    parts = [jnp.asarray(t) for t in (first, second, cos_lo.astype(np.float32), sin_lo.astype(np.float32))]
+    first, second, cos_lo, sin_lo, _ = lax.optimization_barrier((*parts, anchor))
+    table = first[:, None, :] * cos_lo[None, :, :] + second[:, None, :] * sin_lo[None, :, :]
+    table = table.reshape(2 * rows, length)
+    frame = jnp.arange(length, dtype=jnp.int32)
+    both_quarters = jnp.where(frame % 4 < 2, 1.0, -1.0).astype(jnp.float32)
+    row = jnp.arange(2 * rows, dtype=jnp.int32)
+    return jnp.where((row == rows)[:, None], both_quarters[None, :], table)
 
 
 def split_three(values):
@@ -54,25 +55,23 @@
     lower = (frame[None, :] <= frame[:, None]).astype(jnp.float32)
     positions = exact_product(lower, series)
     squares = jnp.sum((positions * positions).reshape(length, 3, count), axis=1)
-    cosine, sine = spectral_tables(length, half, anchor)
+    table_full = spectral_table(length, half, anchor)
     parity = jnp.where(frame % 2 == 0, 1.0, -1.0).astype(jnp.float32)
-    quarter_cos = jnp.where(frame % 4 == 0, 1.0, jnp.where(frame % 4 == 2, -1.0, 0.0))
-    quarter_sin = jnp.where(frame % 4 == 1, 1.0, jnp.where(frame % 4 == 3, -1.0, 0.0))
-    extra = jnp.stack([quarter_cos, quarter_sin]).astype(jnp.float32)
-    both = jnp.concatenate([cosine, sine, extra], axis=0)
+    quarter_cos = jnp.where(frame % 4 == 0, 1.0, jnp.where(frame % 4 == 2, -1.0, 0.0)).astype(jnp.float32)
     signed = jnp.concatenate([positions, positions * parity[:, None]], axis=1)
-    spectrum = jnp.dot(both, signed, precision=lax.Precision.HIGHEST)
+    spectrum = jnp.dot(table_full, signed, precision=lax.Precision.HIGHEST)
     real_part = spectrum[:half]
-    imag_part = spectrum[half : 2 * half]
+    low_rows = jnp.arange(half, dtype=jnp.int32)
+    imag_part = jnp.where((low_rows == 0)[:, None], 0.0, spectrum[half:])
     power = jnp.sum((real_part * real_part + imag_part * imag_part).reshape(half, 2, 3, count), axis=2)
-    top = spectrum[2 * half :, :width]
-    middle = jnp.sum((top * top).reshape(2 * 3, count), axis=0) * (2.0 / (2 * length))
+    plus, minus = spectrum[half, :width], spectrum[half, width:]
+    middle = jnp.sum((0.5 * (plus * plus + minus * minus)).reshape(3, count), axis=0) * (2.0 / (2 * length))
     low_q = jnp.arange(half, dtype=jnp.int32)
     weight = jnp.where(low_q == 0, 1.0, 2.0).astype(jnp.float32) / (2 * length)
     coef = (power * weight[:, None, None]).reshape(half, 2 * count)
     sign_q = jnp.where(low_q % 2 == 0, 1.0, -1.0).astype(jnp.float32)
     coef = jnp.concatenate([coef, coef * sign_q[:, None]], axis=1)
-    table = jnp.concatenate([cosine[:, :half], extra[:1, :half]], axis=0)
+    table = jnp.concatenate([table_full[:half, :half], quarter_cos[None, :half]], axis=0)
     folded = jnp.dot(table, coef, precision=lax.Precision.HIGHEST)
     lag = jnp.arange(half + 1, dtype=jnp.int32)
     sign_m = jnp.where(lag % 2 == 0, 1.0, -1.0).astype(jnp.float32)[:, None]

time: 59.9 us -> 61.7 us (1.030)
  the two profiles are of different devices: /device:TPU:16 before, /device:TPU:2 now
where the time goes in v11:
time: 61.7 us; the launch traced here: 61.3 us
  starting transfers between devices  21.6 us (35%)
  waiting for transfers between devices  16.9 us (27%)
  matrix products  8.11 us (13%)
  other arithmetic  7.83 us (13%)
  local copies, waits for them, and re-layouts  6.7 us (11%)
    all_to_all x1, waiting for transfers between devices, per_device(): lax.all_to_all(outgoing, 'frames', split_axis=0, concat_axis=0, tiled=True)  16.9 us
    all_to_all x1, starting transfers between devices, per_device(): lax.all_to_all(outgoing, 'frames', split_axis=0, concat_axis=0, tiled=True)  12.5 us
    all_to_all x1, starting transfers between devices, per_device(): lax.all_to_all(spread, 'atoms', split_axis=0, concat_axis=0, tiled=True)  9.13 us
    dot_general x1, matrix products, lag_table(): spectrum = jnp.dot(table_full, signed, precision=lax.Precision.HIGHEST)  4.53 us
    slice x1, local copies, waits for them, and re-layouts, lag_table(): table_full[:half, :half]  2.27 us
    select_n x1, other arithmetic, spectral_table(): return jnp.where((row == rows)[:, None], both_quarters[None, :], table)  2.27 us
    dot_general x2, matrix products, exact_product(): jnp.dot(matrix.astype(jnp.bfloat16), split_three(values), preferred_eleme...  2.18 us
    add x1, other arithmetic, spectral_table(): first[:, None, :] * cos_lo[None, :, :]  1.72 us
  transfers between devices with their start and end apart: 2, of which 1 were waited for; matrix products, arithmetic and copies ran while one was open for 11% of the time, Pallas kernels for 0%

profile of v11, /device:TPU:2, one launch (start us, length us, event | category | flops | bytes accessed | tf_op | source)
XLA Modules:
  0.0 61.3 jit_solution(886090918790893883)
XLA Ops:
  0.0 1.1 %reduce_sum.47 = f32[16,3]{0,1:T(4,128)S(1)} reduce(f32[16,3,2048]{2,0,1:T(8,128)} %param.5, f32[]{:T(128)} %constant.87.clone.1), dimensions={2}, to_apply=%region_0.0 | reduce | flops 98256 | bytes 393412 | tf_op jit(solution)/shard_map/reduce_sum | solution.py:96
  1.1 0.1 copy.34
  1.2 0.1 broadcast_in_dim.102
  1.3 0.6 broadcast_in_dim.103
  1.9 9.1 %all-to-all-start = ((f32[8,1,48]{2,1,0:T(1,128)}), f32[8,1,48]{2,1,0:T(1,128)S(1)}, u32[]{:S(2)}, u32[]{:S(2)}) async-start(f32[8,1,48]{2,1,0:T(1,128)} %broadcast_in_dim.103), calls=%async_computation | async-start | bytes 8192 | tf_op jit(solution)/shard_map/all_to_all | solution.py:98
  11.0 1.7 %multiply_add_fusion = f32[32,32,1024]{2,1,0:T(8,128)S(1)} fusion(f32[32,1024]{1,0:T(8,128)} %constant.105.clone, f32[32,1024]{1,0:T(8,128)} %constant.103.clone, f32[32,1024]{1,0:T(8,128)} %constant.104.clone, f32[32,1024]{1,0:T(8,128)} %constant.102.clone), kind=kLoop, calls=%fused_computation.3 | loop fusion | flops 3145728 | bytes 4718592 | tf_op jit(solution)/shard_map/add | solution.py:26
  12.8 2.3 %bitcast_select_fusion = f32[1024,1024]{1,0:T(8,128)} fusion(f32[32,32,1024]{2,1,0:T(8,128)S(1)} %multiply_add_fusion, f32[1024]{0:T(1024)S(1)} %fusion.51, pred[1024]{0:T(1024)(128)(4,1)S(1)} %iota_compare_fusion.3), kind=kLoop, calls=%fused_computation.2 | loop fusion | flops 1048576 | bytes 8393728 | tf_op jit(solution)/shard_map/jit(_where)/select_n | solution.py:31
  15.0 0.5 reshape.139
  15.6 2.3 %slice.74 = f32[512,512]{1,0:T(8,128)} slice(f32[1024,1024]{1,0:T(8,128)} %bitcast_select_fusion), slice={[0:512], [0:512]} | slice | bytes 2097152 | tf_op jit(solution)/shard_map/slice | solution.py:74
  17.9 0.1 div.24
  17.9 0.1 copy.36
  18.0 0.2 subtract_bitcast_fusion
  18.2 0.5 copy.37
  18.7 1.1 %copy.38 = f32[64,1,1536]{2,1,0:T(1,128)} copy(f32[64,1,1536]{0,2,1:T(8,128)S(1)} %bitcast.18) | data formatting | bytes 786432 | tf_op jit(solution)/shard_map/all_to_all | solution.py:104
  19.7 12.5 %all-to-all-start.1 = ((f32[64,1,1536]{2,1,0:T(1,128)}), f32[64,1,1536]{2,1,0:T(1,128)S(1)}, u32[]{:S(2)}, u32[]{:S(2)}) async-start(f32[64,1,1536]{2,1,0:T(1,128)} %copy.38), calls=%async_computation.1 | async-start | bytes 786432 | tf_op jit(solution)/shard_map/all_to_all | solution.py:104
  32.4 16.9 %all-to-all-done.1 = f32[64,1,1536]{2,1,0:T(1,128)S(1)} async-done(((f32[64,1,1536]{2,1,0:T(1,128)}), f32[64,1,1536]{2,1,0:T(1,128)S(1)}, u32[]{:S(2)}, u32[]{:S(2)}) %all-to-all-start.1) | async-done | bytes 393248 | tf_op jit(solution)/shard_map/all_to_all | solution.py:104
  49.2 0.9 %reduce.1 = f32[64,1536]{1,0:T(8,128)S(1)} reduce(f32[64,1,1536]{2,1,0:T(1,128)S(1)} %all-to-all-done.1, f32[]{:T(128)} %constant.107), dimensions={1}, to_apply=%all_to_all.12.reduce_sub_computation | reduce | bytes 786436 | tf_op jit(solution)/shard_map/all_to_all | solution.py:104
  50.2 0.2 reshape.140
  50.3 0.1 reduce-precision_convert_fusion.1
  50.5 1.3 %fusion.1 = f32[1024,288]{0,1:T(8,128)S(1)} fusion(bf16[1024,96]{1,0:T(8,128)(2,1)S(1)} %get-tuple-element.18, bf16[1024,96]{1,0:T(8,128)(2,1)S(1)} %get-tuple-element.19, bf16[1024,96]{1,0:T(8,128)(2,1)S(1)} %get-tuple-element.17), kind=kOutput, calls=%fused_computation.8 | convolution fusion | flops 608894976 | bytes 1769472 | tf_op jit(solution)/shard_map/dot_general | solution.py:44
  51.8 0.1 broadcast_multiply_fusion
  52.0 0.7 %copy-done = f32[1024,1024]{1,0:T(8,128)S(1)} copy-done((f32[1024,1024]{1,0:T(8,128)S(1)}, f32[1024,1024]{1,0:T(8,128)}, u32[]{:S(2)}) %copy-start) | copy-done | bytes 4194328
  52.7 4.5 %fusion.12 = f32[1024,192]{0,1:T(8,128)S(1)} fusion(f32[1024,1024]{1,0:T(8,128)S(1)} %copy-done, f32[1024,96]{0,1:T(8,128)S(1)} %get-tuple-element.15, f32[1024,96]{0,1:T(8,128)S(1)} %get-tuple-element.16), kind=kOutput, calls=%fused_computation.20 | convolution fusion | flops 2416115712 | bytes 5767168 | tf_op jit(solution)/shard_map/dot_general | solution.py:62
  57.2 0.1 fusion.35
  57.4 0.1 mul.169
  57.6 1.4 %fusion.3 = f32[513,128]{0,1:T(8,128)S(1)} fusion(f32[1,512]{1,0:T(1,128)S(1)} %bitcast.23, f32[512,512]{1,0:T(8,128)S(1)} %copy-done.1, f32[512,64]{0,1:T(8,128)S(1)} %get-tuple-element.13, f32[512,64]{0,1:T(8,128)S(1)} %get-tuple-element.14), kind=kOutput, calls=%fused_computation.11 | convolution fusion | flops 403767808 | bytes 1575424 | tf_op jit(solution)/shard_map/dot_general | solution.py:75
  59.0 0.1 fusion.32
  59.1 0.1 slice_add_fusion.4
  59.2 0.3 reverse
  59.5 0.1 slice.134
  59.7 0.9 %fusion = f32[1024,96]{0,1:T(8,128)S(1)} fusion(s32[1024]{0:T(1024)S(1)} %iota_subtract_fusion, bf16[1024,32]{0,1:T(8,128)(2,1)S(1)} %get-tuple-element.24, bf16[1024,32]{0,1:T(8,128)(2,1)S(1)} %get-tuple-element.25, bf16[1024,32]{0,1:T(8,128)(2,1)S(1)} %get-tuple-element.23), kind=kOutput, calls=%fused_computation.7 | convolution fusion | flops 208207872 | bytes 593920 | tf_op jit(solution)/shard_map/dot_general | solution.py:44
  60.6 0.7 %fusion.30 = f32[32,1024]{1,0:T(8,128)} fusion(f32[1024,96]{0,1:T(8,128)S(1)} %fusion, f32[511,32]{0,1:T(8,128)S(1)} %slice.134, f32[513,32]{0,1:T(8,128)S(1)} %get-tuple-element.20, f32[1024]{0:T(1024)S(1)} %subtract_convert_fusion), kind=kLoop, calls=%fused_computation.52 | loop fusion | flops 196608 | bytes 659456 | tf_op jit(solution)/shard_map/transpose | solution.py:88
  (30 shorter events, 0.4 us)
Async XLA Ops:
  1.9 15.9 %all-to-all-start = ((f32[8,1,48]{2,1,0:T(1,128)}), f32[8,1,48]{2,1,0:T(1,128)S(1)}, u32[]{:S(2)}, u32[]{:S(2)}) async-start(f32[8,1,48]{2,1,0:T(1,128)} %broadcast_in_dim.103), calls=%async_computation | async-start | bytes 8192 | tf_op jit(solution)/shard_map/all_to_all | solution.py:98
  12.8 2.3 %copy-start.2 = (f32[16,3,2048]{2,0,1:T(8,128)S(1)}, f32[16,3,2048]{2,0,1:T(8,128)}, u32[]{:S(2)}) copy-start(f32[16,3,2048]{2,0,1:T(8,128)} %param.5) | copy-start | bytes 1179652
  19.7 29.5 %all-to-all-start.1 = ((f32[64,1,1536]{2,1,0:T(1,128)}), f32[64,1,1536]{2,1,0:T(1,128)S(1)}, u32[]{:S(2)}, u32[]{:S(2)}) async-start(f32[64,1,1536]{2,1,0:T(1,128)} %copy.38), calls=%async_computation.1 | async-start | bytes 786432 | tf_op jit(solution)/shard_map/all_to_all | solution.py:104
  32.2 19.5 %copy-start.3 = (f32[1024]{0:T(1024)}, f32[1024]{0:T(1024)S(1)}, u32[]{:S(2)}) copy-start(f32[1024]{0:T(1024)S(1)} %select_select_fusion.1) | copy-start | bytes 12292
  50.5 2.2 %copy-start = (f32[1024,1024]{1,0:T(8,128)S(1)}, f32[1024,1024]{1,0:T(8,128)}, u32[]{:S(2)}) copy-start(f32[1024,1024]{1,0:T(8,128)} %bitcast_select_fusion) | copy-start | bytes 12582916
  51.9 5.6 %copy-start.1 = (f32[512,512]{1,0:T(8,128)S(1)}, f32[512,512]{1,0:T(8,128)}, u32[]{:S(2)}) copy-start(f32[512,512]{1,0:T(8,128)} %slice.74) | copy-start | bytes 3145732
  51.9 5.6 %slice-start = ((f32[1024]{0:T(1024)}), f32[512]{0:T(512)S(1)}, s32[]{:S(2)}) async-start(f32[1024]{0:T(1024)} %copy-done.3), calls=%async_computation.2 | async-start | bytes 4096 | tf_op jit(solution)/shard_map/slice | solution.py:74

commit v12 on v11

--- a/solution.py
+++ b/solution.py
@@ -15,14 +15,17 @@
     return np.cos(coarse), np.sin(coarse), np.cos(fine), np.sin(fine)
 
 
-def spectral_table(length, rows, anchor):
+def table_parts(length, rows):
     split = 32
     blocks = rows // split
     cos_hi, sin_hi, cos_lo, sin_lo = angle_tables(length, split)
     first = np.concatenate([cos_hi[:blocks], sin_hi[:blocks]]).astype(np.float32)
     second = np.concatenate([-sin_hi[:blocks], cos_hi[:blocks]]).astype(np.float32)
-    parts = [jnp.asarray(t) for t in (first, second, cos_lo.astype(np.float32), sin_lo.astype(np.float32))]
-    first, second, cos_lo, sin_lo, _ = lax.optimization_barrier((*parts, anchor))
+    return [jnp.asarray(t) for t in (first, second, cos_lo.astype(np.float32), sin_lo.astype(np.float32))]
+
+
+def spectral_table(length, rows, parts):
+    first, second, cos_lo, sin_lo = parts
     table = first[:, None, :] * cos_lo[None, :, :] + second[:, None, :] * sin_lo[None, :, :]
     table = table.reshape(2 * rows, length)
     frame = jnp.arange(length, dtype=jnp.int32)
@@ -47,7 +50,7 @@
     return out[:, :width] + out[:, width : 2 * width] + out[:, 2 * width :]
 
 
-def lag_table(series, count, anchor):
+def lag_table(series, count, parts):
     length = series.shape[0]
     half = length // 2
     width = 3 * count
@@ -55,7 +58,7 @@
     lower = (frame[None, :] <= frame[:, None]).astype(jnp.float32)
     positions = exact_product(lower, series)
     squares = jnp.sum((positions * positions).reshape(length, 3, count), axis=1)
-    table_full = spectral_table(length, half, anchor)
+    table_full = spectral_table(length, half, parts)
     parity = jnp.where(frame % 2 == 0, 1.0, -1.0).astype(jnp.float32)
     quarter_cos = jnp.where(frame % 4 == 0, 1.0, jnp.where(frame % 4 == 2, -1.0, 0.0)).astype(jnp.float32)
     signed = jnp.concatenate([positions, positions * parity[:, None]], axis=1)
@@ -101,9 +104,11 @@
     blocks = jnp.transpose(displacements.reshape(local_frames, 3, groups, count), (2, 0, 1, 3))
     outgoing = blocks - (summed / atom_total)[None, :, :, None]
     outgoing = outgoing.reshape(groups, local_frames * 3 * count)
+    length = local_frames * groups
+    *parts, outgoing = lax.optimization_barrier((*table_parts(length, length // 2), outgoing))
     moved = lax.all_to_all(outgoing, "frames", split_axis=0, concat_axis=0, tiled=True)
-    series = moved.reshape(groups * local_frames, 3 * count)
-    return lag_table(series, count, outgoing)
+    series = moved.reshape(length, 3 * count)
+    return lag_table(series, count, parts)
 
 
 def solution(mesh):

time: 61.7 us -> 61.4 us (level)
  waiting for transfers between devices: 16.9 us -> 13 us
  local copies, waits for them, and re-layouts: 6.7 us -> 8.63 us
  other arithmetic: 7.83 us -> 9.29 us
    all_to_all x1, waiting for transfers between devices: 16.9 us -> 13 us  [per_device(): lax.all_to_all(outgoing, 'frames', split_axis=0, concat_axis=0, tiled=True)]
    slice x1, local copies, waits for them, and re-layouts: 2.27 us -> 0.09 us  [lag_table(): table_full[:half, :half]]
    unnamed x10 -> x28, local copies, waits for them, and re-layouts: 1.12 us -> 3.08 us
    select_n x1, other arithmetic: 2.27 us -> 0.34 us  [spectral_table(): return jnp.where((row == rows)[:, None], both_quarters[None, :], table)]
    reshape x1, local copies, waits for them, and re-layouts: 0.51 us -> 1.5 us  [per_device(): displacements.reshape(local_frames, 3, groups, count)]
    sub x1, other arithmetic: 0.18 us -> 0.85 us  [per_device(): outgoing = blocks - (summed / atom_total)[None, :, :, None]]
  transfers between devices with their start and end apart: 2 -> 2, of which waited for: 1 -> 1; matrix products, arithmetic and copies ran while one was open for 11% -> 12% of each run, Pallas kernels for 0% -> 0%
where the time goes in v12:
time: 61.4 us; the launch traced here: 61 us
  starting transfers between devices  21.6 us (35%)
  waiting for transfers between devices  13 us (21%)
  other arithmetic  9.29 us (15%)
  local copies, waits for them, and re-layouts  8.63 us (14%)
  matrix products  8.12 us (13%)
    all_to_all x1, waiting for transfers between devices, per_device(): lax.all_to_all(outgoing, 'frames', split_axis=0, concat_axis=0, tiled=True)  13 us
    all_to_all x1, starting transfers between devices, per_device(): lax.all_to_all(outgoing, 'frames', split_axis=0, concat_axis=0, tiled=True)  12.4 us
    all_to_all x1, starting transfers between devices, per_device(): lax.all_to_all(spread, 'atoms', split_axis=0, concat_axis=0, tiled=True)  9.15 us
    dot_general x1, matrix products, lag_table(): spectrum = jnp.dot(table_full, signed, precision=lax.Precision.HIGHEST)  4.53 us
    unnamed x28, local copies, waits for them, and re-layouts  3.08 us
    dot_general x2, matrix products, exact_product(): jnp.dot(matrix.astype(jnp.bfloat16), split_three(values), preferred_eleme...  2.18 us
    add x1, other arithmetic, spectral_table(): first[:, None, :] * cos_lo[None, :, :]  1.54 us
    reshape x1, local copies, waits for them, and re-layouts, per_device(): displacements.reshape(local_frames, 3, groups, count)  1.5 us
  transfers between devices with their start and end apart: 2, of which 1 were waited for; matrix products, arithmetic and copies ran while one was open for 12% of the time, Pallas kernels for 0%

profile of v12, /device:TPU:2, one launch (start us, length us, event | category | flops | bytes accessed | tf_op | source)
XLA Modules:
  0.0 61.0 jit_solution(18124275362034952492)
XLA Ops:
  0.0 1.1 %reduce_sum.47 = f32[16,3]{0,1:T(4,128)S(1)} reduce(f32[16,3,2048]{2,0,1:T(8,128)} %param.5, f32[]{:T(128)} %constant.87.clone.1), dimensions={2}, to_apply=%region_0.0 | reduce | flops 98256 | bytes 393412 | tf_op jit(solution)/shard_map/reduce_sum | solution.py:99
  1.2 0.1 broadcast_in_dim.102
  1.3 0.6 broadcast_in_dim.103
  1.9 9.1 %all-to-all-start = ((f32[8,1,48]{2,1,0:T(1,128)}), f32[8,1,48]{2,1,0:T(1,128)S(1)}, u32[]{:S(2)}, u32[]{:S(2)}) async-start(f32[8,1,48]{2,1,0:T(1,128)} %broadcast_in_dim.103), calls=%async_computation | async-start | bytes 8192 | tf_op jit(solution)/shard_map/all_to_all | solution.py:101
  11.0 0.6 fusion.51
  11.6 0.6 iota_compare_fusion.3
  12.2 0.6 select_multiply_fusion
  12.8 0.6 iota_subtract_fusion
  13.4 0.6 iota_compare_fusion.4
  14.0 1.5 %reshape.140 = f32[16,3,64,32]{3,2,0,1:T(8,128)S(1)} reshape(f32[16,3,2048]{2,0,1:T(8,128)} %param.5) | data formatting | bytes 786432 | tf_op jit(solution)/shard_map/reshape | solution.py:104
  15.6 0.6 %slice.83 = f32[511]{0:T(512)} slice(f32[513]{0:T(1024)S(1)} %get-tuple-element.32), slice={[1:512]} | slice | bytes 4088 | tf_op jit(solution)/shard_map/slice | solution.py:84
  16.3 0.7 %copy.36 = f32[16,3]{0,1:T(4,128)} copy(f32[16,3]{1,0:T(8,128)S(1)} %div.24) | data formatting | bytes 384 | tf_op jit(solution)/shard_map/div | solution.py:105
  17.0 0.8 %subtract_bitcast_fusion = f32[64,16,3,32]{3,0,1,2:T(8,128)S(1)} fusion(f32[16,3,64,32]{3,2,0,1:T(8,128)S(1)} %reshape.140, f32[16,3]{0,1:T(4,128)} %copy.36), kind=kLoop, calls=%fused_computation.10 | loop fusion | flops 98304 | bytes 786624 | tf_op jit(solution)/shard_map/sub | solution.py:105
  17.9 0.5 copy.37
  18.3 1.1 %copy.38 = f32[64,1,1536]{2,1,0:T(1,128)} copy(f32[64,1,1536]{0,2,1:T(8,128)S(1)} %bitcast.19) | data formatting | bytes 786432 | tf_op jit(solution)/shard_map/all_to_all | solution.py:109
  19.4 12.4 %all-to-all-start.1 = ((f32[64,1,1536]{2,1,0:T(1,128)}), f32[64,1,1536]{2,1,0:T(1,128)S(1)}, u32[]{:S(2)}, u32[]{:S(2)}) async-start(f32[64,1,1536]{2,1,0:T(1,128)} %copy.38), calls=%async_computation.1 | async-start | bytes 786432 | tf_op jit(solution)/shard_map/all_to_all | solution.py:109
  31.9 1.5 %multiply_add_fusion = f32[32,32,1024]{2,1,0:T(8,128)S(1)} fusion(f32[32,1024]{1,0:T(8,128)} %constant.105.clone, f32[32,1024]{1,0:T(8,128)S(1)} %copy-done.3, f32[32,1024]{1,0:T(8,128)S(1)} %copy-done.4, f32[32,1024]{1,0:T(8,128)S(1)} %copy-done.2), kind=kLoop, calls=%fused_computation.3 | loop fusion | flops 3145728 | bytes 4718592 | tf_op jit(solution)/shard_map/add | solution.py:29
  33.4 0.3 bitcast_select_fusion
  33.8 1.9 %copy-done = f32[1024,1024]{1,0:T(8,128)} copy-done((f32[1024,1024]{1,0:T(8,128)}, f32[1024,1024]{1,0:T(8,128)S(1)}, u32[]{:S(2)}) %copy-start) | copy-done | bytes 4194328
  35.8 13.0 %all-to-all-done.1 = f32[64,1,1536]{2,1,0:T(1,128)S(1)} async-done(((f32[64,1,1536]{2,1,0:T(1,128)}), f32[64,1,1536]{2,1,0:T(1,128)S(1)}, u32[]{:S(2)}, u32[]{:S(2)}) %all-to-all-start.1) | async-done | bytes 393248 | tf_op jit(solution)/shard_map/all_to_all | solution.py:109
  48.9 0.9 %reduce.1 = f32[64,1536]{1,0:T(8,128)S(1)} reduce(f32[64,1,1536]{2,1,0:T(1,128)S(1)} %all-to-all-done.1, f32[]{:T(128)} %constant.107), dimensions={1}, to_apply=%all_to_all.12.reduce_sub_computation | reduce | bytes 786436 | tf_op jit(solution)/shard_map/all_to_all | solution.py:109
  49.8 0.2 reshape.142
  50.0 0.1 reduce-precision_convert_fusion.1
  50.1 1.3 %fusion.1 = f32[1024,288]{0,1:T(8,128)S(1)} fusion(bf16[1024,96]{1,0:T(8,128)(2,1)S(1)} %get-tuple-element.20, bf16[1024,96]{1,0:T(8,128)(2,1)S(1)} %get-tuple-element.21, bf16[1024,96]{1,0:T(8,128)(2,1)S(1)} %get-tuple-element.19), kind=kOutput, calls=%fused_computation.8 | convolution fusion | flops 608894976 | bytes 1769472 | tf_op jit(solution)/shard_map/dot_general | solution.py:47
  51.6 0.7 %copy-done.1 = f32[1024,1024]{1,0:T(8,128)S(1)} copy-done((f32[1024,1024]{1,0:T(8,128)S(1)}, f32[1024,1024]{1,0:T(8,128)}, u32[]{:S(2)}) %copy-start.1) | copy-done | bytes 4194328
  52.3 4.5 %fusion.12 = f32[1024,192]{0,1:T(8,128)S(1)} fusion(f32[1024,1024]{1,0:T(8,128)S(1)} %copy-done.1, f32[1024,96]{0,1:T(8,128)S(1)} %get-tuple-element.17, f32[1024,96]{0,1:T(8,128)S(1)} %get-tuple-element.18), kind=kOutput, calls=%fused_computation.20 | convolution fusion | flops 2416115712 | bytes 5767168 | tf_op jit(solution)/shard_map/dot_general | solution.py:65
  56.8 0.1 fusion.35
  57.3 1.4 %fusion.3 = f32[513,128]{0,1:T(8,128)S(1)} fusion(f32[1,512]{1,0:T(1,128)S(1)} %bitcast.24, f32[512,512]{1,0:T(8,128)S(1)} %slice.74, f32[512,64]{0,1:T(8,128)S(1)} %get-tuple-element.15, f32[512,64]{0,1:T(8,128)S(1)} %get-tuple-element.16), kind=kOutput, calls=%fused_computation.11 | convolution fusion | flops 403767808 | bytes 1575424 | tf_op jit(solution)/shard_map/dot_general | solution.py:78
  58.8 0.1 slice_add_fusion.4
  58.9 0.3 reverse
  59.4 0.9 %fusion = f32[1024,96]{0,1:T(8,128)S(1)} fusion(s32[1024]{0:T(1024)S(1)} %copy-done.10, bf16[1024,32]{0,1:T(8,128)(2,1)S(1)} %get-tuple-element.26, bf16[1024,32]{0,1:T(8,128)(2,1)S(1)} %get-tuple-element.27, bf16[1024,32]{0,1:T(8,128)(2,1)S(1)} %get-tuple-element.25), kind=kOutput, calls=%fused_computation.7 | convolution fusion | flops 208207872 | bytes 593920 | tf_op jit(solution)/shard_map/dot_general | solution.py:47
  60.3 0.7 %fusion.30 = f32[32,1024]{1,0:T(8,128)} fusion(f32[1024,96]{0,1:T(8,128)S(1)} %fusion, f32[511,32]{0,1:T(8,128)S(1)} %slice.134, f32[513,32]{0,1:T(8,128)S(1)} %get-tuple-element.22, f32[1024]{0:T(1024)S(1)} %subtract_convert_fusion), kind=kLoop, calls=%fused_computation.52 | loop fusion | flops 196608 | bytes 659456 | tf_op jit(solution)/shard_map/transpose | solution.py:91
  (48 shorter events, 1.0 us)
Async XLA Ops:
  1.9 14.3 %all-to-all-start = ((f32[8,1,48]{2,1,0:T(1,128)}), f32[8,1,48]{2,1,0:T(1,128)S(1)}, u32[]{:S(2)}, u32[]{:S(2)}) async-start(f32[8,1,48]{2,1,0:T(1,128)} %broadcast_in_dim.103), calls=%async_computation | async-start | bytes 8192 | tf_op jit(solution)/shard_map/all_to_all | solution.py:101
  12.8 3.4 %copy-start.6 = (f32[1024]{0:T(1024)}, f32[1024]{0:T(1024)S(1)}, u32[]{:S(2)}) copy-start(f32[1024]{0:T(1024)S(1)} %select_select_fusion.1) | copy-start | bytes 12292
  15.5 16.3 %copy-start.2 = (f32[32,1024]{1,0:T(8,128)S(1)}, f32[32,1024]{1,0:T(8,128)}, u32[]{:S(2)}) copy-start(f32[32,1024]{1,0:T(8,128)} %constant.102.clone) | copy-start | bytes 393220
  15.5 16.3 %copy-start.3 = (f32[32,1024]{1,0:T(8,128)S(1)}, f32[32,1024]{1,0:T(8,128)}, u32[]{:S(2)}) copy-start(f32[32,1024]{1,0:T(8,128)} %constant.103.clone) | copy-start | bytes 393220
  15.5 16.3 %copy-start.4 = (f32[32,1024]{1,0:T(8,128)S(1)}, f32[32,1024]{1,0:T(8,128)}, u32[]{:S(2)}) copy-start(f32[32,1024]{1,0:T(8,128)} %constant.104.clone) | copy-start | bytes 393220
  17.9 15.6 %copy-start.5 = (f32[1024]{0:T(1024)S(1)}, f32[1024]{0:T(1024)}, u32[]{:S(2)}) copy-start(f32[1024]{0:T(1024)} %fusion.51) | copy-start | bytes 12292
  17.9 15.6 %copy-start.11 = (pred[1024]{0:T(1024)(128)(4,1)S(1)}, pred[1024]{0:T(1024)(128)(4,1)}, u32[]{:S(2)}) copy-start(pred[1024]{0:T(1024)(128)(4,1)} %iota_compare_fusion.3) | copy-start | bytes 3076
  19.4 29.5 %all-to-all-start.1 = ((f32[64,1,1536]{2,1,0:T(1,128)}), f32[64,1,1536]{2,1,0:T(1,128)S(1)}, u32[]{:S(2)}, u32[]{:S(2)}) async-start(f32[64,1,1536]{2,1,0:T(1,128)} %copy.38), calls=%async_computation.1 | async-start | bytes 786432 | tf_op jit(solution)/shard_map/all_to_all | solution.py:109
  33.8 1.9 %copy-start = (f32[1024,1024]{1,0:T(8,128)}, f32[1024,1024]{1,0:T(8,128)S(1)}, u32[]{:S(2)}) copy-start(f32[1024,1024]{1,0:T(8,128)S(1)} %bitcast_select_fusion) | copy-start | bytes 12582916
  50.1 2.2 %copy-start.1 = (f32[1024,1024]{1,0:T(8,128)S(1)}, f32[1024,1024]{1,0:T(8,128)}, u32[]{:S(2)}) copy-start(f32[1024,1024]{1,0:T(8,128)} %copy-done) | copy-start | bytes 12582916
  51.4 5.6 %copy-start.12 = (pred[512]{0:T(512)(128)(4,1)S(1)}, pred[512]{0:T(512)(128)(4,1)}, u32[]{:S(2)}) copy-start(pred[512]{0:T(512)(128)(4,1)} %iota_compare_fusion.4) | copy-start | bytes 1540
  51.5 5.7 %copy-start.8 = (f32[512]{0:T(512)S(1)}, f32[512]{0:T(512)}, u32[]{:S(2)}) copy-start(f32[512]{0:T(512)} %get-tuple-element.29) | copy-start | bytes 6148
  51.5 5.7 %copy-start.9 = (f32[512]{0:T(512)S(1)}, f32[512]{0:T(512)}, u32[]{:S(2)}) copy-start(f32[512]{0:T(512)} %get-tuple-element.30) | copy-start | bytes 6148
  51.6 5.7 %slice-start = ((f32[1024]{0:T(1024)}), f32[512]{0:T(512)S(1)}, s32[]{:S(2)}) async-start(f32[1024]{0:T(1024)} %copy-done.6), calls=%async_computation.2 | async-start | bytes 4096 | tf_op jit(solution)/shard_map/slice | solution.py:77
  52.3 6.5 %copy-start.7 = (f32[511]{0:T(512)S(1)}, f32[511]{0:T(512)}, u32[]{:S(2)}) copy-start(f32[511]{0:T(512)} %slice.83) | copy-start | bytes 6136
  56.8 2.5 %copy-start.10 = (s32[1024]{0:T(1024)S(1)}, s32[1024]{0:T(1024)}, u32[]{:S(2)}) copy-start(s32[1024]{0:T(1024)} %iota_subtract_fusion) | copy-start | bytes 12292

commit v13 on v12

--- a/solution.py
+++ b/solution.py
@@ -59,26 +59,24 @@
     positions = exact_product(lower, series)
     squares = jnp.sum((positions * positions).reshape(length, 3, count), axis=1)
     table_full = spectral_table(length, half, parts)
-    parity = jnp.where(frame % 2 == 0, 1.0, -1.0).astype(jnp.float32)
-    quarter_cos = jnp.where(frame % 4 == 0, 1.0, jnp.where(frame % 4 == 2, -1.0, 0.0)).astype(jnp.float32)
+    steps = np.arange(length)
+    parity = jnp.asarray(np.where(steps % 2 == 0, 1.0, -1.0).astype(np.float32))
+    quarter_cos = np.where(steps % 4 == 0, 1.0, np.where(steps % 4 == 2, -1.0, 0.0)).astype(np.float32)
     signed = jnp.concatenate([positions, positions * parity[:, None]], axis=1)
     spectrum = jnp.dot(table_full, signed, precision=lax.Precision.HIGHEST)
     real_part = spectrum[:half]
-    low_rows = jnp.arange(half, dtype=jnp.int32)
-    imag_part = jnp.where((low_rows == 0)[:, None], 0.0, spectrum[half:])
+    imag_part = spectrum[half:] * jnp.asarray((steps[:half] != 0).astype(np.float32))[:, None]
     power = jnp.sum((real_part * real_part + imag_part * imag_part).reshape(half, 2, 3, count), axis=2)
     plus, minus = spectrum[half, :width], spectrum[half, width:]
     middle = jnp.sum((0.5 * (plus * plus + minus * minus)).reshape(3, count), axis=0) * (2.0 / (2 * length))
-    low_q = jnp.arange(half, dtype=jnp.int32)
-    weight = jnp.where(low_q == 0, 1.0, 2.0).astype(jnp.float32) / (2 * length)
+    weight = jnp.asarray((np.where(steps[:half] == 0, 1.0, 2.0) / (2 * length)).astype(np.float32))
     coef = (power * weight[:, None, None]).reshape(half, 2 * count)
-    sign_q = jnp.where(low_q % 2 == 0, 1.0, -1.0).astype(jnp.float32)
+    sign_q = parity[:half]
     coef = jnp.concatenate([coef, coef * sign_q[:, None]], axis=1)
-    table = jnp.concatenate([table_full[:half, :half], quarter_cos[None, :half]], axis=0)
+    table = jnp.concatenate([table_full[:half, :half], jnp.asarray(quarter_cos[None, :half])], axis=0)
     folded = jnp.dot(table, coef, precision=lax.Precision.HIGHEST)
-    lag = jnp.arange(half + 1, dtype=jnp.int32)
-    sign_m = jnp.where(lag % 2 == 0, 1.0, -1.0).astype(jnp.float32)[:, None]
-    quarter = jnp.where(lag % 4 == 0, 1.0, jnp.where(lag % 4 == 2, -1.0, 0.0)).astype(jnp.float32)[:, None]
+    sign_m = parity[: half + 1, None]
+    quarter = jnp.asarray(quarter_cos[: half + 1, None])
     near = folded[:, :count] + sign_m * folded[:, count : 2 * count] + middle[None, :] * quarter
     far = folded[:, 2 * count : 3 * count] + sign_m * folded[:, 3 * count :] + middle[None, :] * quarter
     corr = jnp.concatenate([near, jnp.flip(far[1:half], axis=0)], axis=0)
@@ -87,7 +85,7 @@
         + (frame[None, :] <= (length - 1 - frame)[:, None]).astype(jnp.float32)
     )
     numer = exact_product(window, squares) - 2.0 * corr
-    counts = (length - frame).astype(jnp.float32)
+    counts = jnp.asarray((length - steps).astype(np.float32))
     return jnp.transpose(numer / counts[:, None])
 
 

time: 61.4 us -> 58.9 us (0.959)
  the two profiles are of different devices: /device:TPU:2 before, /device:TPU:16 now
where the time goes in v13:
time: 58.9 us; the launch traced here: 58.6 us
  starting transfers between devices  20.8 us (35%)
  waiting for transfers between devices  14.9 us (25%)
  local copies, waits for them, and re-layouts  8.2 us (14%)
  matrix products  8.12 us (14%)
  other arithmetic  6.26 us (11%)
    all_to_all x1, starting transfers between devices, per_device(): lax.all_to_all(outgoing, 'frames', split_axis=0, concat_axis=0, tiled=True)  16.5 us
    all_to_all x1, waiting for transfers between devices, per_device(): lax.all_to_all(outgoing, 'frames', split_axis=0, concat_axis=0, tiled=True)  12.6 us
    dot_general x1, matrix products, lag_table(): spectrum = jnp.dot(table_full, signed, precision=lax.Precision.HIGHEST)  4.53 us
    all_to_all x1, starting transfers between devices, per_device(): lax.all_to_all(spread, 'atoms', split_axis=0, concat_axis=0, tiled=True)  4.3 us
    unnamed x30, local copies, waits for them, and re-layouts  3.07 us
    all_to_all x1, waiting for transfers between devices, per_device(): lax.all_to_all(spread, 'atoms', split_axis=0, concat_axis=0, tiled=True)  2.23 us
    dot_general x2, matrix products, exact_product(): jnp.dot(matrix.astype(jnp.bfloat16), split_three(values), preferred_eleme...  2.18 us
    add x1, other arithmetic, spectral_table(): first[:, None, :] * cos_lo[None, :, :]  1.54 us
  transfers between devices with their start and end apart: 2, of which 2 were waited for; matrix products, arithmetic and copies ran while one was open for 8% of the time, Pallas kernels for 0%

profile of v13, /device:TPU:16, one launch (start us, length us, event | category | flops | bytes accessed | tf_op | source)
XLA Modules:
  0.0 58.6 jit_solution(4321921140231659908)
XLA Ops:
  0.0 1.1 %reduce_sum.47 = f32[16,3]{0,1:T(4,128)S(1)} reduce(f32[16,3,2048]{2,0,1:T(8,128)} %param.11, f32[]{:T(128)} %constant.20.clone.1), dimensions={2}, to_apply=%region_0.0 | reduce | flops 98256 | bytes 393412 | tf_op jit(solution)/shard_map/reduce_sum | solution.py:97
  1.1 0.1 copy.40
  1.2 0.1 broadcast_in_dim.28
  1.3 0.6 %broadcast_in_dim.29 = f32[8,1,48]{2,1,0:T(1,128)} broadcast(f32[48]{0:T(128)S(1)} %broadcast_in_dim.28), dimensions={2} | broadcast | bytes 1728 | tf_op jit(solution)/shard_map/broadcast_in_dim | solution.py:98
  1.9 4.3 %all-to-all-start = ((f32[8,1,48]{2,1,0:T(1,128)}), f32[8,1,48]{2,1,0:T(1,128)S(1)}, u32[]{:S(2)}, u32[]{:S(2)}) async-start(f32[8,1,48]{2,1,0:T(1,128)} %broadcast_in_dim.29), calls=%async_computation | async-start | bytes 8192 | tf_op jit(solution)/shard_map/all_to_all | solution.py:99
  6.2 0.6 iota_compare_fusion.3
  6.8 1.5 %reshape.85 = f32[16,3,64,32]{3,2,0,1:T(8,128)S(1)} reshape(f32[16,3,2048]{2,0,1:T(8,128)} %param.11) | data formatting | bytes 786432 | tf_op jit(solution)/shard_map/reshape | solution.py:102
  8.3 0.8 %slice.87 = f32[511]{0:T(512)S(1)} slice(f32[513]{0:T(1024)} %constant.70), slice={[1:512]} | slice | bytes 4088 | tf_op jit(solution)/shard_map/slice | solution.py:82
  9.1 2.2 %all-to-all-done = f32[8,1,48]{2,1,0:T(1,128)S(1)} async-done(((f32[8,1,48]{2,1,0:T(1,128)}), f32[8,1,48]{2,1,0:T(1,128)S(1)}, u32[]{:S(2)}, u32[]{:S(2)}) %all-to-all-start) | async-done | bytes 1568 | tf_op jit(solution)/shard_map/all_to_all | solution.py:99
  11.6 0.2 subtract_bitcast_fusion
  11.8 0.5 copy.43
  12.2 1.1 %copy.44 = f32[64,1,1536]{2,1,0:T(1,128)} copy(f32[64,1,1536]{0,2,1:T(8,128)S(1)} %bitcast.19) | data formatting | bytes 786432 | tf_op jit(solution)/shard_map/all_to_all | solution.py:107
  13.3 16.5 %all-to-all-start.1 = ((f32[64,1,1536]{2,1,0:T(1,128)}), f32[64,1,1536]{2,1,0:T(1,128)S(1)}, u32[]{:S(2)}, u32[]{:S(2)}) async-start(f32[64,1,1536]{2,1,0:T(1,128)} %copy.44), calls=%async_computation.1 | async-start | bytes 786432 | tf_op jit(solution)/shard_map/all_to_all | solution.py:107
  29.8 1.5 %multiply_add_fusion = f32[32,32,1024]{2,1,0:T(8,128)S(1)} fusion(f32[32,1024]{1,0:T(8,128)} %constant.60.clone, f32[32,1024]{1,0:T(8,128)S(1)} %copy-done.3, f32[32,1024]{1,0:T(8,128)S(1)} %copy-done.4, f32[32,1024]{1,0:T(8,128)S(1)} %copy-done.2), kind=kLoop, calls=%fused_computation.3 | loop fusion | flops 3145728 | bytes 4718592 | tf_op jit(solution)/shard_map/add | solution.py:29
  31.4 0.3 bitcast_select_fusion
  31.7 1.9 %copy-done = f32[1024,1024]{1,0:T(8,128)} copy-done((f32[1024,1024]{1,0:T(8,128)}, f32[1024,1024]{1,0:T(8,128)S(1)}, u32[]{:S(2)}) %copy-start) | copy-done | bytes 4194328
  33.7 0.1 slice.78
  33.8 12.6 %all-to-all-done.1 = f32[64,1,1536]{2,1,0:T(1,128)S(1)} async-done(((f32[64,1,1536]{2,1,0:T(1,128)}), f32[64,1,1536]{2,1,0:T(1,128)S(1)}, u32[]{:S(2)}, u32[]{:S(2)}) %all-to-all-start.1) | async-done | bytes 393248 | tf_op jit(solution)/shard_map/all_to_all | solution.py:107
  46.4 0.9 %reduce.1 = f32[64,1536]{1,0:T(8,128)S(1)} reduce(f32[64,1,1536]{2,1,0:T(1,128)S(1)} %all-to-all-done.1, f32[]{:T(128)} %constant.72), dimensions={1}, to_apply=%all_to_all.12.reduce_sub_computation | reduce | bytes 786436 | tf_op jit(solution)/shard_map/all_to_all | solution.py:107
  47.3 0.2 reshape.87
  47.5 0.1 reduce-precision_convert_fusion.1
  47.7 1.3 %fusion.1 = f32[1024,288]{0,1:T(8,128)S(1)} fusion(bf16[1024,96]{1,0:T(8,128)(2,1)S(1)} %get-tuple-element.18, bf16[1024,96]{1,0:T(8,128)(2,1)S(1)} %get-tuple-element.19, bf16[1024,96]{1,0:T(8,128)(2,1)S(1)} %get-tuple-element.17), kind=kOutput, calls=%fused_computation.8 | convolution fusion | flops 608894976 | bytes 1769472 | tf_op jit(solution)/shard_map/dot_general | solution.py:47
  49.0 0.1 broadcast_multiply_fusion
  49.2 0.7 %copy-done.1 = f32[1024,1024]{1,0:T(8,128)S(1)} copy-done((f32[1024,1024]{1,0:T(8,128)S(1)}, f32[1024,1024]{1,0:T(8,128)}, u32[]{:S(2)}) %copy-start.1) | copy-done | bytes 4194328
  49.9 4.5 %fusion.12 = f32[1024,192]{0,1:T(8,128)S(1)} fusion(f32[1024,1024]{1,0:T(8,128)S(1)} %copy-done.1, f32[1024,96]{0,1:T(8,128)S(1)} %get-tuple-element.15, f32[1024,96]{0,1:T(8,128)S(1)} %get-tuple-element.16), kind=kOutput, calls=%fused_computation.20 | convolution fusion | flops 2416115712 | bytes 5767168 | tf_op jit(solution)/shard_map/dot_general | solution.py:66
  54.4 0.1 fusion.35
  54.8 1.4 %fusion.3 = f32[513,128]{0,1:T(8,128)S(1)} fusion(f32[1,512]{1,0:T(1,128)S(1)} %copy-done.9, f32[512,512]{1,0:T(8,128)S(1)} %slice.78, f32[512,64]{0,1:T(8,128)S(1)} %get-tuple-element.24, f32[512,64]{0,1:T(8,128)S(1)} %get-tuple-element.23), kind=kOutput, calls=%fused_computation.11 | convolution fusion | flops 403767808 | bytes 1575424 | tf_op jit(solution)/shard_map/dot_general | solution.py:77
  56.3 0.1 fusion.32
  56.3 0.1 slice_add_fusion.4
  56.5 0.3 reverse
  56.9 0.9 %fusion = f32[1024,96]{0,1:T(8,128)S(1)} fusion(s32[1024]{0:T(1024)S(1)} %iota_subtract_fusion, bf16[1024,32]{0,1:T(8,128)(2,1)S(1)} %get-tuple-element.26, bf16[1024,32]{0,1:T(8,128)(2,1)S(1)} %get-tuple-element.27, bf16[1024,32]{0,1:T(8,128)(2,1)S(1)} %get-tuple-element.25), kind=kOutput, calls=%fused_computation.7 | convolution fusion | flops 208207872 | bytes 593920 | tf_op jit(solution)/shard_map/dot_general | solution.py:47
  57.9 0.7 %fusion.30 = f32[32,1024]{1,0:T(8,128)} fusion(f32[1024,96]{0,1:T(8,128)S(1)} %fusion, f32[511,32]{0,1:T(8,128)S(1)} %slice.138, f32[513,32]{0,1:T(8,128)S(1)} %get-tuple-element.20, f32[1024]{0:T(1024)S(1)} %copy-done.6), kind=kLoop, calls=%fused_computation.52 | loop fusion | flops 196608 | bytes 659456 | tf_op jit(solution)/shard_map/transpose | solution.py:89
  (42 shorter events, 0.7 us)
Async XLA Ops:
  1.9 9.5 %all-to-all-start = ((f32[8,1,48]{2,1,0:T(1,128)}), f32[8,1,48]{2,1,0:T(1,128)S(1)}, u32[]{:S(2)}, u32[]{:S(2)}) async-start(f32[8,1,48]{2,1,0:T(1,128)} %broadcast_in_dim.29), calls=%async_computation | async-start | bytes 8192 | tf_op jit(solution)/shard_map/all_to_all | solution.py:99
  8.3 21.5 %copy-start.2 = (f32[32,1024]{1,0:T(8,128)S(1)}, f32[32,1024]{1,0:T(8,128)}, u32[]{:S(2)}) copy-start(f32[32,1024]{1,0:T(8,128)} %constant.57.clone) | copy-start | bytes 393220
  8.3 21.5 %copy-start.3 = (f32[32,1024]{1,0:T(8,128)S(1)}, f32[32,1024]{1,0:T(8,128)}, u32[]{:S(2)}) copy-start(f32[32,1024]{1,0:T(8,128)} %constant.58.clone) | copy-start | bytes 393220
  8.3 21.5 %copy-start.4 = (f32[32,1024]{1,0:T(8,128)S(1)}, f32[32,1024]{1,0:T(8,128)}, u32[]{:S(2)}) copy-start(f32[32,1024]{1,0:T(8,128)} %constant.59.clone) | copy-start | bytes 393220
  11.8 19.6 %copy-start.13 = (pred[1024]{0:T(1024)(128)(4,1)S(1)}, pred[1024]{0:T(1024)(128)(4,1)}, u32[]{:S(2)}) copy-start(pred[1024]{0:T(1024)(128)(4,1)} %iota_compare_fusion.3) | copy-start | bytes 3076
  13.3 33.1 %all-to-all-start.1 = ((f32[64,1,1536]{2,1,0:T(1,128)}), f32[64,1,1536]{2,1,0:T(1,128)S(1)}, u32[]{:S(2)}, u32[]{:S(2)}) async-start(f32[64,1,1536]{2,1,0:T(1,128)} %copy.44), calls=%async_computation.1 | async-start | bytes 786432 | tf_op jit(solution)/shard_map/all_to_all | solution.py:107
  31.7 1.9 %copy-start = (f32[1024,1024]{1,0:T(8,128)}, f32[1024,1024]{1,0:T(8,128)S(1)}, u32[]{:S(2)}) copy-start(f32[1024,1024]{1,0:T(8,128)S(1)} %bitcast_select_fusion) | copy-start | bytes 12582916
  33.8 15.2 %copy-start.8 = (f32[1024]{0:T(1024)S(1)}, f32[1024]{0:T(1024)}, u32[]{:S(2)}) copy-start(f32[1024]{0:T(1024)} %constant.61.clone) | copy-start | bytes 12292
  47.7 2.2 %copy-start.1 = (f32[1024,1024]{1,0:T(8,128)S(1)}, f32[1024,1024]{1,0:T(8,128)}, u32[]{:S(2)}) copy-start(f32[1024,1024]{1,0:T(8,128)} %copy-done) | copy-start | bytes 12582916
  49.0 5.5 %copy-start.12 = (f32[512]{0:T(512)S(1)}, f32[512]{0:T(512)}, u32[]{:S(2)}) copy-start(f32[512]{0:T(512)} %constant.62.clone) | copy-start | bytes 6148
  49.1 5.7 %copy-start.10 = (f32[512]{0:T(512)S(1)}, f32[512]{0:T(512)}, u32[]{:S(2)}) copy-start(f32[512]{0:T(512)} %constant.63.clone) | copy-start | bytes 6148
  49.1 5.7 %copy-start.11 = (f32[512]{0:T(512)S(1)}, f32[512]{0:T(512)}, u32[]{:S(2)}) copy-start(f32[512]{0:T(512)} %constant.69) | copy-start | bytes 6148
  49.2 5.6 %copy-start.9 = (f32[1,512]{1,0:T(1,128)S(1)}, f32[1,512]{1,0:T(1,128)}, u32[]{:S(2)}) copy-start(f32[1,512]{1,0:T(1,128)} %constant.64.clone) | copy-start | bytes 6148
  49.9 6.4 %copy-start.5 = (f32[513]{0:T(1024)S(1)}, f32[513]{0:T(1024)}, u32[]{:S(2)}) copy-start(f32[513]{0:T(1024)} %constant.70) | copy-start | bytes 6160
  49.9 6.4 %copy-start.7 = (f32[513]{0:T(1024)S(1)}, f32[513]{0:T(1024)}, u32[]{:S(2)}) copy-start(f32[513]{0:T(1024)} %constant.71) | copy-start | bytes 6160
  54.8 3.0 %copy-start.6 = (f32[1024]{0:T(1024)S(1)}, f32[1024]{0:T(1024)}, u32[]{:S(2)}) copy-start(f32[1024]{0:T(1024)} %constant.68) | copy-start | bytes 12292

commit v14 on v13

--- a/solution.py
+++ b/solution.py
@@ -93,19 +93,23 @@
     local_frames, _, atom_count = displacements.shape
     groups = lax.axis_size("frames")
     atom_total = atom_count * lax.axis_size("atoms")
+    count = atom_count // groups
+    length = local_frames * groups
+    blocks = jnp.transpose(displacements.reshape(local_frames, 3, groups, count), (2, 0, 1, 3))
+    blocks = blocks.reshape(groups, local_frames * 3 * count)
+    *parts, blocks = lax.optimization_barrier((*table_parts(length, length // 2), blocks))
+    moved = lax.all_to_all(blocks, "frames", split_axis=0, concat_axis=0, tiled=True)
     members = lax.axis_size("atoms")
     partial_sum = jnp.sum(displacements, axis=2).reshape(1, local_frames * 3)
     spread = jnp.broadcast_to(partial_sum, (members, local_frames * 3))
+    spread, moved = lax.optimization_barrier((spread, moved))
     gathered = lax.all_to_all(spread, "atoms", split_axis=0, concat_axis=0, tiled=True)
-    summed = jnp.sum(gathered, axis=0).reshape(local_frames, 3)
-    count = atom_count // groups
-    blocks = jnp.transpose(displacements.reshape(local_frames, 3, groups, count), (2, 0, 1, 3))
-    outgoing = blocks - (summed / atom_total)[None, :, :, None]
-    outgoing = outgoing.reshape(groups, local_frames * 3 * count)
-    length = local_frames * groups
-    *parts, outgoing = lax.optimization_barrier((*table_parts(length, length // 2), outgoing))
-    moved = lax.all_to_all(outgoing, "frames", split_axis=0, concat_axis=0, tiled=True)
-    series = moved.reshape(length, 3 * count)
+    drift = jnp.sum(gathered, axis=0, keepdims=True) / atom_total
+    everywhere = lax.all_to_all(
+        jnp.broadcast_to(drift, (groups, local_frames * 3)), "frames", split_axis=0, concat_axis=0, tiled=True
+    )
+    raw = moved.reshape(groups, local_frames, 3, count)
+    series = (raw - everywhere.reshape(groups, local_frames, 3, 1)).reshape(length, 3 * count)
     return lag_table(series, count, parts)
 
 

time: 58.9 us -> 82.9 us (1.41)
  the two profiles are of different devices: /device:TPU:16 before, /device:TPU:2 now
where the time goes in v14:
time: 82.9 us; the launch traced here: 82.5 us
  starting transfers between devices  26.4 us (32%)
  waiting for transfers between devices  23.4 us (28%)
  local copies, waits for them, and re-layouts  13.5 us (16%)
  other arithmetic  10.7 us (13%)
  matrix products  8.11 us (10%)
    all_to_all x1, starting transfers between devices, per_device(): lax.all_to_all(blocks, 'frames', split_axis=0, concat_axis=0, tiled=True)  16.6 us
    all_to_all x1, waiting for transfers between devices, per_device(): lax.all_to_all(blocks, 'frames', split_axis=0, concat_axis=0, tiled=True)  14.1 us
    all_to_all x1, waiting for transfers between devices, per_device(): lax.all_to_all(jnp.broadcast_to(drift, (groups, local_frames * 3)), 'fram...  9.33 us
    all_to_all x1, starting transfers between devices, per_device(): lax.all_to_all(jnp.broadcast_to(drift, (groups, local_frames * 3)), 'fram...  4.95 us
    sub x3, local copies, waits for them, and re-layouts, per_device(): raw - everywhere.reshape(groups, local_frames, 3, 1)  4.85 us
    all_to_all x1, starting transfers between devices, per_device(): lax.all_to_all(spread, 'atoms', split_axis=0, concat_axis=0, tiled=True)  4.83 us
    dot_general x1, matrix products, lag_table(): spectrum = jnp.dot(table_full, signed, precision=lax.Precision.HIGHEST)  4.53 us
    select_n x1, other arithmetic, spectral_table(): return jnp.where((row == rows)[:, None], both_quarters[None, :], table)  4.48 us
  transfers between devices with their start and end apart: 3, of which 2 were waited for; matrix products, arithmetic and copies ran while one was open for 12% of the time, Pallas kernels for 0%

profile of v14, /device:TPU:2, one launch (start us, length us, event | category | flops | bytes accessed | tf_op | source)
XLA Modules:
  0.0 82.5 jit_solution(15491563368136270551)
XLA Ops:
  0.0 1.6 %reshape.87 = f32[16,3,64,32]{3,2,0,1:T(8,128)S(1)} reshape(f32[16,3,2048]{2,0,1:T(8,128)} %param.11) | data formatting | bytes 786432 | tf_op jit(solution)/shard_map/reshape | solution.py:98
  1.6 0.5 copy.24
  2.1 1.1 %copy.25 = f32[64,1,1536]{2,1,0:T(1,128)} copy(f32[64,1,1536]{0,2,1:T(8,128)S(1)} %bitcast.22) | data formatting | bytes 786432 | tf_op jit(solution)/shard_map/all_to_all | solution.py:101
  3.2 16.6 %all-to-all-start = ((f32[64,1,1536]{2,1,0:T(1,128)}), f32[64,1,1536]{2,1,0:T(1,128)S(1)}, u32[]{:S(2)}, u32[]{:S(2)}) async-start(f32[64,1,1536]{2,1,0:T(1,128)} %copy.25), calls=%async_computation | async-start | bytes 786432 | tf_op jit(solution)/shard_map/all_to_all | solution.py:101
  19.8 0.1 reduce_sum.47
  20.0 0.1 broadcast_in_dim.24
  20.1 2.6 %multiply_add_fusion = f32[32,32,1024]{2,1,0:T(8,128)} fusion(f32[32,1024]{1,0:T(8,128)S(1)} %copy-done.5, f32[32,1024]{1,0:T(8,128)S(1)} %copy-done.3, f32[32,1024]{1,0:T(8,128)S(1)} %copy-done.4, f32[32,1024]{1,0:T(8,128)S(1)} %copy-done.2), kind=kLoop, calls=%fused_computation.3 | loop fusion | flops 3145728 | bytes 4718592 | tf_op jit(solution)/shard_map/add | solution.py:29
  22.7 14.1 %all-to-all-done = f32[64,1,1536]{2,1,0:T(1,128)S(1)} async-done(((f32[64,1,1536]{2,1,0:T(1,128)}), f32[64,1,1536]{2,1,0:T(1,128)S(1)}, u32[]{:S(2)}, u32[]{:S(2)}) %all-to-all-start) | async-done | bytes 393248 | tf_op jit(solution)/shard_map/all_to_all | solution.py:101
  36.8 0.6 broadcast_in_dim.31
  37.4 4.8 %all-to-all-start.1 = ((f32[8,1,48]{2,1,0:T(1,128)}), f32[8,1,48]{2,1,0:T(1,128)S(1)}, u32[]{:S(2)}, u32[]{:S(2)}) async-start(f32[8,1,48]{2,1,0:T(1,128)} %bitcast.3), calls=%async_computation.1 | async-start | bytes 8192 | tf_op jit(solution)/shard_map/all_to_all | solution.py:106
  42.2 4.5 %bitcast_select_fusion = f32[1024,1024]{1,0:T(8,128)} fusion(f32[32,32,1024]{2,1,0:T(8,128)} %multiply_add_fusion, f32[1024]{0:T(1024)S(1)} %fusion.40, pred[1024]{0:T(1024)(128)(4,1)S(1)} %iota_compare_fusion.3), kind=kLoop, calls=%fused_computation.2 | loop fusion | flops 1048576 | bytes 8393728 | tf_op jit(solution)/shard_map/jit(_where)/select_n | solution.py:34
  46.8 0.6 broadcast_in_dim.32
  47.4 4.9 %all-to-all-start.2 = ((f32[64,1,48]{2,1,0:T(1,128)}), f32[64,1,48]{2,1,0:T(1,128)S(1)}, u32[]{:S(2)}, u32[]{:S(2)}) async-start(f32[64,1,48]{2,1,0:T(1,128)} %broadcast_in_dim.32), calls=%async_computation.2 | async-start | bytes 65536 | tf_op jit(solution)/shard_map/all_to_all | solution.py:108
  52.4 1.3 %slice.78 = f32[512,512]{1,0:T(8,128)S(1)} slice(f32[1024,1024]{1,0:T(8,128)} %bitcast_select_fusion), slice={[0:512], [0:512]} | slice | bytes 2097152 | tf_op jit(solution)/shard_map/slice | solution.py:76
  53.7 1.0 %reshape.89 = f32[1024,96]{1,0:T(8,128)} reshape(f32[64,1536]{1,0:T(8,128)S(1)} %bitcast.23) | data formatting | bytes 786432 | tf_op jit(solution)/shard_map/reshape | solution.py:111
  54.8 9.3 %all-to-all-done.2 = f32[64,1,48]{2,1,0:T(1,128)S(1)} async-done(((f32[64,1,48]{2,1,0:T(1,128)}), f32[64,1,48]{2,1,0:T(1,128)S(1)}, u32[]{:S(2)}, u32[]{:S(2)}) %all-to-all-start.2) | async-done | bytes 12320 | tf_op jit(solution)/shard_map/all_to_all | solution.py:108
  64.1 0.5 broadcast.84
  64.6 0.7 reduce.6
  65.3 1.1 %reshape.92 = f32[64,16,3]{2,1,0:T(8,128)} reshape(f32[64,48]{1,0:T(8,128)S(1)} %reduce.6) | data formatting | bytes 24576 | tf_op jit(solution)/shard_map/sub | solution.py:112
  66.4 2.2 %sub.41 = f32[64,16,3,32]{3,2,1,0:T(4,128)S(1)} broadcast(f32[64,16,3]{2,1,0:T(8,128)} %reshape.92), dimensions={0,1,2} | broadcast | bytes 405504 | tf_op jit(solution)/shard_map/sub | solution.py:112
  68.6 1.5 %sub.42 = f32[1024,96]{1,0:T(8,128)} reshape(f32[64,16,3,32]{3,2,1,0:T(4,128)S(1)} %sub.41) | data formatting | bytes 786432 | tf_op jit(solution)/shard_map/sub | solution.py:112
  70.2 1.4 %reduce-precision_convert_fusion.1 = (bf16[1024,96]{1,0:T(8,128)(2,1)S(1)}, bf16[1024,96]{1,0:T(8,128)(2,1)S(1)}, bf16[1024,96]{1,0:T(8,128)(2,1)S(1)}) fusion(f32[1024,96]{1,0:T(8,128)} %reshape.89, f32[1024,96]{1,0:T(8,128)} %sub.42), kind=kLoop, calls=%fused_computation.26 | loop fusion | flops 786432 | bytes 1376256 | tf_op jit(solution)/shard_map/convert.3
  71.6 1.3 %fusion.1 = f32[1024,288]{0,1:T(8,128)S(1)} fusion(bf16[1024,96]{1,0:T(8,128)(2,1)S(1)} %get-tuple-element.23, bf16[1024,96]{1,0:T(8,128)(2,1)S(1)} %get-tuple-element.22, bf16[1024,96]{1,0:T(8,128)(2,1)S(1)} %get-tuple-element.21), kind=kOutput, calls=%fused_computation.8 | convolution fusion | flops 608894976 | bytes 1769472 | tf_op jit(solution)/shard_map/dot_general | solution.py:47
  72.9 0.1 broadcast_multiply_fusion
  73.1 0.7 copy-done
  73.7 4.5 %fusion.12 = f32[1024,192]{0,1:T(8,128)S(1)} fusion(f32[1024,1024]{1,0:T(8,128)S(1)} %copy-done, f32[1024,96]{0,1:T(8,128)S(1)} %get-tuple-element.19, f32[1024,96]{0,1:T(8,128)S(1)} %get-tuple-element.20), kind=kOutput, calls=%fused_computation.19 | convolution fusion | flops 2416115712 | bytes 5767168 | tf_op jit(solution)/shard_map/dot_general | solution.py:66
  78.3 0.1 fusion.35
  78.7 1.4 %fusion.3 = f32[513,128]{0,1:T(8,128)S(1)} fusion(f32[1,512]{1,0:T(1,128)S(1)} %copy-done.10, f32[512,512]{1,0:T(8,128)S(1)} %slice.78, f32[512,64]{0,1:T(8,128)S(1)} %get-tuple-element.28, f32[512,64]{0,1:T(8,128)S(1)} %get-tuple-element.27), kind=kOutput, calls=%fused_computation.10 | convolution fusion | flops 403767808 | bytes 1575424 | tf_op jit(solution)/shard_map/dot_general | solution.py:77
  80.2 0.1 slice_add_fusion.4
  80.3 0.3 reverse
  80.8 0.9 %fusion = f32[1024,96]{0,1:T(8,128)S(1)} fusion(s32[1024]{0:T(1024)S(1)} %iota_subtract_fusion, bf16[1024,32]{0,1:T(8,128)(2,1)S(1)} %get-tuple-element.30, bf16[1024,32]{0,1:T(8,128)(2,1)S(1)} %get-tuple-element.31, bf16[1024,32]{0,1:T(8,128)(2,1)S(1)} %get-tuple-element.29), kind=kOutput, calls=%fused_computation.7 | convolution fusion | flops 208207872 | bytes 593920 | tf_op jit(solution)/shard_map/dot_general | solution.py:47
  81.7 0.7 fusion.30
  (47 shorter events, 0.8 us)
Async XLA Ops:
  0.0 20.1 %copy-start.2 = (f32[32,1024]{1,0:T(8,128)S(1)}, f32[32,1024]{1,0:T(8,128)}, u32[]{:S(2)}) copy-start(f32[32,1024]{1,0:T(8,128)} %constant.57.clone) | copy-start | bytes 393220
  0.0 20.1 %copy-start.3 = (f32[32,1024]{1,0:T(8,128)S(1)}, f32[32,1024]{1,0:T(8,128)}, u32[]{:S(2)}) copy-start(f32[32,1024]{1,0:T(8,128)} %constant.58.clone) | copy-start | bytes 393220
  0.0 20.1 %copy-start.4 = (f32[32,1024]{1,0:T(8,128)S(1)}, f32[32,1024]{1,0:T(8,128)}, u32[]{:S(2)}) copy-start(f32[32,1024]{1,0:T(8,128)} %constant.59.clone) | copy-start | bytes 393220
  0.0 20.1 %copy-start.5 = (f32[32,1024]{1,0:T(8,128)S(1)}, f32[32,1024]{1,0:T(8,128)}, u32[]{:S(2)}) copy-start(f32[32,1024]{1,0:T(8,128)} %constant.60.clone) | copy-start | bytes 393220
  0.0 19.7 %copy-start.1 = (f32[16,3,2048]{2,0,1:T(8,128)S(1)}, f32[16,3,2048]{2,0,1:T(8,128)}, u32[]{:S(2)}) copy-start(f32[16,3,2048]{2,0,1:T(8,128)} %param.11) | copy-start | bytes 1179652
  3.2 33.6 %all-to-all-start = ((f32[64,1,1536]{2,1,0:T(1,128)}), f32[64,1,1536]{2,1,0:T(1,128)S(1)}, u32[]{:S(2)}, u32[]{:S(2)}) async-start(f32[64,1,1536]{2,1,0:T(1,128)} %copy.25), calls=%async_computation | async-start | bytes 786432 | tf_op jit(solution)/shard_map/all_to_all | solution.py:101
  37.4 9.3 %all-to-all-start.1 = ((f32[8,1,48]{2,1,0:T(1,128)}), f32[8,1,48]{2,1,0:T(1,128)S(1)}, u32[]{:S(2)}, u32[]{:S(2)}) async-start(f32[8,1,48]{2,1,0:T(1,128)} %bitcast.3), calls=%async_computation.1 | async-start | bytes 8192 | tf_op jit(solution)/shard_map/all_to_all | solution.py:106
  42.2 11.4 %copy-start.6 = (f32[513]{0:T(1024)S(1)}, f32[513]{0:T(1024)}, u32[]{:S(2)}) copy-start(f32[513]{0:T(1024)} %constant.70) | copy-start | bytes 6160
  47.4 16.7 %all-to-all-start.2 = ((f32[64,1,48]{2,1,0:T(1,128)}), f32[64,1,48]{2,1,0:T(1,128)S(1)}, u32[]{:S(2)}, u32[]{:S(2)}) async-start(f32[64,1,48]{2,1,0:T(1,128)} %broadcast_in_dim.32), calls=%async_computation.2 | async-start | bytes 65536 | tf_op jit(solution)/shard_map/all_to_all | solution.py:108
  70.2 2.7 %copy-start.9 = (f32[1024]{0:T(1024)S(1)}, f32[1024]{0:T(1024)}, u32[]{:S(2)}) copy-start(f32[1024]{0:T(1024)} %constant.61.clone) | copy-start | bytes 12292
  71.6 2.2 %copy-start = (f32[1024,1024]{1,0:T(8,128)S(1)}, f32[1024,1024]{1,0:T(8,128)}, u32[]{:S(2)}) copy-start(f32[1024,1024]{1,0:T(8,128)} %bitcast_select_fusion) | copy-start | bytes 12582916
  72.9 5.5 %copy-start.13 = (f32[512]{0:T(512)S(1)}, f32[512]{0:T(512)}, u32[]{:S(2)}) copy-start(f32[512]{0:T(512)} %constant.62.clone) | copy-start | bytes 6148
  73.0 5.7 %copy-start.11 = (f32[512]{0:T(512)S(1)}, f32[512]{0:T(512)}, u32[]{:S(2)}) copy-start(f32[512]{0:T(512)} %constant.63.clone) | copy-start | bytes 6148
  73.0 5.7 %copy-start.12 = (f32[512]{0:T(512)S(1)}, f32[512]{0:T(512)}, u32[]{:S(2)}) copy-start(f32[512]{0:T(512)} %constant.69) | copy-start | bytes 6148
  73.0 5.7 %copy-start.10 = (f32[1,512]{1,0:T(1,128)S(1)}, f32[1,512]{1,0:T(1,128)}, u32[]{:S(2)}) copy-start(f32[1,512]{1,0:T(1,128)} %constant.64.clone) | copy-start | bytes 6148
  73.7 6.4 %copy-start.8 = (f32[513]{0:T(1024)S(1)}, f32[513]{0:T(1024)}, u32[]{:S(2)}) copy-start(f32[513]{0:T(1024)} %constant.71) | copy-start | bytes 6160
  78.7 3.0 %copy-start.7 = (f32[1024]{0:T(1024)S(1)}, f32[1024]{0:T(1024)}, u32[]{:S(2)}) copy-start(f32[1024]{0:T(1024)} %constant.68) | copy-start | bytes 12292

commit v15 on v13

--- a/solution.py
+++ b/solution.py
@@ -71,15 +71,14 @@
     middle = jnp.sum((0.5 * (plus * plus + minus * minus)).reshape(3, count), axis=0) * (2.0 / (2 * length))
     weight = jnp.asarray((np.where(steps[:half] == 0, 1.0, 2.0) / (2 * length)).astype(np.float32))
     coef = (power * weight[:, None, None]).reshape(half, 2 * count)
-    sign_q = parity[:half]
-    coef = jnp.concatenate([coef, coef * sign_q[:, None]], axis=1)
-    table = jnp.concatenate([table_full[:half, :half], jnp.asarray(quarter_cos[None, :half])], axis=0)
-    folded = jnp.dot(table, coef, precision=lax.Precision.HIGHEST)
-    sign_m = parity[: half + 1, None]
-    quarter = jnp.asarray(quarter_cos[: half + 1, None])
-    near = folded[:, :count] + sign_m * folded[:, count : 2 * count] + middle[None, :] * quarter
-    far = folded[:, 2 * count : 3 * count] + sign_m * folded[:, 3 * count :] + middle[None, :] * quarter
-    corr = jnp.concatenate([near, jnp.flip(far[1:half], axis=0)], axis=0)
+    folded = lax.dot_general(
+        table_full[:half], coef, (((0,), (0,)), ((), ())), precision=lax.Precision.HIGHEST
+    )
+    corr = (
+        folded[:, :count]
+        + parity[:, None] * folded[:, count:]
+        + middle[None, :] * jnp.asarray(quarter_cos[:, None])
+    )
     window = (
         (frame[None, :] >= frame[:, None]).astype(jnp.float32)
         + (frame[None, :] <= (length - 1 - frame)[:, None]).astype(jnp.float32)

time: 58.9 us -> 59.9 us (1.017)
  local copies, waits for them, and re-layouts: 8.2 us -> 5.02 us
  matrix products: 8.12 us -> 9.73 us
  waiting for transfers between devices: 14.9 us -> 16.4 us
  other arithmetic: 6.26 us -> 7.37 us
    unnamed x30 -> x18, local copies, waits for them, and re-layouts: 3.07 us -> 0.79 us
    select_n x1, other arithmetic: 0.34 us -> 2.27 us  [spectral_table(): return jnp.where((row == rows)[:, None], both_quarters[None, :], table)]
    dot_general x1, matrix products: 1.41 us -> 3.02 us  [lag_table(): lax.dot_general(table_full[:half], coef, (((0,), (0,)), ((), ())), precis...]
    all_to_all x1, waiting for transfers between devices: 2.23 us -> 3.61 us  [per_device(): lax.all_to_all(spread, 'atoms', split_axis=0, concat_axis=0, tiled=True)]
    slice x2 -> x0, local copies, waits for them, and re-layouts: 0.9 us -> none  [the longest x1 0.81 us: lag_table(): corr = jnp.concatenate([near, jnp.flip(far[1:half], axis=0)], axis=0)]
  transfers between devices with their start and end apart: 2 -> 2, of which waited for: 2 -> 2; matrix products, arithmetic and copies ran while one was open for 8% -> 9% of each run, Pallas kernels for 0% -> 0%
where the time goes in v15:
time: 59.9 us; the launch traced here: 59.6 us
  starting transfers between devices  20.8 us (35%)
  waiting for transfers between devices  16.4 us (27%)
  matrix products  9.73 us (16%)
  other arithmetic  7.37 us (12%)
  local copies, waits for them, and re-layouts  5.02 us (8%)
    all_to_all x1, starting transfers between devices, per_device(): lax.all_to_all(outgoing, 'frames', split_axis=0, concat_axis=0, tiled=True)  16.5 us
    all_to_all x1, waiting for transfers between devices, per_device(): lax.all_to_all(outgoing, 'frames', split_axis=0, concat_axis=0, tiled=True)  12.8 us
    dot_general x1, matrix products, lag_table(): spectrum = jnp.dot(table_full, signed, precision=lax.Precision.HIGHEST)  4.53 us
    all_to_all x1, starting transfers between devices, per_device(): lax.all_to_all(spread, 'atoms', split_axis=0, concat_axis=0, tiled=True)  4.3 us
    all_to_all x1, waiting for transfers between devices, per_device(): lax.all_to_all(spread, 'atoms', split_axis=0, concat_axis=0, tiled=True)  3.61 us
    dot_general x1, matrix products, lag_table(): lax.dot_general(table_full[:half], coef, (((0,), (0,)), ((), ())), precis...  3.02 us
    select_n x1, other arithmetic, spectral_table(): return jnp.where((row == rows)[:, None], both_quarters[None, :], table)  2.27 us
    dot_general x2, matrix products, exact_product(): jnp.dot(matrix.astype(jnp.bfloat16), split_three(values), preferred_eleme...  2.18 us
  transfers between devices with their start and end apart: 2, of which 2 were waited for; matrix products, arithmetic and copies ran while one was open for 9% of the time, Pallas kernels for 0%

profile of v15, /device:TPU:16, one launch (start us, length us, event | category | flops | bytes accessed | tf_op | source)
XLA Modules:
  0.0 59.6 jit_solution(13078371611858278686)
XLA Ops:
  0.0 1.1 %reduce_sum.47 = f32[16,3]{0,1:T(4,128)S(1)} reduce(f32[16,3,2048]{2,0,1:T(8,128)} %param.10, f32[]{:T(128)} %constant.19.clone.1), dimensions={2}, to_apply=%region_0.0 | reduce | flops 98256 | bytes 393412 | tf_op jit(solution)/shard_map/reduce_sum | solution.py:96
  1.1 0.1 copy.23
  1.2 0.1 broadcast_in_dim.28
  1.3 0.6 %broadcast_in_dim.29 = f32[8,1,48]{2,1,0:T(1,128)} broadcast(f32[48]{0:T(128)S(1)} %broadcast_in_dim.28), dimensions={2} | broadcast | bytes 1728 | tf_op jit(solution)/shard_map/broadcast_in_dim | solution.py:97
  1.9 4.3 %all-to-all-start = ((f32[8,1,48]{2,1,0:T(1,128)}), f32[8,1,48]{2,1,0:T(1,128)S(1)}, u32[]{:S(2)}, u32[]{:S(2)}) async-start(f32[8,1,48]{2,1,0:T(1,128)} %broadcast_in_dim.29), calls=%async_computation | async-start | bytes 8192 | tf_op jit(solution)/shard_map/all_to_all | solution.py:98
  6.2 1.5 %reshape.83 = f32[16,3,64,32]{3,2,0,1:T(8,128)S(1)} reshape(f32[16,3,2048]{2,0,1:T(8,128)} %param.10) | data formatting | bytes 786432 | tf_op jit(solution)/shard_map/reshape | solution.py:101
  7.7 0.0 copy-start.1
  7.7 0.0 copy-start.2
  7.8 0.0 copy-start.3
  7.8 3.6 %all-to-all-done = f32[8,1,48]{2,1,0:T(1,128)S(1)} async-done(((f32[8,1,48]{2,1,0:T(1,128)}), f32[8,1,48]{2,1,0:T(1,128)S(1)}, u32[]{:S(2)}, u32[]{:S(2)}) %all-to-all-start) | async-done | bytes 1568 | tf_op jit(solution)/shard_map/all_to_all | solution.py:98
  11.4 0.1 div.18
  11.5 0.1 copy.25
  11.6 0.2 subtract_bitcast_fusion
  11.8 0.5 copy.26
  12.2 1.1 %copy.27 = f32[64,1,1536]{2,1,0:T(1,128)} copy(f32[64,1,1536]{0,2,1:T(8,128)S(1)} %bitcast.17) | data formatting | bytes 786432 | tf_op jit(solution)/shard_map/all_to_all | solution.py:106
  13.3 16.5 %all-to-all-start.1 = ((f32[64,1,1536]{2,1,0:T(1,128)}), f32[64,1,1536]{2,1,0:T(1,128)S(1)}, u32[]{:S(2)}, u32[]{:S(2)}) async-start(f32[64,1,1536]{2,1,0:T(1,128)} %copy.27), calls=%async_computation.1 | async-start | bytes 786432 | tf_op jit(solution)/shard_map/all_to_all | solution.py:106
  29.8 1.5 %multiply_add_fusion = f32[32,32,1024]{2,1,0:T(8,128)S(1)} fusion(f32[32,1024]{1,0:T(8,128)} %constant.58.clone, f32[32,1024]{1,0:T(8,128)S(1)} %copy-done.2, f32[32,1024]{1,0:T(8,128)S(1)} %copy-done.3, f32[32,1024]{1,0:T(8,128)S(1)} %copy-done.1), kind=kLoop, calls=%fused_computation.3 | loop fusion | flops 3145728 | bytes 4718592 | tf_op jit(solution)/shard_map/add | solution.py:29
  31.4 2.3 %bitcast_select_fusion = f32[1024,1024]{1,0:T(8,128)} fusion(f32[32,32,1024]{2,1,0:T(8,128)S(1)} %multiply_add_fusion, f32[1024]{0:T(1024)S(1)} %fusion.36, pred[1024]{0:T(1024)(128)(4,1)S(1)} %iota_compare_fusion.3), kind=kLoop, calls=%fused_computation.2 | loop fusion | flops 1048576 | bytes 8393728 | tf_op jit(solution)/shard_map/jit(_where)/select_n | solution.py:34
  33.6 12.8 %all-to-all-done.1 = f32[64,1,1536]{2,1,0:T(1,128)S(1)} async-done(((f32[64,1,1536]{2,1,0:T(1,128)}), f32[64,1,1536]{2,1,0:T(1,128)S(1)}, u32[]{:S(2)}, u32[]{:S(2)}) %all-to-all-start.1) | async-done | bytes 393248 | tf_op jit(solution)/shard_map/all_to_all | solution.py:106
  46.4 0.9 %reduce.1 = f32[64,1536]{1,0:T(8,128)S(1)} reduce(f32[64,1,1536]{2,1,0:T(1,128)S(1)} %all-to-all-done.1, f32[]{:T(128)} %constant.67), dimensions={1}, to_apply=%all_to_all.12.reduce_sub_computation | reduce | bytes 786436 | tf_op jit(solution)/shard_map/all_to_all | solution.py:106
  47.3 0.2 reshape.85
  47.5 0.1 reduce-precision_convert_fusion.1
  47.7 1.3 %fusion.1 = f32[1024,288]{0,1:T(8,128)S(1)} fusion(bf16[1024,96]{1,0:T(8,128)(2,1)S(1)} %get-tuple-element.18, bf16[1024,96]{1,0:T(8,128)(2,1)S(1)} %get-tuple-element.19, bf16[1024,96]{1,0:T(8,128)(2,1)S(1)} %get-tuple-element.17), kind=kOutput, calls=%fused_computation.8 | convolution fusion | flops 608894976 | bytes 1769472 | tf_op jit(solution)/shard_map/dot_general | solution.py:47
  49.0 0.1 fusion.40
  49.1 0.7 %copy-done = f32[1024,1024]{1,0:T(8,128)S(1)} copy-done((f32[1024,1024]{1,0:T(8,128)S(1)}, f32[1024,1024]{1,0:T(8,128)}, u32[]{:S(2)}) %copy-start) | copy-done | bytes 4194328
  49.9 4.5 %fusion.10 = f32[1024,192]{0,1:T(8,128)S(1)} fusion(f32[1024,1024]{1,0:T(8,128)S(1)} %copy-done, f32[1024,96]{0,1:T(8,128)S(1)} %broadcast_multiply_fusion, f32[1024,96]{0,1:T(8,128)S(1)} %get-tuple-element.16), kind=kOutput, calls=%fused_computation.18 | convolution fusion | flops 2416115712 | bytes 5767168 | tf_op jit(solution)/shard_map/dot_general | solution.py:66
  54.4 0.1 fusion.31
  54.5 0.1 fusion.16
  54.7 3.0 %fusion.2 = f32[1024,64]{0,1:T(8,128)S(1)} fusion(f32[512,64]{0,1:T(8,128)S(1)} %bitcast_multiply_fusion, f32[1024,1024]{1,0:T(8,128)} %bitcast_select_fusion), kind=kOutput, calls=%fused_computation.9 | convolution fusion | flops 402653184 | bytes 2490368 | tf_op jit(solution)/shard_map/dot_general | solution.py:74
  57.8 0.1 mul.156
  57.9 0.9 %fusion = f32[1024,96]{0,1:T(8,128)S(1)} fusion(s32[1024]{0:T(1024)S(1)} %iota_subtract_fusion, bf16[1024,32]{0,1:T(8,128)(2,1)S(1)} %get-tuple-element.21, bf16[1024,32]{0,1:T(8,128)(2,1)S(1)} %get-tuple-element.22, bf16[1024,32]{0,1:T(8,128)(2,1)S(1)} %get-tuple-element.20), kind=kOutput, calls=%fused_computation.7 | convolution fusion | flops 208207872 | bytes 593920 | tf_op jit(solution)/shard_map/dot_general | solution.py:47
  58.8 0.8 %fusion.28 = f32[32,1024]{1,0:T(8,128)} fusion(f32[1024,64]{0,1:T(8,128)S(1)} %fusion.2, f32[1024,96]{0,1:T(8,128)S(1)} %fusion, f32[1024]{0:T(1024)S(1)} %copy-done.5, f32[1024]{0:T(1024)S(1)} %copy-done.6, f32[32]{0:T(128)S(1)} %broadcast_multiply_fusion.1, f32[1024]{0:T(1024)S(1)} %copy-done.4), kind=kLoop, calls=%fused_computation.50 | loop fusion | flops 294912 | bytes 798848 | tf_op jit(solution)/shard_map/transpose | solution.py:88
  (26 shorter events, 0.2 us)
Async XLA Ops:
  1.9 9.5 %all-to-all-start = ((f32[8,1,48]{2,1,0:T(1,128)}), f32[8,1,48]{2,1,0:T(1,128)S(1)}, u32[]{:S(2)}, u32[]{:S(2)}) async-start(f32[8,1,48]{2,1,0:T(1,128)} %broadcast_in_dim.29), calls=%async_computation | async-start | bytes 8192 | tf_op jit(solution)/shard_map/all_to_all | solution.py:98
  7.7 22.0 %copy-start.1 = (f32[32,1024]{1,0:T(8,128)S(1)}, f32[32,1024]{1,0:T(8,128)}, u32[]{:S(2)}) copy-start(f32[32,1024]{1,0:T(8,128)} %constant.55.clone) | copy-start | bytes 393220
  7.7 22.0 %copy-start.2 = (f32[32,1024]{1,0:T(8,128)S(1)}, f32[32,1024]{1,0:T(8,128)}, u32[]{:S(2)}) copy-start(f32[32,1024]{1,0:T(8,128)} %constant.56.clone) | copy-start | bytes 393220
  7.8 22.0 %copy-start.3 = (f32[32,1024]{1,0:T(8,128)S(1)}, f32[32,1024]{1,0:T(8,128)}, u32[]{:S(2)}) copy-start(f32[32,1024]{1,0:T(8,128)} %constant.57.clone) | copy-start | bytes 393220
  13.3 33.1 %all-to-all-start.1 = ((f32[64,1,1536]{2,1,0:T(1,128)}), f32[64,1,1536]{2,1,0:T(1,128)S(1)}, u32[]{:S(2)}, u32[]{:S(2)}) async-start(f32[64,1,1536]{2,1,0:T(1,128)} %copy.27), calls=%async_computation.1 | async-start | bytes 786432 | tf_op jit(solution)/shard_map/all_to_all | solution.py:106
  47.5 1.6 %copy-start.4 = (f32[1024]{0:T(1024)S(1)}, f32[1024]{0:T(1024)}, u32[]{:S(2)}) copy-start(f32[1024]{0:T(1024)} %constant.59.clone) | copy-start | bytes 12292
  47.7 2.2 %copy-start = (f32[1024,1024]{1,0:T(8,128)S(1)}, f32[1024,1024]{1,0:T(8,128)}, u32[]{:S(2)}) copy-start(f32[1024,1024]{1,0:T(8,128)} %bitcast_select_fusion) | copy-start | bytes 12582916
  49.0 5.5 %copy-start.8 = (f32[512]{0:T(512)S(1)}, f32[512]{0:T(512)}, u32[]{:S(2)}) copy-start(f32[512]{0:T(512)} %constant.60.clone) | copy-start | bytes 6148
  49.1 5.6 %copy-start.7 = (f32[512]{0:T(512)S(1)}, f32[512]{0:T(512)}, u32[]{:S(2)}) copy-start(f32[512]{0:T(512)} %constant.61.clone) | copy-start | bytes 6148
  54.6 4.2 %copy-start.5 = (f32[1024]{0:T(1024)S(1)}, f32[1024]{0:T(1024)}, u32[]{:S(2)}) copy-start(f32[1024]{0:T(1024)} %constant.65) | copy-start | bytes 12292
  54.7 4.2 %copy-start.6 = (f32[1024]{0:T(1024)S(1)}, f32[1024]{0:T(1024)}, u32[]{:S(2)}) copy-start(f32[1024]{0:T(1024)} %constant.66) | copy-start | bytes 12292

commit v16 on v13

--- a/solution.py
+++ b/solution.py
@@ -97,11 +97,13 @@
     partial_sum = jnp.sum(displacements, axis=2).reshape(1, local_frames * 3)
     spread = jnp.broadcast_to(partial_sum, (members, local_frames * 3))
     gathered = lax.all_to_all(spread, "atoms", split_axis=0, concat_axis=0, tiled=True)
-    summed = jnp.sum(gathered, axis=0).reshape(local_frames, 3)
     count = atom_count // groups
     blocks = jnp.transpose(displacements.reshape(local_frames, 3, groups, count), (2, 0, 1, 3))
-    outgoing = blocks - (summed / atom_total)[None, :, :, None]
-    outgoing = outgoing.reshape(groups, local_frames * 3 * count)
+    blocks = blocks.reshape(groups, local_frames * 3 * count)
+    gathered, blocks = lax.optimization_barrier((gathered, blocks))
+    summed = jnp.sum(gathered, axis=0).reshape(local_frames, 3)
+    drift_row = jnp.broadcast_to((summed / atom_total)[:, :, None], (local_frames, 3, count))
+    outgoing = blocks - drift_row.reshape(1, local_frames * 3 * count)
     length = local_frames * groups
     *parts, outgoing = lax.optimization_barrier((*table_parts(length, length // 2), outgoing))
     moved = lax.all_to_all(outgoing, "frames", split_axis=0, concat_axis=0, tiled=True)

time: 58.9 us -> 58.7 us (level)
  waiting for transfers between devices: 14.9 us -> 16.6 us
  other arithmetic: 6.26 us -> 4.94 us
  local copies, waits for them, and re-layouts: 8.2 us -> 7.56 us
    add x1, other arithmetic: 1.54 us -> 0.64 us  [spectral_table(): first[:, None, :] * cos_lo[None, :, :]]
    all_to_all x1, waiting for transfers between devices: 12.6 us -> 13.5 us  [per_device(): lax.all_to_all(outgoing, 'frames', split_axis=0, concat_axis=0, tiled=True)]
    all_to_all x1, waiting for transfers between devices: 2.23 us -> 3.1 us  [per_device(): lax.all_to_all(spread, 'atoms', split_axis=0, concat_axis=0, tiled=True)]
    slice x1, local copies, waits for them, and re-layouts: 0.81 us -> 0.07 us  [lag_table(): corr = jnp.concatenate([near, jnp.flip(far[1:half], axis=0)], axis=0)]
  transfers between devices with their start and end apart: 2 -> 2, of which waited for: 2 -> 2; matrix products, arithmetic and copies ran while one was open for 8% -> 5% of each run, Pallas kernels for 0% -> 0%
where the time goes in v16:
time: 58.7 us; the launch traced here: 58.4 us
  starting transfers between devices  20.8 us (35%)
  waiting for transfers between devices  16.6 us (28%)
  matrix products  8.11 us (14%)
  local copies, waits for them, and re-layouts  7.56 us (13%)
  other arithmetic  4.94 us (8%)
    all_to_all x1, starting transfers between devices, per_device(): lax.all_to_all(outgoing, 'frames', split_axis=0, concat_axis=0, tiled=True)  16.5 us
    all_to_all x1, waiting for transfers between devices, per_device(): lax.all_to_all(outgoing, 'frames', split_axis=0, concat_axis=0, tiled=True)  13.5 us
    dot_general x1, matrix products, lag_table(): spectrum = jnp.dot(table_full, signed, precision=lax.Precision.HIGHEST)  4.53 us
    all_to_all x1, starting transfers between devices, per_device(): lax.all_to_all(spread, 'atoms', split_axis=0, concat_axis=0, tiled=True)  4.3 us
    all_to_all x1, waiting for transfers between devices, per_device(): lax.all_to_all(spread, 'atoms', split_axis=0, concat_axis=0, tiled=True)  3.1 us
    unnamed x30, local copies, waits for them, and re-layouts  3.07 us
    dot_general x2, matrix products, exact_product(): jnp.dot(matrix.astype(jnp.bfloat16), split_three(values), preferred_eleme...  2.18 us
    reshape x1, local copies, waits for them, and re-layouts, per_device(): displacements.reshape(local_frames, 3, groups, count)  1.51 us
  transfers between devices with their start and end apart: 2, of which 2 were waited for; matrix products, arithmetic and copies ran while one was open for 5% of the time, Pallas kernels for 0%

profile of v16, /device:TPU:16, one launch (start us, length us, event | category | flops | bytes accessed | tf_op | source)
XLA Modules:
  0.0 58.4 jit_solution(17861075707968023783)
XLA Ops:
  0.0 1.2 %reduce_sum.47 = f32[16,3]{0,1:T(4,128)S(1)} reduce(f32[16,3,2048]{2,0,1:T(8,128)} %param.11, f32[]{:T(128)} %constant.20.clone.1), dimensions={2}, to_apply=%region_0.0 | reduce | flops 98256 | bytes 393412 | tf_op jit(solution)/shard_map/reduce_sum | solution.py:97
  1.2 0.1 copy.22
  1.3 0.1 broadcast_in_dim.24
  1.4 0.6 %broadcast_in_dim.31 = f32[8,1,48]{2,1,0:T(1,128)} broadcast(f32[48]{0:T(128)S(1)} %broadcast_in_dim.24), dimensions={2} | broadcast | bytes 1728 | tf_op jit(solution)/shard_map/broadcast_in_dim | solution.py:98
  2.0 4.3 %all-to-all-start = ((f32[8,1,48]{2,1,0:T(1,128)}), f32[8,1,48]{2,1,0:T(1,128)S(1)}, u32[]{:S(2)}, u32[]{:S(2)}) async-start(f32[8,1,48]{2,1,0:T(1,128)} %broadcast_in_dim.31), calls=%async_computation | async-start | bytes 8192 | tf_op jit(solution)/shard_map/all_to_all | solution.py:99
  6.3 1.5 %reshape.87 = f32[16,3,64,32]{3,2,0,1:T(8,128)S(1)} reshape(f32[16,3,2048]{2,0,1:T(8,128)} %param.11) | data formatting | bytes 786432 | tf_op jit(solution)/shard_map/reshape | solution.py:101
  7.8 0.5 copy.23
  8.4 3.1 %all-to-all-done = f32[8,1,48]{2,1,0:T(1,128)S(1)} async-done(((f32[8,1,48]{2,1,0:T(1,128)}), f32[8,1,48]{2,1,0:T(1,128)S(1)}, u32[]{:S(2)}, u32[]{:S(2)}) %all-to-all-start) | async-done | bytes 1568 | tf_op jit(solution)/shard_map/all_to_all | solution.py:99
  11.5 0.1 div.18
  11.7 0.1 sub.37
  11.8 0.3 broadcast_subtract_fusion
  12.0 1.1 %copy.24 = f32[64,1,1536]{2,1,0:T(1,128)} copy(f32[64,1,1536]{0,2,1:T(8,128)S(1)} %bitcast.19) | data formatting | bytes 786432 | tf_op jit(solution)/shard_map/all_to_all | solution.py:109
  13.1 16.5 %all-to-all-start.1 = ((f32[64,1,1536]{2,1,0:T(1,128)}), f32[64,1,1536]{2,1,0:T(1,128)S(1)}, u32[]{:S(2)}, u32[]{:S(2)}) async-start(f32[64,1,1536]{2,1,0:T(1,128)} %copy.24), calls=%async_computation.1 | async-start | bytes 786432 | tf_op jit(solution)/shard_map/all_to_all | solution.py:109
  29.6 0.6 %multiply_add_fusion = f32[32,32,1024]{2,1,0:T(8,128)S(1)} fusion(f32[32,1024]{1,0:T(8,128)S(1)} %copy-done.5, f32[32,1024]{1,0:T(8,128)S(1)} %copy-done.3, f32[32,1024]{1,0:T(8,128)S(1)} %copy-done.4, f32[32,1024]{1,0:T(8,128)S(1)} %copy-done.2), kind=kLoop, calls=%fused_computation.3 | loop fusion | flops 3145728 | bytes 4718592 | tf_op jit(solution)/shard_map/add | solution.py:29
  30.3 0.3 bitcast_select_fusion
  30.7 1.9 %copy-done = f32[1024,1024]{1,0:T(8,128)} copy-done((f32[1024,1024]{1,0:T(8,128)}, f32[1024,1024]{1,0:T(8,128)S(1)}, u32[]{:S(2)}) %copy-start) | copy-done | bytes 4194328
  32.6 0.1 slice.78
  32.7 13.5 %all-to-all-done.1 = f32[64,1,1536]{2,1,0:T(1,128)S(1)} async-done(((f32[64,1,1536]{2,1,0:T(1,128)}), f32[64,1,1536]{2,1,0:T(1,128)S(1)}, u32[]{:S(2)}, u32[]{:S(2)}) %all-to-all-start.1) | async-done | bytes 393248 | tf_op jit(solution)/shard_map/all_to_all | solution.py:109
  46.2 0.9 %reduce = f32[64,1536]{1,0:T(8,128)S(1)} reduce(f32[64,1,1536]{2,1,0:T(1,128)S(1)} %all-to-all-done.1, f32[]{:T(128)} %constant.72), dimensions={1}, to_apply=%all_to_all.15.reduce_sub_computation | reduce | bytes 786436 | tf_op jit(solution)/shard_map/all_to_all | solution.py:109
  47.2 0.2 reshape.89
  47.3 0.1 reduce-precision_convert_fusion.1
  47.5 1.3 %fusion.1 = f32[1024,288]{0,1:T(8,128)S(1)} fusion(bf16[1024,96]{1,0:T(8,128)(2,1)S(1)} %get-tuple-element.22, bf16[1024,96]{1,0:T(8,128)(2,1)S(1)} %get-tuple-element.23, bf16[1024,96]{1,0:T(8,128)(2,1)S(1)} %get-tuple-element.21), kind=kOutput, calls=%fused_computation.8 | convolution fusion | flops 608894976 | bytes 1769472 | tf_op jit(solution)/shard_map/dot_general | solution.py:47
  48.8 0.1 broadcast_multiply_fusion
  49.0 0.7 %copy-done.1 = f32[1024,1024]{1,0:T(8,128)S(1)} copy-done((f32[1024,1024]{1,0:T(8,128)S(1)}, f32[1024,1024]{1,0:T(8,128)}, u32[]{:S(2)}) %copy-start.1) | copy-done | bytes 4194328
  49.7 4.5 %fusion.12 = f32[1024,192]{0,1:T(8,128)S(1)} fusion(f32[1024,1024]{1,0:T(8,128)S(1)} %copy-done.1, f32[1024,96]{0,1:T(8,128)S(1)} %get-tuple-element.19, f32[1024,96]{0,1:T(8,128)S(1)} %get-tuple-element.20), kind=kOutput, calls=%fused_computation.19 | convolution fusion | flops 2416115712 | bytes 5767168 | tf_op jit(solution)/shard_map/dot_general | solution.py:66
  54.2 0.1 fusion.35
  54.6 1.4 %fusion.3 = f32[513,128]{0,1:T(8,128)S(1)} fusion(f32[1,512]{1,0:T(1,128)S(1)} %copy-done.10, f32[512,512]{1,0:T(8,128)S(1)} %slice.78, f32[512,64]{0,1:T(8,128)S(1)} %get-tuple-element.28, f32[512,64]{0,1:T(8,128)S(1)} %get-tuple-element.27), kind=kOutput, calls=%fused_computation.10 | convolution fusion | flops 403767808 | bytes 1575424 | tf_op jit(solution)/shard_map/dot_general | solution.py:77
  56.1 0.1 fusion.32
  56.1 0.1 slice_add_fusion.4
  56.3 0.3 reverse
  56.7 0.9 %fusion = f32[1024,96]{0,1:T(8,128)S(1)} fusion(s32[1024]{0:T(1024)S(1)} %iota_subtract_fusion, bf16[1024,32]{0,1:T(8,128)(2,1)S(1)} %get-tuple-element.30, bf16[1024,32]{0,1:T(8,128)(2,1)S(1)} %get-tuple-element.31, bf16[1024,32]{0,1:T(8,128)(2,1)S(1)} %get-tuple-element.29), kind=kOutput, calls=%fused_computation.7 | convolution fusion | flops 208207872 | bytes 593920 | tf_op jit(solution)/shard_map/dot_general | solution.py:47
  57.7 0.7 %fusion.30 = f32[32,1024]{1,0:T(8,128)} fusion(f32[1024,96]{0,1:T(8,128)S(1)} %fusion, f32[511,32]{0,1:T(8,128)S(1)} %slice.138, f32[513,32]{0,1:T(8,128)S(1)} %get-tuple-element.24, f32[1024]{0:T(1024)S(1)} %copy-done.7), kind=kLoop, calls=%fused_computation.52 | loop fusion | flops 196608 | bytes 659456 | tf_op jit(solution)/shard_map/transpose | solution.py:89
  (43 shorter events, 0.7 us)
Async XLA Ops:
  0.0 8.3 %copy-start.6 = (f32[513]{0:T(1024)S(1)}, f32[513]{0:T(1024)}, u32[]{:S(2)}) copy-start(f32[513]{0:T(1024)} %constant.70) | copy-start | bytes 6160
  0.0 29.6 %copy-start.2 = (f32[32,1024]{1,0:T(8,128)S(1)}, f32[32,1024]{1,0:T(8,128)}, u32[]{:S(2)}) copy-start(f32[32,1024]{1,0:T(8,128)} %constant.57.clone) | copy-start | bytes 393220
  0.0 29.6 %copy-start.3 = (f32[32,1024]{1,0:T(8,128)S(1)}, f32[32,1024]{1,0:T(8,128)}, u32[]{:S(2)}) copy-start(f32[32,1024]{1,0:T(8,128)} %constant.58.clone) | copy-start | bytes 393220
  0.0 29.6 %copy-start.4 = (f32[32,1024]{1,0:T(8,128)S(1)}, f32[32,1024]{1,0:T(8,128)}, u32[]{:S(2)}) copy-start(f32[32,1024]{1,0:T(8,128)} %constant.59.clone) | copy-start | bytes 393220
  0.0 29.6 %copy-start.5 = (f32[32,1024]{1,0:T(8,128)S(1)}, f32[32,1024]{1,0:T(8,128)}, u32[]{:S(2)}) copy-start(f32[32,1024]{1,0:T(8,128)} %constant.60.clone) | copy-start | bytes 393220
  2.0 9.5 %all-to-all-start = ((f32[8,1,48]{2,1,0:T(1,128)}), f32[8,1,48]{2,1,0:T(1,128)S(1)}, u32[]{:S(2)}, u32[]{:S(2)}) async-start(f32[8,1,48]{2,1,0:T(1,128)} %broadcast_in_dim.31), calls=%async_computation | async-start | bytes 8192 | tf_op jit(solution)/shard_map/all_to_all | solution.py:99
  13.1 33.1 %all-to-all-start.1 = ((f32[64,1,1536]{2,1,0:T(1,128)}), f32[64,1,1536]{2,1,0:T(1,128)S(1)}, u32[]{:S(2)}, u32[]{:S(2)}) async-start(f32[64,1,1536]{2,1,0:T(1,128)} %copy.24), calls=%async_computation.1 | async-start | bytes 786432 | tf_op jit(solution)/shard_map/all_to_all | solution.py:109
  30.6 1.9 %copy-start = (f32[1024,1024]{1,0:T(8,128)}, f32[1024,1024]{1,0:T(8,128)S(1)}, u32[]{:S(2)}) copy-start(f32[1024,1024]{1,0:T(8,128)S(1)} %bitcast_select_fusion) | copy-start | bytes 12582916
  32.7 16.1 %copy-start.9 = (f32[1024]{0:T(1024)S(1)}, f32[1024]{0:T(1024)}, u32[]{:S(2)}) copy-start(f32[1024]{0:T(1024)} %constant.61.clone) | copy-start | bytes 12292
  47.5 2.2 %copy-start.1 = (f32[1024,1024]{1,0:T(8,128)S(1)}, f32[1024,1024]{1,0:T(8,128)}, u32[]{:S(2)}) copy-start(f32[1024,1024]{1,0:T(8,128)} %copy-done) | copy-start | bytes 12582916
  48.8 5.5 %copy-start.13 = (f32[512]{0:T(512)S(1)}, f32[512]{0:T(512)}, u32[]{:S(2)}) copy-start(f32[512]{0:T(512)} %constant.62.clone) | copy-start | bytes 6148
  48.9 5.7 %copy-start.11 = (f32[512]{0:T(512)S(1)}, f32[512]{0:T(512)}, u32[]{:S(2)}) copy-start(f32[512]{0:T(512)} %constant.63.clone) | copy-start | bytes 6148
  48.9 5.7 %copy-start.12 = (f32[512]{0:T(512)S(1)}, f32[512]{0:T(512)}, u32[]{:S(2)}) copy-start(f32[512]{0:T(512)} %constant.69) | copy-start | bytes 6148
  49.0 5.7 %copy-start.10 = (f32[1,512]{1,0:T(1,128)S(1)}, f32[1,512]{1,0:T(1,128)}, u32[]{:S(2)}) copy-start(f32[1,512]{1,0:T(1,128)} %constant.64.clone) | copy-start | bytes 6148
  49.7 6.4 %copy-start.8 = (f32[513]{0:T(1024)S(1)}, f32[513]{0:T(1024)}, u32[]{:S(2)}) copy-start(f32[513]{0:T(1024)} %constant.71) | copy-start | bytes 6160
  54.6 3.0 %copy-start.7 = (f32[1024]{0:T(1024)S(1)}, f32[1024]{0:T(1024)}, u32[]{:S(2)}) copy-start(f32[1024]{0:T(1024)} %constant.68) | copy-start | bytes 12292

commit v17 on v16

--- a/solution.py
+++ b/solution.py
@@ -84,9 +84,13 @@
         (frame[None, :] >= frame[:, None]).astype(jnp.float32)
         + (frame[None, :] <= (length - 1 - frame)[:, None]).astype(jnp.float32)
     )
-    numer = exact_product(window, squares) - 2.0 * corr
+    parts_t = lax.dot_general(
+        split_three(squares), window.astype(jnp.bfloat16), (((0,), (1,)), ((), ())),
+        preferred_element_type=jnp.float32,
+    )
+    spans = parts_t[:count] + parts_t[count : 2 * count] + parts_t[2 * count :]
     counts = jnp.asarray((length - steps).astype(np.float32))
-    return jnp.transpose(numer / counts[:, None])
+    return (spans - 2.0 * jnp.transpose(corr)) / counts[None, :]
 
 
 def per_device(displacements):

time: 58.7 us -> 58.7 us (level)
    dot_general x2 -> x1, matrix products: 2.18 us -> 1.28 us  [exact_product(): jnp.dot(matrix.astype(jnp.bfloat16), split_three(values), preferred_eleme...]
    dot_general x0 -> x1, matrix products: none -> 0.9 us  [lag_table(): lax.dot_general(split_three(squares), window.astype(jnp.bfloat16), (((0,)...]
    div x0 -> x1, other arithmetic: none -> 0.75 us  [lag_table(): return (spans - 2.0 * jnp.transpose(corr)) / counts[None, :]]
    transpose x1 -> x0, other arithmetic: 0.75 us -> none  [lag_table(): return jnp.transpose(numer / counts[:, None])]
where the time goes in v17:
time: 58.7 us; the launch traced here: 58.4 us
  starting transfers between devices  20.8 us (35%)
  waiting for transfers between devices  16.6 us (28%)
  matrix products  8.11 us (14%)
  local copies, waits for them, and re-layouts  7.56 us (13%)
  other arithmetic  4.94 us (8%)
    all_to_all x1, starting transfers between devices, per_device(): lax.all_to_all(outgoing, 'frames', split_axis=0, concat_axis=0, tiled=True)  16.5 us
    all_to_all x1, waiting for transfers between devices, per_device(): lax.all_to_all(outgoing, 'frames', split_axis=0, concat_axis=0, tiled=True)  13.5 us
    dot_general x1, matrix products, lag_table(): spectrum = jnp.dot(table_full, signed, precision=lax.Precision.HIGHEST)  4.53 us
    all_to_all x1, starting transfers between devices, per_device(): lax.all_to_all(spread, 'atoms', split_axis=0, concat_axis=0, tiled=True)  4.3 us
    all_to_all x1, waiting for transfers between devices, per_device(): lax.all_to_all(spread, 'atoms', split_axis=0, concat_axis=0, tiled=True)  3.1 us
    unnamed x30, local copies, waits for them, and re-layouts  3.07 us
    reshape x1, local copies, waits for them, and re-layouts, per_device(): displacements.reshape(local_frames, 3, groups, count)  1.51 us
    dot_general x1, matrix products, lag_table(): folded = jnp.dot(table, coef, precision=lax.Precision.HIGHEST)  1.4 us
  transfers between devices with their start and end apart: 2, of which 2 were waited for; matrix products, arithmetic and copies ran while one was open for 5% of the time, Pallas kernels for 0%

profile of v17, /device:TPU:16, one launch (start us, length us, event | category | flops | bytes accessed | tf_op | source)
XLA Modules:
  0.0 58.4 jit_solution(18272112475821718568)
XLA Ops:
  0.0 1.2 %reduce_sum.47 = f32[16,3]{0,1:T(4,128)S(1)} reduce(f32[16,3,2048]{2,0,1:T(8,128)} %param.11, f32[]{:T(128)} %constant.23.clone.1), dimensions={2}, to_apply=%region_0.0 | reduce | flops 98256 | bytes 393412 | tf_op jit(solution)/shard_map/reduce_sum | solution.py:101
  1.2 0.1 copy.22
  1.3 0.1 broadcast_in_dim.24
  1.4 0.6 %broadcast_in_dim.31 = f32[8,1,48]{2,1,0:T(1,128)} broadcast(f32[48]{0:T(128)S(1)} %broadcast_in_dim.24), dimensions={2} | broadcast | bytes 1728 | tf_op jit(solution)/shard_map/broadcast_in_dim | solution.py:102
  2.0 4.3 %all-to-all-start = ((f32[8,1,48]{2,1,0:T(1,128)}), f32[8,1,48]{2,1,0:T(1,128)S(1)}, u32[]{:S(2)}, u32[]{:S(2)}) async-start(f32[8,1,48]{2,1,0:T(1,128)} %broadcast_in_dim.31), calls=%async_computation | async-start | bytes 8192 | tf_op jit(solution)/shard_map/all_to_all | solution.py:103
  6.3 1.5 %reshape.87 = f32[16,3,64,32]{3,2,0,1:T(8,128)S(1)} reshape(f32[16,3,2048]{2,0,1:T(8,128)} %param.11) | data formatting | bytes 786432 | tf_op jit(solution)/shard_map/reshape | solution.py:105
  7.8 0.5 copy.23
  8.4 3.1 %all-to-all-done = f32[8,1,48]{2,1,0:T(1,128)S(1)} async-done(((f32[8,1,48]{2,1,0:T(1,128)}), f32[8,1,48]{2,1,0:T(1,128)S(1)}, u32[]{:S(2)}, u32[]{:S(2)}) %all-to-all-start) | async-done | bytes 1568 | tf_op jit(solution)/shard_map/all_to_all | solution.py:103
  11.5 0.1 div.18
  11.7 0.1 sub.35
  11.8 0.3 broadcast_subtract_fusion
  12.0 1.1 %copy.24 = f32[64,1,1536]{2,1,0:T(1,128)} copy(f32[64,1,1536]{0,2,1:T(8,128)S(1)} %bitcast.21) | data formatting | bytes 786432 | tf_op jit(solution)/shard_map/all_to_all | solution.py:113
  13.1 16.5 %all-to-all-start.1 = ((f32[64,1,1536]{2,1,0:T(1,128)}), f32[64,1,1536]{2,1,0:T(1,128)S(1)}, u32[]{:S(2)}, u32[]{:S(2)}) async-start(f32[64,1,1536]{2,1,0:T(1,128)} %copy.24), calls=%async_computation.1 | async-start | bytes 786432 | tf_op jit(solution)/shard_map/all_to_all | solution.py:113
  29.6 0.6 %multiply_add_fusion = f32[32,32,1024]{2,1,0:T(8,128)S(1)} fusion(f32[32,1024]{1,0:T(8,128)S(1)} %copy-done.5, f32[32,1024]{1,0:T(8,128)S(1)} %copy-done.3, f32[32,1024]{1,0:T(8,128)S(1)} %copy-done.4, f32[32,1024]{1,0:T(8,128)S(1)} %copy-done.2), kind=kLoop, calls=%fused_computation.3 | loop fusion | flops 3145728 | bytes 4718592 | tf_op jit(solution)/shard_map/add | solution.py:29
  30.3 0.3 bitcast_select_fusion
  30.7 1.9 %copy-done = f32[1024,1024]{1,0:T(8,128)} copy-done((f32[1024,1024]{1,0:T(8,128)}, f32[1024,1024]{1,0:T(8,128)S(1)}, u32[]{:S(2)}) %copy-start) | copy-done | bytes 4194328
  32.6 0.1 slice.78
  32.7 13.5 %all-to-all-done.1 = f32[64,1,1536]{2,1,0:T(1,128)S(1)} async-done(((f32[64,1,1536]{2,1,0:T(1,128)}), f32[64,1,1536]{2,1,0:T(1,128)S(1)}, u32[]{:S(2)}, u32[]{:S(2)}) %all-to-all-start.1) | async-done | bytes 393248 | tf_op jit(solution)/shard_map/all_to_all | solution.py:113
  46.2 0.9 %reduce = f32[64,1536]{1,0:T(8,128)S(1)} reduce(f32[64,1,1536]{2,1,0:T(1,128)S(1)} %all-to-all-done.1, f32[]{:T(128)} %constant.72), dimensions={1}, to_apply=%all_to_all.15.reduce_sub_computation | reduce | bytes 786436 | tf_op jit(solution)/shard_map/all_to_all | solution.py:113
  47.2 0.2 reshape.89
  47.3 0.1 reduce-precision_convert_fusion.1
  47.5 1.3 %fusion = f32[1024,288]{0,1:T(8,128)S(1)} fusion(bf16[1024,96]{1,0:T(8,128)(2,1)S(1)} %get-tuple-element.22, bf16[1024,96]{1,0:T(8,128)(2,1)S(1)} %get-tuple-element.23, bf16[1024,96]{1,0:T(8,128)(2,1)S(1)} %get-tuple-element.21), kind=kOutput, calls=%fused_computation.7 | convolution fusion | flops 608894976 | bytes 1769472 | tf_op jit(solution)/shard_map/dot_general | solution.py:47
  48.8 0.1 broadcast_multiply_fusion
  49.0 0.7 %copy-done.1 = f32[1024,1024]{1,0:T(8,128)S(1)} copy-done((f32[1024,1024]{1,0:T(8,128)S(1)}, f32[1024,1024]{1,0:T(8,128)}, u32[]{:S(2)}) %copy-start.1) | copy-done | bytes 4194328
  49.7 4.5 %fusion.12 = f32[1024,192]{0,1:T(8,128)S(1)} fusion(f32[1024,1024]{1,0:T(8,128)S(1)} %copy-done.1, f32[1024,96]{0,1:T(8,128)S(1)} %get-tuple-element.19, f32[1024,96]{0,1:T(8,128)S(1)} %get-tuple-element.20), kind=kOutput, calls=%fused_computation.19 | convolution fusion | flops 2416115712 | bytes 5767168 | tf_op jit(solution)/shard_map/dot_general | solution.py:66
  54.2 0.1 fusion.35
  54.6 1.4 %fusion.3 = f32[513,128]{0,1:T(8,128)S(1)} fusion(f32[1,512]{1,0:T(1,128)S(1)} %copy-done.10, f32[512,512]{1,0:T(8,128)S(1)} %slice.78, f32[512,64]{0,1:T(8,128)S(1)} %get-tuple-element.28, f32[512,64]{0,1:T(8,128)S(1)} %get-tuple-element.27), kind=kOutput, calls=%fused_computation.10 | convolution fusion | flops 403767808 | bytes 1575424 | tf_op jit(solution)/shard_map/dot_general | solution.py:77
  56.1 0.1 fusion.32
  56.1 0.1 slice_add_fusion.4
  56.3 0.3 reverse
  56.7 0.9 %fusion.1 = f32[96,1024]{1,0:T(8,128)S(1)} fusion(s32[1024]{0:T(1024)S(1)} %iota_subtract_fusion, bf16[1024,32]{0,1:T(8,128)(2,1)S(1)} %get-tuple-element.30, bf16[1024,32]{0,1:T(8,128)(2,1)S(1)} %get-tuple-element.31, bf16[1024,32]{0,1:T(8,128)(2,1)S(1)} %get-tuple-element.29), kind=kOutput, calls=%fused_computation.8 | convolution fusion | flops 208207872 | bytes 593920 | tf_op jit(solution)/shard_map/dot_general | solution.py:87
  57.7 0.7 %fusion.29 = f32[32,1024]{1,0:T(8,128)} fusion(f32[96,1024]{1,0:T(8,128)S(1)} %fusion.1, f32[511,32]{0,1:T(8,128)S(1)} %slice.136, f32[513,32]{0,1:T(8,128)S(1)} %get-tuple-element.24, f32[1024]{0:T(1024)S(1)} %copy-done.7), kind=kLoop, calls=%fused_computation.51 | loop fusion | flops 196608 | bytes 659456 | tf_op jit(solution)/shard_map/div | solution.py:93
  (43 shorter events, 0.7 us)
Async XLA Ops:
  0.0 8.3 %copy-start.6 = (f32[513]{0:T(1024)S(1)}, f32[513]{0:T(1024)}, u32[]{:S(2)}) copy-start(f32[513]{0:T(1024)} %constant.70) | copy-start | bytes 6160
  0.0 29.6 %copy-start.2 = (f32[32,1024]{1,0:T(8,128)S(1)}, f32[32,1024]{1,0:T(8,128)}, u32[]{:S(2)}) copy-start(f32[32,1024]{1,0:T(8,128)} %constant.57.clone) | copy-start | bytes 393220
  0.0 29.6 %copy-start.3 = (f32[32,1024]{1,0:T(8,128)S(1)}, f32[32,1024]{1,0:T(8,128)}, u32[]{:S(2)}) copy-start(f32[32,1024]{1,0:T(8,128)} %constant.58.clone) | copy-start | bytes 393220
  0.0 29.6 %copy-start.4 = (f32[32,1024]{1,0:T(8,128)S(1)}, f32[32,1024]{1,0:T(8,128)}, u32[]{:S(2)}) copy-start(f32[32,1024]{1,0:T(8,128)} %constant.59.clone) | copy-start | bytes 393220
  0.0 29.6 %copy-start.5 = (f32[32,1024]{1,0:T(8,128)S(1)}, f32[32,1024]{1,0:T(8,128)}, u32[]{:S(2)}) copy-start(f32[32,1024]{1,0:T(8,128)} %constant.60.clone) | copy-start | bytes 393220
  2.0 9.5 %all-to-all-start = ((f32[8,1,48]{2,1,0:T(1,128)}), f32[8,1,48]{2,1,0:T(1,128)S(1)}, u32[]{:S(2)}, u32[]{:S(2)}) async-start(f32[8,1,48]{2,1,0:T(1,128)} %broadcast_in_dim.31), calls=%async_computation | async-start | bytes 8192 | tf_op jit(solution)/shard_map/all_to_all | solution.py:103
  13.1 33.1 %all-to-all-start.1 = ((f32[64,1,1536]{2,1,0:T(1,128)}), f32[64,1,1536]{2,1,0:T(1,128)S(1)}, u32[]{:S(2)}, u32[]{:S(2)}) async-start(f32[64,1,1536]{2,1,0:T(1,128)} %copy.24), calls=%async_computation.1 | async-start | bytes 786432 | tf_op jit(solution)/shard_map/all_to_all | solution.py:113
  30.6 1.9 %copy-start = (f32[1024,1024]{1,0:T(8,128)}, f32[1024,1024]{1,0:T(8,128)S(1)}, u32[]{:S(2)}) copy-start(f32[1024,1024]{1,0:T(8,128)S(1)} %bitcast_select_fusion) | copy-start | bytes 12582916
  32.7 16.1 %copy-start.9 = (f32[1024]{0:T(1024)S(1)}, f32[1024]{0:T(1024)}, u32[]{:S(2)}) copy-start(f32[1024]{0:T(1024)} %constant.61.clone) | copy-start | bytes 12292
  47.5 2.2 %copy-start.1 = (f32[1024,1024]{1,0:T(8,128)S(1)}, f32[1024,1024]{1,0:T(8,128)}, u32[]{:S(2)}) copy-start(f32[1024,1024]{1,0:T(8,128)} %copy-done) | copy-start | bytes 12582916
  48.8 5.5 %copy-start.13 = (f32[512]{0:T(512)S(1)}, f32[512]{0:T(512)}, u32[]{:S(2)}) copy-start(f32[512]{0:T(512)} %constant.62.clone) | copy-start | bytes 6148
  48.9 5.7 %copy-start.11 = (f32[512]{0:T(512)S(1)}, f32[512]{0:T(512)}, u32[]{:S(2)}) copy-start(f32[512]{0:T(512)} %constant.63.clone) | copy-start | bytes 6148
  48.9 5.7 %copy-start.12 = (f32[512]{0:T(512)S(1)}, f32[512]{0:T(512)}, u32[]{:S(2)}) copy-start(f32[512]{0:T(512)} %constant.69) | copy-start | bytes 6148
  49.0 5.7 %copy-start.10 = (f32[1,512]{1,0:T(1,128)S(1)}, f32[1,512]{1,0:T(1,128)}, u32[]{:S(2)}) copy-start(f32[1,512]{1,0:T(1,128)} %constant.64.clone) | copy-start | bytes 6148
  49.7 6.4 %copy-start.8 = (f32[513]{0:T(1024)S(1)}, f32[513]{0:T(1024)}, u32[]{:S(2)}) copy-start(f32[513]{0:T(1024)} %constant.71) | copy-start | bytes 6160
  54.5 3.2 %copy-start.7 = (f32[1024]{0:T(1024)S(1)}, f32[1024]{0:T(1024)}, u32[]{:S(2)}) copy-start(f32[1024]{0:T(1024)} %constant.68) | copy-start | bytes 12292

commit v18 on v17

--- a/solution.py
+++ b/solution.py
@@ -63,7 +63,20 @@
     parity = jnp.asarray(np.where(steps % 2 == 0, 1.0, -1.0).astype(np.float32))
     quarter_cos = np.where(steps % 4 == 0, 1.0, np.where(steps % 4 == 2, -1.0, 0.0)).astype(np.float32)
     signed = jnp.concatenate([positions, positions * parity[:, None]], axis=1)
-    spectrum = jnp.dot(table_full, signed, precision=lax.Precision.HIGHEST)
+    table_one = lax.reduce_precision(table_full, exponent_bits=8, mantissa_bits=7)
+    table_rest = table_full - table_one
+    table_two = lax.reduce_precision(table_rest, exponent_bits=8, mantissa_bits=7)
+    table_three = table_rest - table_two
+    pieces = split_three(signed)
+    wide = 2 * width
+    by_one = jnp.dot(table_one.astype(jnp.bfloat16), pieces, preferred_element_type=jnp.float32)
+    by_two = jnp.dot(table_two.astype(jnp.bfloat16), pieces[:, : 2 * wide], preferred_element_type=jnp.float32)
+    by_three = jnp.dot(table_three.astype(jnp.bfloat16), pieces[:, :wide], preferred_element_type=jnp.float32)
+    spectrum = (
+        (by_one[:, 2 * wide :] + by_two[:, wide:] + by_three)
+        + (by_one[:, wide : 2 * wide] + by_two[:, :wide])
+        + by_one[:, :wide]
+    )
     real_part = spectrum[:half]
     imag_part = spectrum[half:] * jnp.asarray((steps[:half] != 0).astype(np.float32))[:, None]
     power = jnp.sum((real_part * real_part + imag_part * imag_part).reshape(half, 2, 3, count), axis=2)

time: 58.7 us -> 59 us (level)
  local copies, waits for them, and re-layouts: 7.56 us -> 8.75 us
  matrix products: 8.11 us -> 7.09 us
    unnamed x30, local copies, waits for them, and re-layouts: 3.07 us -> 4.22 us
    dot_general x1 -> x3, matrix products: 4.53 us -> 3.51 us  [the longest x1 1.43 us: lag_table(): jnp.dot(table_one.astype(jnp.bfloat16), pieces, preferred_element_type=jn...]
where the time goes in v18:
time: 59 us; the launch traced here: 58.7 us
  starting transfers between devices  20.8 us (35%)
  waiting for transfers between devices  16.6 us (28%)
  local copies, waits for them, and re-layouts  8.75 us (15%)
  matrix products  7.09 us (12%)
  other arithmetic  5.09 us (9%)
    all_to_all x1, starting transfers between devices, per_device(): lax.all_to_all(outgoing, 'frames', split_axis=0, concat_axis=0, tiled=True)  16.5 us
    all_to_all x1, waiting for transfers between devices, per_device(): lax.all_to_all(outgoing, 'frames', split_axis=0, concat_axis=0, tiled=True)  13.6 us
    all_to_all x1, starting transfers between devices, per_device(): lax.all_to_all(spread, 'atoms', split_axis=0, concat_axis=0, tiled=True)  4.3 us
    unnamed x30, local copies, waits for them, and re-layouts  4.22 us
    all_to_all x1, waiting for transfers between devices, per_device(): lax.all_to_all(spread, 'atoms', split_axis=0, concat_axis=0, tiled=True)  3.05 us
    reshape x1, local copies, waits for them, and re-layouts, per_device(): displacements.reshape(local_frames, 3, groups, count)  1.51 us
    dot_general x1, matrix products, lag_table(): jnp.dot(table_one.astype(jnp.bfloat16), pieces, preferred_element_type=jn...  1.43 us
    dot_general x1, matrix products, lag_table(): folded = jnp.dot(table, coef, precision=lax.Precision.HIGHEST)  1.4 us
  transfers between devices with their start and end apart: 2, of which 2 were waited for; matrix products, arithmetic and copies ran while one was open for 5% of the time, Pallas kernels for 0%

profile of v18, /device:TPU:16, one launch (start us, length us, event | category | flops | bytes accessed | tf_op | source)
XLA Modules:
  0.0 58.7 jit_solution(15558159958312005906)
XLA Ops:
  0.0 1.1 %reduce_sum.47 = f32[16,3]{0,1:T(4,128)S(1)} reduce(f32[16,3,2048]{2,0,1:T(8,128)} %param.11, f32[]{:T(128)} %constant.23.clone.1), dimensions={2}, to_apply=%region_0.0 | reduce | flops 98256 | bytes 393412 | tf_op jit(solution)/shard_map/reduce_sum | solution.py:114
  1.2 0.1 broadcast_in_dim.24
  1.3 0.6 %broadcast_in_dim.31 = f32[8,1,48]{2,1,0:T(1,128)} broadcast(f32[48]{0:T(128)S(1)} %broadcast_in_dim.24), dimensions={2} | broadcast | bytes 1728 | tf_op jit(solution)/shard_map/broadcast_in_dim | solution.py:115
  1.9 4.3 %all-to-all-start = ((f32[8,1,48]{2,1,0:T(1,128)}), f32[8,1,48]{2,1,0:T(1,128)S(1)}, u32[]{:S(2)}, u32[]{:S(2)}) async-start(f32[8,1,48]{2,1,0:T(1,128)} %broadcast_in_dim.31), calls=%async_computation | async-start | bytes 8192 | tf_op jit(solution)/shard_map/all_to_all | solution.py:116
  6.2 1.5 %reshape.87 = f32[16,3,64,32]{3,2,0,1:T(8,128)S(1)} reshape(f32[16,3,2048]{2,0,1:T(8,128)} %param.11) | data formatting | bytes 786432 | tf_op jit(solution)/shard_map/reshape | solution.py:118
  7.7 0.5 copy.23
  8.3 3.0 %all-to-all-done = f32[8,1,48]{2,1,0:T(1,128)S(1)} async-done(((f32[8,1,48]{2,1,0:T(1,128)}), f32[8,1,48]{2,1,0:T(1,128)S(1)}, u32[]{:S(2)}, u32[]{:S(2)}) %all-to-all-start) | async-done | bytes 1568 | tf_op jit(solution)/shard_map/all_to_all | solution.py:116
  11.6 0.1 sub.47
  11.7 0.3 broadcast_subtract_fusion
  12.0 1.1 %copy.24 = f32[64,1,1536]{2,1,0:T(1,128)} copy(f32[64,1,1536]{0,2,1:T(8,128)S(1)} %bitcast.21) | data formatting | bytes 786432 | tf_op jit(solution)/shard_map/all_to_all | solution.py:126
  13.1 16.5 %all-to-all-start.1 = ((f32[64,1,1536]{2,1,0:T(1,128)}), f32[64,1,1536]{2,1,0:T(1,128)S(1)}, u32[]{:S(2)}, u32[]{:S(2)}) async-start(f32[64,1,1536]{2,1,0:T(1,128)} %copy.24), calls=%async_computation.1 | async-start | bytes 786432 | tf_op jit(solution)/shard_map/all_to_all | solution.py:126
  29.6 0.6 %multiply_add_fusion = f32[32,32,1024]{2,1,0:T(8,128)S(1)} fusion(f32[32,1024]{1,0:T(8,128)S(1)} %copy-done.5, f32[32,1024]{1,0:T(8,128)S(1)} %copy-done.3, f32[32,1024]{1,0:T(8,128)S(1)} %copy-done.4, f32[32,1024]{1,0:T(8,128)S(1)} %copy-done.2), kind=kLoop, calls=%fused_computation.8 | loop fusion | flops 3145728 | bytes 4718592 | tf_op jit(solution)/shard_map/add | solution.py:29
  30.2 0.3 bitcast_select_fusion
  30.6 1.9 %copy-done = f32[1024,1024]{1,0:T(8,128)} copy-done((f32[1024,1024]{1,0:T(8,128)}, f32[1024,1024]{1,0:T(8,128)S(1)}, u32[]{:S(2)}) %copy-start) | copy-done | bytes 4194328
  32.5 0.1 slice.104
  32.6 13.6 %all-to-all-done.1 = f32[64,1,1536]{2,1,0:T(1,128)S(1)} async-done(((f32[64,1,1536]{2,1,0:T(1,128)}), f32[64,1,1536]{2,1,0:T(1,128)S(1)}, u32[]{:S(2)}, u32[]{:S(2)}) %all-to-all-start.1) | async-done | bytes 393248 | tf_op jit(solution)/shard_map/all_to_all | solution.py:126
  46.2 0.9 %reduce = f32[64,1536]{1,0:T(8,128)S(1)} reduce(f32[64,1,1536]{2,1,0:T(1,128)S(1)} %all-to-all-done.1, f32[]{:T(128)} %constant.72), dimensions={1}, to_apply=%all_to_all.15.reduce_sub_computation | reduce | bytes 786436 | tf_op jit(solution)/shard_map/all_to_all | solution.py:126
  47.1 0.2 reshape.89
  47.3 0.1 reduce-precision_convert_fusion.7
  47.4 1.3 %fusion.1 = f32[1024,288]{0,1:T(8,128)S(1)} fusion(bf16[1024,96]{1,0:T(8,128)(2,1)S(1)} %get-tuple-element.25, bf16[1024,96]{1,0:T(8,128)(2,1)S(1)} %get-tuple-element.26, bf16[1024,96]{1,0:T(8,128)(2,1)S(1)} %get-tuple-element.24), kind=kOutput, calls=%fused_computation.12 | convolution fusion | flops 608894976 | bytes 1769472 | tf_op jit(solution)/shard_map/dot_general | solution.py:47
  48.8 0.1 broadcast_multiply_fusion
  48.9 0.2 reduce-precision_convert_fusion.4
  49.1 1.8 %copy-done.1 = f32[1024,1024]{1,0:T(8,128)S(1)} copy-done((f32[1024,1024]{1,0:T(8,128)S(1)}, f32[1024,1024]{1,0:T(8,128)}, u32[]{:S(2)}) %copy-start.1) | copy-done | bytes 4194328
  50.9 1.0 %fusion.4 = f32[1024,384]{0,1:T(8,128)S(1)} fusion(f32[1024,1024]{1,0:T(8,128)S(1)} %copy-done.1, bf16[1024,192]{0,1:T(8,128)(2,1)S(1)} %get-tuple-element.21, bf16[1024,192]{0,1:T(8,128)(2,1)S(1)} %get-tuple-element.23), kind=kOutput, calls=%fused_computation.15 | convolution fusion | flops 811073536 | bytes 6553600 | tf_op jit(solution)/shard_map/dot_general | solution.py:73
  52.0 1.4 %fusion.3 = f32[1024,576]{0,1:T(8,128)S(1)} fusion(f32[1024,1024]{1,0:T(8,128)S(1)} %copy-done.1, bf16[1024,192]{0,1:T(8,128)(2,1)S(1)} %get-tuple-element.22, bf16[1024,192]{0,1:T(8,128)(2,1)S(1)} %get-tuple-element.21, bf16[1024,192]{0,1:T(8,128)(2,1)S(1)} %get-tuple-element.23), kind=kOutput, calls=%fused_computation.14 | convolution fusion | flops 1213595648 | bytes 7733248 | tf_op jit(solution)/shard_map/dot_general | solution.py:72
  53.4 1.1 %fusion.14 = f32[1024,192]{0,1:T(8,128)S(1)} fusion(bf16[1024,192]{0,1:T(8,128)(2,1)S(1)} %get-tuple-element.23, f32[1024,1024]{1,0:T(8,128)S(1)} %copy-done.1, f32[1024,576]{0,1:T(8,128)S(1)} %fusion.3, f32[1024,384]{0,1:T(8,128)S(1)} %fusion.4), kind=kOutput, calls=%fused_computation.20 | convolution fusion | flops 408879104 | bytes 9306112 | tf_op jit(solution)/shard_map/dot_general | solution.py:74
  54.5 0.1 fusion.54
  54.9 1.4 %fusion.22 = f32[513,128]{0,1:T(8,128)S(1)} fusion(f32[1,512]{1,0:T(1,128)S(1)} %copy-done.10, f32[512,512]{1,0:T(8,128)S(1)} %slice.104, f32[512,64]{0,1:T(8,128)S(1)} %get-tuple-element.31, f32[512,64]{0,1:T(8,128)S(1)} %get-tuple-element.30), kind=kOutput, calls=%fused_computation.30 | convolution fusion | flops 403767808 | bytes 1575424 | tf_op jit(solution)/shard_map/dot_general | solution.py:90
  56.4 0.1 slice_add_fusion.6
  56.6 0.3 reverse
  57.1 0.9 %fusion.2 = f32[96,1024]{1,0:T(8,128)S(1)} fusion(s32[1024]{0:T(1024)S(1)} %iota_subtract_fusion, bf16[1024,32]{0,1:T(8,128)(2,1)S(1)} %get-tuple-element.33, bf16[1024,32]{0,1:T(8,128)(2,1)S(1)} %get-tuple-element.34, bf16[1024,32]{0,1:T(8,128)(2,1)S(1)} %get-tuple-element.32), kind=kOutput, calls=%fused_computation.13 | convolution fusion | flops 208207872 | bytes 593920 | tf_op jit(solution)/shard_map/dot_general | solution.py:100
  58.0 0.7 %fusion.48 = f32[32,1024]{1,0:T(8,128)} fusion(f32[96,1024]{1,0:T(8,128)S(1)} %fusion.2, f32[511,32]{0,1:T(8,128)S(1)} %slice.177, f32[513,32]{0,1:T(8,128)S(1)} %get-tuple-element.27, f32[1024]{0:T(1024)S(1)} %copy-done.7), kind=kLoop, calls=%fused_computation.74 | loop fusion | flops 196608 | bytes 659456 | tf_op jit(solution)/shard_map/div | solution.py:106
  (46 shorter events, 1.0 us)
Async XLA Ops:
  0.0 8.2 %copy-start.6 = (f32[513]{0:T(1024)S(1)}, f32[513]{0:T(1024)}, u32[]{:S(2)}) copy-start(f32[513]{0:T(1024)} %constant.70) | copy-start | bytes 6160
  1.9 9.5 %all-to-all-start = ((f32[8,1,48]{2,1,0:T(1,128)}), f32[8,1,48]{2,1,0:T(1,128)S(1)}, u32[]{:S(2)}, u32[]{:S(2)}) async-start(f32[8,1,48]{2,1,0:T(1,128)} %broadcast_in_dim.31), calls=%async_computation | async-start | bytes 8192 | tf_op jit(solution)/shard_map/all_to_all | solution.py:116
  8.2 21.3 %copy-start.2 = (f32[32,1024]{1,0:T(8,128)S(1)}, f32[32,1024]{1,0:T(8,128)}, u32[]{:S(2)}) copy-start(f32[32,1024]{1,0:T(8,128)} %constant.57.clone) | copy-start | bytes 393220
  8.2 21.3 %copy-start.3 = (f32[32,1024]{1,0:T(8,128)S(1)}, f32[32,1024]{1,0:T(8,128)}, u32[]{:S(2)}) copy-start(f32[32,1024]{1,0:T(8,128)} %constant.58.clone) | copy-start | bytes 393220
  8.2 21.3 %copy-start.4 = (f32[32,1024]{1,0:T(8,128)S(1)}, f32[32,1024]{1,0:T(8,128)}, u32[]{:S(2)}) copy-start(f32[32,1024]{1,0:T(8,128)} %constant.59.clone) | copy-start | bytes 393220
  8.3 21.3 %copy-start.5 = (f32[32,1024]{1,0:T(8,128)S(1)}, f32[32,1024]{1,0:T(8,128)}, u32[]{:S(2)}) copy-start(f32[32,1024]{1,0:T(8,128)} %constant.60.clone) | copy-start | bytes 393220
  13.1 33.1 %all-to-all-start.1 = ((f32[64,1,1536]{2,1,0:T(1,128)}), f32[64,1,1536]{2,1,0:T(1,128)S(1)}, u32[]{:S(2)}, u32[]{:S(2)}) async-start(f32[64,1,1536]{2,1,0:T(1,128)} %copy.24), calls=%async_computation.1 | async-start | bytes 786432 | tf_op jit(solution)/shard_map/all_to_all | solution.py:126
  30.6 1.9 %copy-start = (f32[1024,1024]{1,0:T(8,128)}, f32[1024,1024]{1,0:T(8,128)S(1)}, u32[]{:S(2)}) copy-start(f32[1024,1024]{1,0:T(8,128)S(1)} %bitcast_select_fusion) | copy-start | bytes 12582916
  47.4 1.3 %copy-start.9 = (f32[1024]{0:T(1024)S(1)}, f32[1024]{0:T(1024)}, u32[]{:S(2)}) copy-start(f32[1024]{0:T(1024)} %constant.61.clone) | copy-start | bytes 12292
  48.7 2.2 %copy-start.1 = (f32[1024,1024]{1,0:T(8,128)S(1)}, f32[1024,1024]{1,0:T(8,128)}, u32[]{:S(2)}) copy-start(f32[1024,1024]{1,0:T(8,128)} %copy-done) | copy-start | bytes 12582916
  53.4 1.2 %copy-start.13 = (f32[512]{0:T(512)S(1)}, f32[512]{0:T(512)}, u32[]{:S(2)}) copy-start(f32[512]{0:T(512)} %constant.62.clone) | copy-start | bytes 6148
  53.4 1.5 %copy-start.11 = (f32[512]{0:T(512)S(1)}, f32[512]{0:T(512)}, u32[]{:S(2)}) copy-start(f32[512]{0:T(512)} %constant.63.clone) | copy-start | bytes 6148
  53.4 1.5 %copy-start.12 = (f32[512]{0:T(512)S(1)}, f32[512]{0:T(512)}, u32[]{:S(2)}) copy-start(f32[512]{0:T(512)} %constant.69) | copy-start | bytes 6148
  53.4 1.5 %copy-start.10 = (f32[1,512]{1,0:T(1,128)S(1)}, f32[1,512]{1,0:T(1,128)}, u32[]{:S(2)}) copy-start(f32[1,512]{1,0:T(1,128)} %constant.64.clone) | copy-start | bytes 6148
  54.5 1.8 %copy-start.8 = (f32[513]{0:T(1024)S(1)}, f32[513]{0:T(1024)}, u32[]{:S(2)}) copy-start(f32[513]{0:T(1024)} %constant.71) | copy-start | bytes 6160
  57.0 1.0 %copy-start.7 = (f32[1024]{0:T(1024)S(1)}, f32[1024]{0:T(1024)}, u32[]{:S(2)}) copy-start(f32[1024]{0:T(1024)} %constant.68) | copy-start | bytes 12292

commit v19 on v17

--- a/solution.py
+++ b/solution.py
@@ -50,12 +50,11 @@
     return out[:, :width] + out[:, width : 2 * width] + out[:, 2 * width :]
 
 
-def lag_table(series, count, parts):
+def lag_table(series, count, parts, lower, window):
     length = series.shape[0]
     half = length // 2
     width = 3 * count
     frame = jnp.arange(length, dtype=jnp.int32)
-    lower = (frame[None, :] <= frame[:, None]).astype(jnp.float32)
     positions = exact_product(lower, series)
     squares = jnp.sum((positions * positions).reshape(length, 3, count), axis=1)
     table_full = spectral_table(length, half, parts)
@@ -80,12 +79,8 @@
     near = folded[:, :count] + sign_m * folded[:, count : 2 * count] + middle[None, :] * quarter
     far = folded[:, 2 * count : 3 * count] + sign_m * folded[:, 3 * count :] + middle[None, :] * quarter
     corr = jnp.concatenate([near, jnp.flip(far[1:half], axis=0)], axis=0)
-    window = (
-        (frame[None, :] >= frame[:, None]).astype(jnp.float32)
-        + (frame[None, :] <= (length - 1 - frame)[:, None]).astype(jnp.float32)
-    )
     parts_t = lax.dot_general(
-        split_three(squares), window.astype(jnp.bfloat16), (((0,), (1,)), ((), ())),
+        split_three(squares), window, (((0,), (1,)), ((), ())),
         preferred_element_type=jnp.float32,
     )
     spans = parts_t[:count] + parts_t[count : 2 * count] + parts_t[2 * count :]
@@ -109,10 +104,18 @@
     drift_row = jnp.broadcast_to((summed / atom_total)[:, :, None], (local_frames, 3, count))
     outgoing = blocks - drift_row.reshape(1, local_frames * 3 * count)
     length = local_frames * groups
-    *parts, outgoing = lax.optimization_barrier((*table_parts(length, length // 2), outgoing))
+    frame = jnp.arange(length, dtype=jnp.int32)
+    lower = (frame[None, :] <= frame[:, None]).astype(jnp.bfloat16)
+    window = (
+        (frame[None, :] >= frame[:, None]).astype(jnp.float32)
+        + (frame[None, :] <= (length - 1 - frame)[:, None]).astype(jnp.float32)
+    ).astype(jnp.bfloat16)
+    *parts, lower, window, outgoing = lax.optimization_barrier(
+        (*table_parts(length, length // 2), lower, window, outgoing)
+    )
     moved = lax.all_to_all(outgoing, "frames", split_axis=0, concat_axis=0, tiled=True)
     series = moved.reshape(length, 3 * count)
-    return lag_table(series, count, parts)
+    return lag_table(series, count, parts, lower, window)
 
 
 def solution(mesh):

time: 58.7 us -> 78.2 us (1.33)
  the two profiles are of different devices: /device:TPU:16 before, /device:TPU:2 now
where the time goes in v19:
time: 78.2 us; the launch traced here: 77.6 us
  starting transfers between devices  21.6 us (28%)
  other arithmetic  17.8 us (23%)
  waiting for transfers between devices  14 us (18%)
  matrix products  13.1 us (17%)
  local copies, waits for them, and re-layouts  10.8 us (14%)
    all_to_all x1, waiting for transfers between devices, per_device(): lax.all_to_all(outgoing, 'frames', split_axis=0, concat_axis=0, tiled=True)  14 us
    all_to_all x1, starting transfers between devices, per_device(): lax.all_to_all(outgoing, 'frames', split_axis=0, concat_axis=0, tiled=True)  12.5 us
    all_to_all x1, starting transfers between devices, per_device(): lax.all_to_all(spread, 'atoms', split_axis=0, concat_axis=0, tiled=True)  9.13 us
    dot_general x1, matrix products, lag_table(): spectrum = jnp.dot(table_full, signed, precision=lax.Precision.HIGHEST)  6.41 us
    dot_general x1, matrix products, exact_product(): jnp.dot(matrix.astype(jnp.bfloat16), split_three(values), preferred_eleme...  2.88 us
    another operation x2, other arithmetic  2.8 us
    transpose x1, local copies, waits for them, and re-layouts, per_device(): jnp.transpose(displacements.reshape(local_frames, 3, groups, count), (2,...  2.76 us
    unnamed x22, local copies, waits for them, and re-layouts  2.36 us
  transfers between devices with their start and end apart: 2, of which 1 were waited for; matrix products, arithmetic and copies ran while one was open for 10% of the time, Pallas kernels for 0%

profile of v19, /device:TPU:2, one launch (start us, length us, event | category | flops | bytes accessed | tf_op | source)
XLA Modules:
  0.0 77.6 jit_solution(11503141679893934408)
XLA Ops:
  0.0 1.2 %reduce_sum.47 = f32[16,3]{0,1:T(4,128)S(1)} reduce(f32[16,3,2048]{2,0,1:T(8,128)} %param.11, f32[]{:T(128)} %constant.20.clone.1), dimensions={2}, to_apply=%region_0.0 | reduce | flops 98256 | bytes 393412 | tf_op jit(solution)/shard_map/reduce_sum | solution.py:96
  1.4 0.6 broadcast_in_dim.25
  2.0 9.1 %all-to-all-start = ((f32[8,1,48]{2,1,0:T(1,128)}), f32[8,1,48]{2,1,0:T(1,128)S(1)}, u32[]{:S(2)}, u32[]{:S(2)}) async-start(f32[8,1,48]{2,1,0:T(1,128)} %broadcast_in_dim.25), calls=%async_computation | async-start | bytes 8192 | tf_op jit(solution)/shard_map/all_to_all | solution.py:98
  11.1 1.6 %fusion = bf16[1024,1024]{1,0:T(8,128)(2,1)} fusion(), kind=kLoop, calls=%fused_computation.6 | loop fusion | flops 2097152 | bytes 2097152 | tf_op jit(solution)/shard_map/convert_element_type | solution.py:108
  12.7 0.5 add_convert_fusion
  13.3 1.7 %reshape.87 = f32[16,3,64,32]{3,2,0,1:T(8,128)} reshape(f32[16,3,2048]{2,0,1:T(8,128)S(1)} %copy-done.1) | data formatting | bytes 786432 | tf_op jit(solution)/shard_map/reshape | solution.py:100
  15.0 2.8 %copy.23 = f32[64,16,3,32]{0,3,2,1:T(8,128)} copy(f32[64,16,3,32]{3,0,1,2:T(8,128)} %bitcast.22) | data formatting | bytes 786432 | tf_op jit(solution)/shard_map/transpose | solution.py:100
  18.1 1.4 %broadcast_subtract_fusion = f32[64,1536]{0,1:T(8,128)S(1)} fusion(f32[64,1536]{0,1:T(8,128)} %bitcast.24, f32[1536]{0:T(1024)S(1)} %sub.37), kind=kLoop, calls=%fused_computation.32 | loop fusion | flops 98304 | bytes 792576 | tf_op jit(solution)/shard_map/sub | solution.py:105
  19.5 1.1 %copy.24 = f32[64,1,1536]{2,1,0:T(1,128)} copy(f32[64,1,1536]{0,2,1:T(8,128)S(1)} %bitcast.23) | data formatting | bytes 786432 | tf_op jit(solution)/shard_map/all_to_all | solution.py:116
  20.6 12.5 %all-to-all-start.1 = ((f32[64,1,1536]{2,1,0:T(1,128)}), f32[64,1,1536]{2,1,0:T(1,128)}, u32[]{:S(2)}, u32[]{:S(2)}) async-start(f32[64,1,1536]{2,1,0:T(1,128)} %copy.24), calls=%async_computation.1 | async-start | bytes 786432 | tf_op jit(solution)/shard_map/all_to_all | solution.py:116
  33.2 0.6 multiply_add_fusion
  33.8 0.3 bitcast_select_fusion
  34.2 1.9 %copy-done = f32[1024,1024]{1,0:T(8,128)} copy-done((f32[1024,1024]{1,0:T(8,128)}, f32[1024,1024]{1,0:T(8,128)S(1)}, u32[]{:S(2)}) %copy-start) | copy-done | bytes 4194328
  36.2 14.0 %all-to-all-done.1 = f32[64,1,1536]{2,1,0:T(1,128)} async-done(((f32[64,1,1536]{2,1,0:T(1,128)}), f32[64,1,1536]{2,1,0:T(1,128)}, u32[]{:S(2)}, u32[]{:S(2)}) %all-to-all-start.1) | async-done | bytes 393248 | tf_op jit(solution)/shard_map/all_to_all | solution.py:116
  50.2 1.9 %reduce = f32[64,1536]{1,0:T(8,128)S(1)} reduce(f32[64,1,1536]{2,1,0:T(1,128)} %all-to-all-done.1, f32[]{:T(128)} %constant.72), dimensions={1}, to_apply=%all_to_all.15.reduce_sub_computation | reduce | bytes 786436 | tf_op jit(solution)/shard_map/all_to_all | solution.py:116
  52.1 1.0 %reshape.89 = f32[1024,96]{1,0:T(8,128)} reshape(f32[64,1536]{1,0:T(8,128)S(1)} %reduce) | data formatting | bytes 786432 | tf_op jit(solution)/shard_map/reshape | solution.py:117
  53.1 1.2 %reduce-precision_convert_fusion.1 = (bf16[1024,96]{1,0:T(8,128)(2,1)S(1)}, bf16[1024,96]{1,0:T(8,128)(2,1)S(1)}, bf16[1024,96]{1,0:T(8,128)(2,1)S(1)}) fusion(f32[1024,96]{1,0:T(8,128)} %reshape.89), kind=kLoop, calls=%fused_computation.24 | loop fusion | flops 688128 | bytes 983040 | tf_op jit(solution)/shard_map/convert.3
  54.3 2.9 %fusion.5 = f32[1024,288]{0,1:T(8,128)S(1)} fusion(bf16[1024,1024]{1,0:T(8,128)(2,1)} %fusion, bf16[1024,96]{1,0:T(8,128)(2,1)S(1)} %get-tuple-element.26, bf16[1024,96]{1,0:T(8,128)(2,1)S(1)} %get-tuple-element.27, bf16[1024,96]{1,0:T(8,128)(2,1)S(1)} %get-tuple-element.25), kind=kOutput, calls=%fused_computation.11 | convolution fusion | flops 605749248 | bytes 3866624 | tf_op jit(solution)/shard_map/dot_general | solution.py:47
  57.2 0.9 %broadcast_multiply_fusion = (f32[1024,96]{0,1:T(8,128)}, f32[1024,96]{0,1:T(8,128)S(1)}) fusion(f32[1024]{0:T(1024)S(1)} %copy-done.9, f32[1024,288]{0,1:T(8,128)S(1)} %fusion.5), kind=kLoop, calls=%fused_computation.42 | loop fusion | flops 294912 | bytes 1970176 | tf_op jit(solution)/shard_map/mul | solution.py:64
  58.0 0.8 %mul.159 = f32[1024,96]{0,1:T(8,128)} multiply(f32[1024,96]{0,1:T(8,128)S(1)} %get-tuple-element.24, f32[1024,96]{0,1:T(8,128)S(1)} %get-tuple-element.24) | non-fusion elementwise | flops 98304 | bytes 1179648 | tf_op jit(solution)/shard_map/mul | solution.py:59
  58.8 1.7 %reduce_sum.49 = f32[1024,32]{0,1:T(8,128)} reduce(f32[1024,3,32]{0,2,1:T(8,128)} %bitcast.26, f32[]{:T(128)} %constant.20.clone.1), dimensions={1}, to_apply=%region_2.0 | reduce | flops 65536 | bytes 524292 | tf_op jit(solution)/shard_map/reduce_sum | solution.py:59
  60.5 1.6 %reduce-precision_convert_fusion.3 = (bf16[1024,32]{0,1:T(8,128)(2,1)}, bf16[1024,32]{0,1:T(8,128)(2,1)}, bf16[1024,32]{0,1:T(8,128)(2,1)}) fusion(f32[1024,32]{0,1:T(8,128)} %reduce_sum.49), kind=kLoop, calls=%fused_computation.46 | loop fusion | flops 229376 | bytes 327680 | tf_op jit(solution)/shard_map/convert
  62.1 6.4 %fusion.11 = f32[1024,192]{0,1:T(8,128)S(1)} fusion(f32[1024,1024]{1,0:T(8,128)} %copy-done, f32[1024,96]{0,1:T(8,128)} %get-tuple-element.23, f32[1024,96]{0,1:T(8,128)S(1)} %get-tuple-element.24), kind=kOutput, calls=%fused_computation.17 | convolution fusion | flops 2416115712 | bytes 5767168 | tf_op jit(solution)/shard_map/dot_general | solution.py:65
  68.6 0.7 fusion.35
  69.3 0.8 fusion.17
  70.0 0.7 reduce_sum.50
  70.7 0.8 mul.182
  71.5 0.9 %bitcast_multiply_fusion = (f32[512,64]{0,1:T(8,128)S(1)}, f32[512,64]{0,1:T(8,128)S(1)}) fusion(f32[512,2,32]{0,2,1:T(8,128)} %reduce_sum.50, f32[512]{0:T(512)} %constant.63.clone, f32[512]{0:T(512)} %constant.69), kind=kLoop, calls=%fused_computation.54 | loop fusion | flops 65536 | bytes 397312 | tf_op jit(solution)/shard_map/mul | solution.py:72
  72.5 2.1 %fusion.1 = f32[513,128]{0,1:T(8,128)S(1)} fusion(f32[1,512]{1,0:T(1,128)} %constant.64.clone, f32[512,512]{1,0:T(8,128)S(1)} %slice.78, f32[512,64]{0,1:T(8,128)S(1)} %get-tuple-element.32, f32[512,64]{0,1:T(8,128)S(1)} %get-tuple-element.31), kind=kOutput, calls=%fused_computation.7 | convolution fusion | flops 403767808 | bytes 1575424 | tf_op jit(solution)/shard_map/dot_general | solution.py:76
  74.8 0.3 reverse
  75.2 1.7 %fusion.21 = f32[96,1024]{1,0:T(8,128)S(1)} fusion(bf16[1024,1024]{1,0:T(8,128)(2,1)S(1)} %add_convert_fusion, bf16[1024,32]{0,1:T(8,128)(2,1)} %get-tuple-element.34, bf16[1024,32]{0,1:T(8,128)(2,1)} %get-tuple-element.35, bf16[1024,32]{0,1:T(8,128)(2,1)} %get-tuple-element.33), kind=kOutput, calls=%fused_computation.36 | convolution fusion | flops 201916416 | bytes 2686976 | tf_op jit(solution)/shard_map/dot_general | solution.py:82
  76.9 0.7 fusion.29
  (37 shorter events, 1.0 us)
Async XLA Ops:
  0.0 13.3 %copy-start.1 = (f32[16,3,2048]{2,0,1:T(8,128)S(1)}, f32[16,3,2048]{2,0,1:T(8,128)}, u32[]{:S(2)}) copy-start(f32[16,3,2048]{2,0,1:T(8,128)} %param.11) | copy-start | bytes 1179652
  2.0 15.8 %all-to-all-start = ((f32[8,1,48]{2,1,0:T(1,128)}), f32[8,1,48]{2,1,0:T(1,128)S(1)}, u32[]{:S(2)}, u32[]{:S(2)}) async-start(f32[8,1,48]{2,1,0:T(1,128)} %broadcast_in_dim.25), calls=%async_computation | async-start | bytes 8192 | tf_op jit(solution)/shard_map/all_to_all | solution.py:98
  11.1 6.6 %copy-start.6 = (f32[513]{0:T(1024)S(1)}, f32[513]{0:T(1024)}, u32[]{:S(2)}) copy-start(f32[513]{0:T(1024)} %constant.70) | copy-start | bytes 6160
  13.2 19.9 %copy-start.2 = (f32[32,1024]{1,0:T(8,128)S(1)}, f32[32,1024]{1,0:T(8,128)}, u32[]{:S(2)}) copy-start(f32[32,1024]{1,0:T(8,128)} %constant.57.clone) | copy-start | bytes 393220
  13.2 19.9 %copy-start.3 = (f32[32,1024]{1,0:T(8,128)S(1)}, f32[32,1024]{1,0:T(8,128)}, u32[]{:S(2)}) copy-start(f32[32,1024]{1,0:T(8,128)} %constant.58.clone) | copy-start | bytes 393220
  13.2 19.9 %copy-start.4 = (f32[32,1024]{1,0:T(8,128)S(1)}, f32[32,1024]{1,0:T(8,128)}, u32[]{:S(2)}) copy-start(f32[32,1024]{1,0:T(8,128)} %constant.59.clone) | copy-start | bytes 393220
  13.3 19.9 %copy-start.5 = (f32[32,1024]{1,0:T(8,128)S(1)}, f32[32,1024]{1,0:T(8,128)}, u32[]{:S(2)}) copy-start(f32[32,1024]{1,0:T(8,128)} %constant.60.clone) | copy-start | bytes 393220
  20.6 29.6 %all-to-all-start.1 = ((f32[64,1,1536]{2,1,0:T(1,128)}), f32[64,1,1536]{2,1,0:T(1,128)}, u32[]{:S(2)}, u32[]{:S(2)}) async-start(f32[64,1,1536]{2,1,0:T(1,128)} %copy.24), calls=%async_computation.1 | async-start | bytes 786432 | tf_op jit(solution)/shard_map/all_to_all | solution.py:116
  34.2 1.9 %copy-start = (f32[1024,1024]{1,0:T(8,128)}, f32[1024,1024]{1,0:T(8,128)S(1)}, u32[]{:S(2)}) copy-start(f32[1024,1024]{1,0:T(8,128)S(1)} %bitcast_select_fusion) | copy-start | bytes 12582916
  53.1 4.1 %copy-start.9 = (f32[1024]{0:T(1024)S(1)}, f32[1024]{0:T(1024)}, u32[]{:S(2)}) copy-start(f32[1024]{0:T(1024)} %constant.61.clone) | copy-start | bytes 12292
  62.1 12.4 %copy-start.8 = (f32[513]{0:T(1024)S(1)}, f32[513]{0:T(1024)}, u32[]{:S(2)}) copy-start(f32[513]{0:T(1024)} %constant.71) | copy-start | bytes 6160
  68.5 8.3 %copy-start.7 = (f32[1024]{0:T(1024)S(1)}, f32[1024]{0:T(1024)}, u32[]{:S(2)}) copy-start(f32[1024]{0:T(1024)} %constant.68) | copy-start | bytes 12292
